TPU v7x, 512 devices: a whole 4x8x8 slice. The times are simulated.
512 devices in a mesh: seq: 64 (over x, y, core), tp: 8 (over z).
Axes of the slice: x: 4, y: 8, z: 8, core: 2. Of those that a mesh axis runs over, the one named last changes fastest.
Arguments:
- x_proj: bfloat16 [32768, 8192], P('seq', 'tp'), may hold values from -27 to 27
- bc_proj: bfloat16 [32768, 2, 1024], P('seq', None, 'tp'), may hold values from -6 to 6
- z_proj: bfloat16 [32768, 8192], P('seq', 'tp'), may hold values from -6 to 6
- dt_raw: float32 [32768, 128], P('seq', 'tp'), may hold values from -2.5 to 63
- conv_x: bfloat16 [4, 8192], P(None, 'tp'), may hold values from -3 to 3
- conv_bc: bfloat16 [4, 2, 1024], P(None, None, 'tp'), may hold values from -3 to 3
- bias_x: float32 [8192], P('tp'), may hold values from -0.5 to 0.5
- bias_bc: float32 [2, 1024], P(None, 'tp'), may hold values from -0.5 to 0.5
- dt_bias: float32 [128], P('tp'), may hold values from -4.5 to -3
- a_log: float32 [128], P('tp'), may hold values from -5.5 to 0.5
- d_skip: float32 [128], P('tp'), may hold values from 0.15 to 5
- norm_gain: float32 [8192], P('tp'), may hold values from 0.1 to 1.9
- seg_ids: int32 [32768], P('seq'), may hold values from 0 to 15, never falling along the last dimension, each value on 1 to 8192 neighbouring positions
Outputs:
- normed: bfloat16 [32768, 8192], P('seq', 'tp')
Inputs may be any that keep to these rules, and one draw needn't show every extreme that they name: `seg_ids`: each prompt's tokens are contiguous; ids start at 0 and never fall, each id from 0 to 15 has one token or more, at most 8192 tokens, and one prompt has exactly 8192.
All inputs are finite; a program needn't handle non-finite values.
Results may differ from a plain program's by a relative error of at most 0.0036.
Values may be sent and summed in bfloat16 or wider, within the bound.
No kernel may reach another device: no remote copies, remote signals or barrier semaphores. Data moves between devices by JAX's collectives and lax.ppermute only.
A program may use at most 128 MiB of HBM per device.

v0:
```python
import jax
import jax.numpy as jnp
from jax import lax
from jax.sharding import PartitionSpec as P

STATE = 128
STRETCH = 256


def from_behind(block, axis, distance):
    devices = range(lax.axis_size(axis))
    route = [(i - distance, i) for i in devices if i - distance in devices]
    return lax.ppermute(block, axis, route)


def carried_in(value, axis, join, neutral):
    count, mine = (lax.axis_size(axis), lax.axis_index(axis))
    pieces = jax.tree.map(lambda part: lax.all_gather(part, axis), value)
    running = jax.tree.map(
        lambda part, zero: jnp.full_like(part, 0) + jnp.asarray(zero, part.dtype), value, neutral
    )

    def step(position, running):
        longer = join(running, jax.tree.map(lambda part: part[position], pieces))
        return jax.tree.map(lambda new, old: jnp.where(position < mine, new, old), longer, running)

    return lax.fori_loop(0, count - 1, step, running)


def causal_conv(window, window_ids, weight, bias, rows):
    taps = weight.shape[0]
    own_ids = window_ids[taps - 1 :]
    extra = (1,) * (window.ndim - 1)
    result = jnp.broadcast_to(bias, (rows,) + bias.shape)
    for offset in range(taps):
        piece = window[offset : offset + rows].astype(jnp.float32)
        same = (window_ids[offset : offset + rows] == own_ids).reshape((rows,) + extra)
        result = result + jnp.where(same, piece * weight[offset].astype(jnp.float32), 0.0)
    return jax.nn.silu(result).astype(jnp.bfloat16)


def on_device(
    x_proj,
    bc_proj,
    z_proj,
    dt_raw,
    conv_x,
    conv_bc,
    bias_x,
    bias_bc,
    dt_bias,
    a_log,
    d_skip,
    norm_gain,
    seg_ids,
):
    tok_rows, inner_local = x_proj.shape
    heads_local = dt_raw.shape[1]
    state_size = STATE
    groups_local = bc_proj.shape[2] // state_size
    heads_group = heads_local // groups_local
    head_size = inner_local // heads_local
    block = STRETCH
    blocks = tok_rows // block
    margin = conv_x.shape[0] - 1
    tails = (
        x_proj[tok_rows - margin :],
        bc_proj[tok_rows - margin :],
        seg_ids[tok_rows - margin :].astype(jnp.bfloat16),
    )
    rim_x, rim_bc, rim_ids = from_behind((tails[0], tails[1], tails[2]), "seq", 1)
    own_ids = seg_ids.astype(jnp.float32)
    window_ids = jnp.concatenate([rim_ids.astype(jnp.float32), own_ids])
    x_conv = causal_conv(jnp.concatenate([rim_x, x_proj]), window_ids, conv_x, bias_x, tok_rows)
    bc_conv = causal_conv(
        jnp.concatenate([rim_bc, bc_proj]), window_ids, conv_bc, bias_bc, tok_rows
    )
    step_size = jax.nn.softplus(dt_raw + dt_bias)
    log_decay = step_size * -jnp.exp(a_log)
    cumul = jnp.cumsum(log_decay.reshape(blocks, block, heads_local), axis=1)
    cum_heads = cumul.reshape(blocks, block, groups_local, heads_group).transpose(0, 2, 3, 1)
    step_heads = step_size.reshape(blocks, block, groups_local, heads_group).transpose(0, 2, 3, 1)
    block_ids = own_ids.reshape(blocks, block)
    before_ids = window_ids[margin - 1 : margin - 1 + tok_rows : block]
    b_in = bc_conv[:, 0].reshape(blocks, block, groups_local, state_size)
    c_out = bc_conv[:, 1].reshape(blocks, block, groups_local, state_size)
    lower = jnp.tril(jnp.ones((block, block), dtype=bool))
    same = (block_ids[:, :, None] == block_ids[:, None, :]) & lower
    scores = jnp.einsum("cqgn,csgn->cgqs", c_out, b_in, preferred_element_type=jnp.float32)
    same_heads = same[:, None, None]
    spread = cum_heads[..., :, None] - cum_heads[..., None, :]
    decay = jnp.where(same_heads, jnp.exp(jnp.where(same_heads, spread, 0.0)), 0.0)
    mixing = (scores[:, :, None] * decay * step_heads[..., None, :]).astype(jnp.bfloat16)
    x_heads = x_conv.reshape(blocks, block, groups_local, heads_group, head_size)
    y_intra = jnp.einsum("cghqs,csghp->cqghp", mixing, x_heads, preferred_element_type=jnp.float32)
    tail_same = (block_ids == block_ids[:, -1:]).astype(jnp.float32)[:, None, None, :]
    weights = jnp.exp(cum_heads[..., -1:] - cum_heads) * step_heads * tail_same
    b_weighted = (
        b_in.transpose(0, 2, 1, 3)[:, :, None].astype(jnp.float32) * weights[..., None]
    ).astype(jnp.bfloat16)
    increment = jnp.einsum(
        "cghsn,csghp->cghpn", b_weighted, x_heads, preferred_element_type=jnp.float32
    )
    carry_gain = (
        jnp.exp(cum_heads[..., -1])
        * (block_ids[:, -1] == before_ids).astype(jnp.float32)[:, None, None]
    )
    link = (
        jnp.exp(cum_heads)
        * (block_ids == before_ids[:, None]).astype(jnp.float32)[:, None, None, :]
    )
    c_float = c_out.astype(jnp.float32)

    def recur(start_state):
        stacked = []
        current = start_state
        for index in range(blocks):
            stacked.append(current)
            current = carry_gain[index][..., None, None] * current + increment[index]
        return (jnp.stack(stacked), current)

    empty = jnp.zeros((groups_local, heads_group, head_size, state_size), jnp.float32)
    zero_states, summary = recur(empty)
    device_gain = carry_gain[0]
    index = 1
    device_gain = device_gain * carry_gain[index]

    def combine(earlier, later):
        return (earlier[0] * later[0], later[0][..., None, None] * earlier[1] + later[1])

    identity = (jnp.ones_like(device_gain), empty)
    _, entering = carried_in((device_gain, summary), "seq", combine, identity)
    states, _ = recur(entering)
    product = jnp.einsum("cqgn,cghpn->cqghp", c_float, states, precision=lax.Precision.HIGHEST)
    y_inter = product * link.transpose(0, 3, 1, 2)[..., None]
    skip = d_skip.reshape(groups_local, heads_group)[..., None]
    mixed = y_intra + y_inter + skip * x_heads.astype(jnp.float32)
    gated = mixed.reshape(tok_rows, inner_local) * jax.nn.silu(z_proj.astype(jnp.float32))
    squares = lax.psum(jnp.sum(gated * gated, axis=-1), "tp")
    scale = lax.rsqrt(squares / (inner_local * lax.axis_size("tp")) + 1e-05)
    return (gated * scale[:, None] * norm_gain).astype(jnp.bfloat16)


def solution(mesh):
    in_specs = (
        P("seq", "tp"),
        P("seq", None, "tp"),
        P("seq", "tp"),
        P("seq", "tp"),
        P(None, "tp"),
        P(None, None, "tp"),
        P("tp"),
        P(None, "tp"),
        P("tp"),
        P("tp"),
        P("tp"),
        P("tp"),
        P("seq"),
    )
    out_specs = P("seq", "tp")
    return jax.shard_map(
        on_device, mesh=mesh, in_specs=in_specs, out_specs=out_specs, check_vma=False
    )
```

profile of v0, /device:TPU:6, one launch (start us, length us, event | category | flops | bytes accessed | tf_op | source)
XLA Modules:
  0.0 333.3 jit_solution(14920317206801027827)
XLA Ops:
  7.5 1.9 collective-permute-start
  10.4 3.6 %collective-permute-start.2 = (bf16[3,2,128]{2,0,1:T(4,128)(2,1)S(1)}, bf16[3,2,128]{2,0,1:T(4,128)(2,1)S(1)}, u32[]{:S(2)}, u32[]{:S(2)}) collective-permute-start(bf16[3,2,128]{2,0,1:T(4,128)(2,1)S(1)} %slice.140), channel_id=1, source_target_pairs={{0,8},{8,16},{16,24},{24,32},{32,40},{40,48},{48,56},{56,64},{64,7... | collective-permute-start | bytes 4616 | tf_op jit(solution)/shard_map/ppermute | solution.py:13
  14.9 1.9 collective-permute-start.1
  16.8 1.5 copy.62
  22.5 2.2 collective-permute-done.1
  24.7 2.8 multiply_convert_fusion.5
  28.7 2.7 fusion.12
  34.0 1.5 copy.77
  35.7 35.4 %all_gather.10 = f32[64,1,16]{2,1,0:T(1,128)} all-gather(f32[1,1,16]{2,1,0:T(1,128)S(1)} %get-tuple-element.174), channel_id=1, replica_groups=mesh['seq'=64,'tp'=8] {'seq'}, dimensions={0}, use_global_device_ids=true | all-gather | bytes 4160 | tf_op jit(solution)/shard_map/all_gather | solution.py:18
  72.0 2.3 reshape.268
  74.4 107.7 %all-gather.3.cloned.1.call-done = f32[64,16,64,128]{3,2,1,0:T(8,128)} async-done(((f32[1,16,64,128]{3,2,1,0:T(8,128)}), f32[64,16,64,128]{3,2,1,0:T(8,128)}) %all-gather.3.cloned.1.call-update) | async-done | bytes 33554448 | tf_op jit(solution)/shard_map/all_gather | solution.py:18
  182.1 115.0 %while.14 = (s32[]{:T(128)}, f32[1,16,64,128]{3,2,1,0:T(8,128)S(1)}, s32[]{:T(128)}, f32[64,1,16]{2,1,0:T(1,128)}, f32[64,1,16,64,128]{4,3,2,1,0:T(8,128)}, /*index=5*/s32[]{:T(128)}, s32[]{:T(128)}) while((s32[]{:T(128)}, f32[1,16,64,128]{3,2,1,0:T(8,128)S(1)}, s32[]{:T(128)}, f32[64,1,16]{2,1,0:T(1,128)}, ...), condition=%wide.region_3.4_spmd.clone, body=%wide.region_2.3_spmd.clone.sunk | while | flops 524292 | bytes 1573161 | solution.py:27
  182.7 1.2 fusion.39
  184.5 1.2 fusion.39
  186.3 1.2 fusion.39
  188.2 1.2 fusion.39
  190.0 1.2 fusion.39
  191.8 1.2 fusion.39
  193.7 1.2 fusion.39
  195.5 1.2 fusion.39
  197.3 1.2 fusion.39
  199.2 1.2 fusion.39
  201.0 1.2 fusion.39
  202.8 1.2 fusion.39
  204.7 1.2 fusion.39
  206.5 1.2 fusion.39
  281.5 1.2 fusion.39
  299.0 2.9 fusion.14
  301.9 1.6 copy.76
  304.4 18.1 %psum.7 = f32[512]{0:T(512)S(1)} all-reduce(f32[512]{0:T(512)S(1)} %multiply_reduce_fusion), channel_id=1, replica_groups=mesh['seq'=64,'tp'=8] {'tp'}, use_global_device_ids=true, to_apply=%region_5.6 | all-reduce | flops 512 | bytes 4096 | tf_op jit(solution)/shard_map/psum | solution.py:139
  322.5 1.7 multiply_convert_fusion.4
  324.2 2.3 copy.78
  (195 shorter events, 110.6 us)
Async XLA Ops:
  6.5 14.6 %copy-start.9 = (s32[512]{0:T(512)S(1)}, s32[512]{0:T(512)}, u32[]{:S(2)}) copy-start(s32[512]{0:T(512)} %param.27) | copy-start | bytes 6148
  6.5 11.8 %copy-start.12 = (bf16[4,2,128]{2,1,0:T(2,128)(2,1)S(1)}, bf16[4,2,128]{2,1,0:T(2,128)(2,1)}, u32[]{:S(2)}) copy-start(bf16[4,2,128]{2,1,0:T(2,128)(2,1)} %param.20) | copy-start | bytes 6148
  6.5 11.8 %copy-start.8 = (bf16[4,1024]{1,0:T(4,128)(2,1)S(1)}, bf16[4,1024]{1,0:T(4,128)(2,1)}, u32[]{:S(2)}) copy-start(bf16[4,1024]{1,0:T(4,128)(2,1)} %param.19) | copy-start | bytes 24580
  6.5 12.1 %copy-start.15 = (f32[16]{0:T(128)S(1)}, f32[16]{0:T(128)}, u32[]{:S(2)}) copy-start(f32[16]{0:T(128)} %param.24) | copy-start | bytes 196
  6.5 12.1 %copy-start.4 = (f32[512,16]{0,1:T(8,128)S(1)}, f32[512,16]{0,1:T(8,128)}, u32[]{:S(2)}) copy-start(f32[512,16]{0,1:T(8,128)} %param.18) | copy-start | bytes 98308
  6.5 12.1 %copy-start.14 = (f32[16]{0:T(128)S(1)}, f32[16]{0:T(128)}, u32[]{:S(2)}) copy-start(f32[16]{0:T(128)} %param.23) | copy-start | bytes 196
  6.6 15.0 %copy-start.13 = (f32[2,128]{1,0:T(2,128)S(1)}, f32[2,128]{1,0:T(2,128)}, u32[]{:S(2)}) copy-start(f32[2,128]{1,0:T(2,128)} %param.22) | copy-start | bytes 3076
  6.6 175.5 %all-gather.3.cloned.1.call-start = ((), (), s32[]{:S(2)}) async-start(), calls=%async_computation | async-start | bytes 34078720 | tf_op jit(solution)/shard_map/all_gather | solution.py:18
  7.5 13.6 %collective-permute-start = (bf16[3]{0:T(256)(128)(2,1)S(1)}, bf16[3]{0:T(256)(128)(2,1)S(1)}, u32[]{:S(2)}, u32[]{:S(2)}) collective-permute-start(bf16[3]{0:T(256)(128)(2,1)S(1)} %slice.105), channel_id=1, source_target_pairs={{0,8},{8,16},{16,24},{24,32},{32,40},{40,48},{48,56},{56,64},{64,7... | collective-permute-start | bytes 26 | tf_op jit(solution)/shard_map/ppermute | solution.py:13
  10.4 11.2 %collective-permute-start.2 = (bf16[3,2,128]{2,0,1:T(4,128)(2,1)S(1)}, bf16[3,2,128]{2,0,1:T(4,128)(2,1)S(1)}, u32[]{:S(2)}, u32[]{:S(2)}) collective-permute-start(bf16[3,2,128]{2,0,1:T(4,128)(2,1)S(1)} %slice.140), channel_id=1, source_target_pairs={{0,8},{8,16},{16,24},{24,32},{32,40},{40,48},{48,56},{56,64},{64,7... | collective-permute-start | bytes 4616 | tf_op jit(solution)/shard_map/ppermute | solution.py:13
  14.9 9.8 %copy-start.10 = (f32[1024]{0:T(1024)S(1)}, f32[1024]{0:T(1024)}, u32[]{:S(2)}) copy-start(f32[1024]{0:T(1024)} %param.21) | copy-start | bytes 12292
  14.9 9.8 %collective-permute-start.1 = (bf16[3,1024]{0,1:T(8,128)(2,1)S(1)}, bf16[3,1024]{0,1:T(8,128)(2,1)S(1)}, u32[]{:S(2)}, u32[]{:S(2)}) collective-permute-start(bf16[3,1024]{0,1:T(8,128)(2,1)S(1)} %copy.61), channel_id=1, source_target_pairs={{0,8},{8,16},{16,24},{24,32},{32,40},{40,48},{48,56},{56,64},{64,7... | collective-permute-start | bytes 18440 | tf_op jit(solution)/shard_map/ppermute | solution.py:13
  31.4 1.0 copy-start
  182.1 115.0 %copy-start.1 = (f32[2,16,64,128]{3,2,1,0:T(8,128)S(1)}, f32[2,16,64,128]{3,2,1,0:T(8,128)}, u32[]{:S(2)}) copy-start(f32[2,16,64,128]{3,2,1,0:T(8,128)} %copy-done) | copy-start | bytes 3145732
  297.1 1.6 copy-start.2
  297.1 1.8 copy-start.3
  297.1 1.8 copy-start.5
  297.1 1.8 copy-start.6
  297.1 1.8 copy-start.7
  297.1 1.8 copy-start.16
  303.7 18.8 %copy-start.11 = (f32[1024]{0:T(1024)S(1)}, f32[1024]{0:T(1024)}, u32[]{:S(2)}) copy-start(f32[1024]{0:T(1024)} %param.26) | copy-start | bytes 12292
Sparse Core Ops, SparseCore 0:
  33.5 148.5 all-gather.2
where the time goes:
time: 339 us; the launch traced here: 333 us
  waiting for transfers between devices  110 us (32%)
  other arithmetic  84.8 us (25%)
  local copies, waits for them, and re-layouts  55.7 us (16%)
  blocking collectives  53.5 us (16%)
  between operations  13.8 us (4%)
  starting transfers between devices  7.45 us (2%)
  matrix products  6.85 us (2%)
    all_gather x1, waiting for transfers between devices, carried_in(): pieces = jax.tree.map(lambda part: lax.all_gather(part, axis), value)  108 us
    select_n x63, other arithmetic, step(): jnp.where(position < mine, new, old)  73.6 us
    mul x63, local copies, waits for them, and re-layouts, combine(): later[0][..., None, None] * earlier[1] + later[1]  40.3 us
    all_gather x1, blocking collectives, carried_in(): pieces = jax.tree.map(lambda part: lax.all_gather(part, axis), value)  35.4 us
    psum x1, blocking collectives, on_device(): squares = lax.psum(jnp.sum(gated * gated, axis=-1), 'tp')  18.1 us
    ppermute x3, starting transfers between devices, from_behind(): return lax.ppermute(block, axis, route)  7.42 us
  transfers between devices with their start and end apart: 4, of which 2 were waited for; matrix products, arithmetic and copies ran while one was open for 4% of the time, Pallas kernels for 0%

commit v1 on v0

--- a/solution.py
+++ b/solution.py
@@ -13,18 +13,30 @@
     return lax.ppermute(block, axis, route)
 
 
-def carried_in(value, axis, join, neutral):
-    count, mine = (lax.axis_size(axis), lax.axis_index(axis))
-    pieces = jax.tree.map(lambda part: lax.all_gather(part, axis), value)
-    running = jax.tree.map(
-        lambda part, zero: jnp.full_like(part, 0) + jnp.asarray(zero, part.dtype), value, neutral
-    )
+def shifted(block, axis, pairs):
+    return lax.ppermute(block, axis, pairs)
 
-    def step(position, running):
-        longer = join(running, jax.tree.map(lambda part: part[position], pieces))
-        return jax.tree.map(lambda new, old: jnp.where(position < mine, new, old), longer, running)
 
-    return lax.fori_loop(0, count - 1, step, running)
+def fold(earlier, later):
+    gain_e, state_e = earlier
+    gain_l, state_l = later
+    return (gain_e * gain_l, gain_l[..., None, None] * state_e + state_l)
+
+
+def entering_state(gain, state, axis):
+    count = lax.axis_size(axis)
+    chips = count // 2
+    own = (gain, state)
+    pair = shifted(own, axis, [(2 * c, 2 * c + 1) for c in range(chips)])
+    chip_total = fold(pair, own)
+    for reach in (1, 2, 4):
+        route = [(2 * c + 1, 2 * (c + reach) + 1) for c in range(chips - reach)]
+        chip_total = fold(shifted(chip_total, axis, route), chip_total)
+    behind = shifted(chip_total[1], axis, [(2 * c - 1, 2 * c) for c in range(1, chips)])
+    passed = gain[..., None, None] * behind + state
+    ahead = shifted(passed, axis, [(2 * c, 2 * c + 1) for c in range(chips)])
+    mine = lax.axis_index(axis)
+    return jnp.where(mine % 2 == 0, behind, ahead)
 
 
 def causal_conv(window, window_ids, weight, bias, rows):
@@ -121,15 +133,8 @@
 
     empty = jnp.zeros((groups_local, heads_group, head_size, state_size), jnp.float32)
     zero_states, summary = recur(empty)
-    device_gain = carry_gain[0]
-    index = 1
-    device_gain = device_gain * carry_gain[index]
-
-    def combine(earlier, later):
-        return (earlier[0] * later[0], later[0][..., None, None] * earlier[1] + later[1])
-
-    identity = (jnp.ones_like(device_gain), empty)
-    _, entering = carried_in((device_gain, summary), "seq", combine, identity)
+    device_gain = carry_gain[0] * carry_gain[1]
+    entering = entering_state(device_gain, summary, "seq")
     states, _ = recur(entering)
     product = jnp.einsum("cqgn,cghpn->cqghp", c_float, states, precision=lax.Precision.HIGHEST)
     y_inter = product * link.transpose(0, 3, 1, 2)[..., None]

time: 339 us -> 134 us (0.40); the launches traced: 333 us -> 133 us
  other arithmetic: 84.8 us -> 15.5 us
  waiting for transfers between devices: 110 us -> 50.1 us
  local copies, waits for them, and re-layouts: 55.7 us -> 14 us
  blocking collectives: 53.5 us -> 23.2 us
  starting transfers between devices: 7.45 us -> 22.1 us
  between operations: 13.8 us -> 0.56 us
    all_gather x1 -> x0, waiting for transfers between devices: 108 us -> none  [carried_in(): pieces = jax.tree.map(lambda part: lax.all_gather(part, axis), value)]
    select_n x63 -> x0, other arithmetic: 73.6 us -> none  [step(): jnp.where(position < mine, new, old)]
    ppermute x0 -> x9, waiting for transfers between devices: none -> 49.6 us  [shifted(): return lax.ppermute(block, axis, pairs)]
    mul x63 -> x0, local copies, waits for them, and re-layouts: 40.3 us -> none  [combine(): later[0][..., None, None] * earlier[1] + later[1]]
    all_gather x1 -> x0, blocking collectives: 35.4 us -> none  [carried_in(): pieces = jax.tree.map(lambda part: lax.all_gather(part, axis), value)]
    ppermute x0 -> x9, starting transfers between devices: none -> 14.7 us  [shifted(): return lax.ppermute(block, axis, pairs)]
    psum x1, blocking collectives: 18.1 us -> 23.2 us  [on_device(): squares = lax.psum(jnp.sum(gated * gated, axis=-1), 'tp')]
  transfers between devices with their start and end apart: 4 -> 12, of which waited for: 2 -> 4; matrix products, arithmetic and copies ran while one was open for 4% -> 12% of each run, Pallas kernels for 0% -> 0%
where the time goes in v1:
time: 134 us; the launch traced here: 133 us
  waiting for transfers between devices  50.1 us (37%)
  blocking collectives  23.2 us (17%)
  starting transfers between devices  22.1 us (16%)
  other arithmetic  15.5 us (12%)
  local copies, waits for them, and re-layouts  14 us (10%)
  matrix products  7.65 us (6%)
    ppermute x9, waiting for transfers between devices, shifted(): return lax.ppermute(block, axis, pairs)  49.6 us
    psum x1, blocking collectives, on_device(): squares = lax.psum(jnp.sum(gated * gated, axis=-1), 'tp')  23.2 us
    ppermute x9, starting transfers between devices, shifted(): return lax.ppermute(block, axis, pairs)  14.7 us
    ppermute x3, starting transfers between devices, from_behind(): return lax.ppermute(block, axis, route)  7.42 us
    unnamed x42, local copies, waits for them, and re-layouts  5.87 us
    convert_element_type x2, other arithmetic, causal_conv(): return jax.nn.silu(result).astype(jnp.bfloat16)  3.62 us
    dot_general x1, matrix products, on_device(): jnp.einsum('cghqs,csghp->cqghp', mixing, x_heads, preferred_element_type=...  2.91 us
    dot_general x1, matrix products, on_device(): jnp.einsum('cghsn,csghp->cghpn', b_weighted, x_heads, preferred_element_t...  2.72 us
  transfers between devices with their start and end apart: 12, of which 4 were waited for; matrix products, arithmetic and copies ran while one was open for 12% of the time, Pallas kernels for 0%

profile of v1, /device:TPU:6, one launch (start us, length us, event | category | flops | bytes accessed | tf_op | source)
XLA Modules:
  0.0 133.1 jit_solution(1151740626959941339)
XLA Ops:
  0.0 1.0 copy.42
  1.1 1.9 %collective-permute-start.2 = (bf16[3,2,128]{2,0,1:T(4,128)(2,1)S(1)}, bf16[3,2,128]{2,0,1:T(4,128)(2,1)S(1)}, u32[]{:S(2)}, u32[]{:S(2)}) collective-permute-start(bf16[3,2,128]{2,0,1:T(4,128)(2,1)S(1)} %slice.140), channel_id=1, source_target_pairs={{0,8},{8,16},{16,24},{24,32},{32,40},{40,48},{48,56},{56,64},{64,7... | collective-permute-start | bytes 4616 | tf_op jit(solution)/shard_map/ppermute | solution.py:13
  3.0 0.8 fusion.34
  3.9 3.6 %collective-permute-start = (bf16[3]{0:T(256)(128)(2,1)S(1)}, bf16[3]{0:T(256)(128)(2,1)S(1)}, u32[]{:S(2)}, u32[]{:S(2)}) collective-permute-start(bf16[3]{0:T(256)(128)(2,1)S(1)} %slice.105), channel_id=1, source_target_pairs={{0,8},{8,16},{16,24},{24,32},{32,40},{40,48},{48,56},{56,64},{64,7... | collective-permute-start | bytes 26 | tf_op jit(solution)/shard_map/ppermute | solution.py:13
  7.4 0.7 slice.107
  8.4 1.9 %collective-permute-start.1 = (bf16[3,1024]{0,1:T(8,128)(2,1)S(1)}, bf16[3,1024]{0,1:T(8,128)(2,1)S(1)}, u32[]{:S(2)}, u32[]{:S(2)}) collective-permute-start(bf16[3,1024]{0,1:T(8,128)(2,1)S(1)} %copy.39), channel_id=1, source_target_pairs={{0,8},{8,16},{16,24},{24,32},{32,40},{40,48},{48,56},{56,64},{64,7... | collective-permute-start | bytes 18440 | tf_op jit(solution)/shard_map/ppermute | solution.py:13
  10.3 1.5 %copy.40 = bf16[512,1024]{0,1:T(8,128)(2,1)S(1)} copy(bf16[512,1024]{1,0:T(8,128)(2,1)} %param.13) | data formatting | bytes 2097152 | tf_op args[0]
  12.2 1.2 reduce-window.6
  16.1 0.8 multiply_convert_fusion.8
  18.2 2.8 %multiply_convert_fusion.5 = bf16[512,1024]{0,1:T(8,128)(2,1)S(1)} fusion(bf16[512,1024]{0,1:T(8,128)(2,1)S(1)} %copy.40, bf16[3,1024]{0,1:T(8,128)(2,1)S(1)} %collective-permute-done.1, f32[1024]{0:T(1024)S(1)} %bitcast.129, f32[1024]{0:T(1024)S(1)} %bitcast.130, f32[1024]{0:T(1024)S(1)} %bitcast.128, f32[1024]{0:T(1024)S(1)} %bitcast.127, ...), kind=kLoop, calls=%fused_computation.24 | loop fusion | flops 15728640 | bytes 2125824 | tf_op jit(solution)/shard_map/convert_element_type | solution.py:51
  21.3 2.7 %fusion.11 = f32[2,16,64,128]{3,2,1,0:T(8,128)S(1)} fusion(f32[2,16,256]{2,1,0:T(8,128)S(1)} %fusion.28, f32[2,256,128]{2,1,0:T(8,128)} %convert_element_type.125, bf16[2,256,16,64]{1,0,3,2:T(2,128)(2,1)S(1)} %reshape.281), kind=kOutput, calls=%fused_computation.15 | convolution fusion | flops 136314880 | bytes 2392064 | tf_op jit(solution)/shard_map/cghsn,csghp->cghpn/dot_general | solution.py:113
  24.2 3.1 %collective-permute-start.6 = (f32[1,16,64,128]{3,2,1,0:T(8,128)S(1)}, f32[1,16,64,128]{3,2,1,0:T(8,128)S(1)}, u32[]{:S(2)}, u32[]{:S(2)}) collective-permute-start(f32[1,16,64,128]{3,2,1,0:T(8,128)S(1)} %slice_add_fusion), channel_id=1, source_target_pairs={{0,8},{16,24},{32,40},{48,56},{64,72},{80,88},{96,104},{112,120},{... | collective-permute-start | bytes 1572872 | tf_op jit(solution)/shard_map/ppermute | solution.py:17
  27.4 1.5 %collective-permute-done.6 = f32[1,16,64,128]{3,2,1,0:T(8,128)S(1)} collective-permute-done((f32[1,16,64,128]{3,2,1,0:T(8,128)S(1)}, f32[1,16,64,128]{3,2,1,0:T(8,128)S(1)}, u32[]{:S(2)}, u32[]{:S(2)}) %collective-permute-start.6) | collective-permute-done | bytes 524320 | tf_op jit(solution)/shard_map/ppermute | solution.py:17
  29.8 4.8 %collective-permute-start.3 = (f32[1,16]{1,0:T(1,128)S(1)}, f32[1,16]{1,0:T(1,128)S(1)}, u32[]{:S(2)}, u32[]{:S(2)}) collective-permute-start(f32[1,16]{1,0:T(1,128)S(1)} %copy-done.16), channel_id=1, source_target_pairs={{0,8},{16,24},{32,40},{48,56},{64,72},{80,88},{96,104},{112,120},{... | collective-permute-start | bytes 200 | tf_op jit(solution)/shard_map/ppermute | solution.py:17
  34.6 0.8 collective-permute-done.3
  38.5 1.3 collective-permute-start.10
  39.9 47.3 %collective-permute-done.10 = f32[1,16,64,128]{3,2,1,0:T(8,128)S(1)} collective-permute-done((f32[1,16,64,128]{3,2,1,0:T(8,128)S(1)}, f32[1,16,64,128]{3,2,1,0:T(8,128)S(1)}, u32[]{:S(2)}, u32[]{:S(2)}) %collective-permute-start.10) | collective-permute-done | bytes 524320 | tf_op jit(solution)/shard_map/ppermute | solution.py:17
  87.2 0.8 copy-done.1
  88.0 1.0 multiply_add_fusion
  89.0 2.1 %collective-permute-start.11 = (f32[1,16,64,128]{3,2,1,0:T(8,128)}, f32[1,16,64,128]{3,2,1,0:T(8,128)}, u32[]{:S(2)}, u32[]{:S(2)}) collective-permute-start(f32[1,16,64,128]{3,2,1,0:T(8,128)} %multiply_add_fusion), channel_id=1, source_target_pairs={{0,8},{16,24},{32,40},{48,56},{64,72},{80,88},{96,104},{112,120},{... | collective-permute-start | bytes 1572872 | tf_op jit(solution)/shard_map/ppermute | solution.py:17
  91.0 0.8 compare_and_fusion
  91.9 1.5 %copy.53 = bf16[512,1024]{0,1:T(8,128)(2,1)S(1)} copy(bf16[512,1024]{1,0:T(8,128)(2,1)} %param.15) | data formatting | bytes 2097152 | tf_op args[2]
  93.4 0.8 fusion.26
  94.1 1.0 fusion.35
  95.2 2.3 %reshape.299 = f32[2,256,1,16,64]{1,0,4,3,2:T(2,128)} reshape(bf16[512,1024]{0,1:T(8,128)(2,1)S(1)} %multiply_convert_fusion.5) | data formatting | bytes 3145728 | tf_op jit(solution)/shard_map/convert_element_type | solution.py:142
  97.4 1.2 fusion.25
  98.7 1.0 fusion.18
  100.5 2.9 %fusion.13 = f32[2,256,1,16,64]{1,4,3,0,2:T(8,128)S(1)} fusion(f32[2,16,64,256]{3,2,1,0:T(8,128)S(1)} %fusion.18, f32[2,256,1,16,64]{1,0,4,3,2:T(2,128)S(1)} %copy-done, f32[2,16,256]{2,1,0:T(8,128)S(1)} %bitcast.126, f32[2,16,256]{2,1,0:T(8,128)S(1)} %get-tuple-element.13, f32[2,256,256]{2,1,0:T(8,128)S(1)} %copy-done.4, ...), kind=kOutput, calls=%fused_computation.18 | convolution fusion | flops 283115520 | bytes 8093760 | tf_op jit(solution)/shard_map/cghqs,csghp->cqghp/dot_general | solution.py:107
  103.4 1.6 %copy.52 = f32[2,256,1,16,64]{1,0,4,3,2:T(2,128)S(1)} copy(f32[2,256,1,16,64]{1,4,3,0,2:T(8,128)S(1)} %fusion.13) | data formatting | bytes 4194304 | tf_op jit(solution)/shard_map/add | solution.py:142
  106.0 23.2 %psum.7 = f32[512]{0:T(512)S(1)} all-reduce(f32[512]{0:T(512)S(1)} %multiply_reduce_fusion), channel_id=1, replica_groups=mesh['seq'=64,'tp'=8] {'tp'}, use_global_device_ids=true, to_apply=%region_3.4 | all-reduce | flops 512 | bytes 4096 | tf_op jit(solution)/shard_map/psum | solution.py:144
  129.2 1.7 %multiply_convert_fusion.4 = bf16[512,1024]{0,1:T(8,128)(2,1)} fusion(f32[1024]{0:T(1024)S(1)} %copy-done.11, f32[512]{0:T(512)S(1)} %add_rsqrt_fusion, f32[512,1024]{0,1:T(8,128)S(1)} %bitcast.119, bf16[512,1024]{0,1:T(8,128)(2,1)S(1)} %copy.53), kind=kLoop, calls=%fused_computation.20 | loop fusion | flops 4718592 | bytes 4200448 | tf_op jit(solution)/shard_map/convert_element_type | solution.py:146
  130.9 2.3 %copy.54 = bf16[512,1024]{1,0:T(8,128)(2,1)} copy(bf16[512,1024]{0,1:T(8,128)(2,1)} %multiply_convert_fusion.4) | data formatting | bytes 2097152 | tf_op jit(solution)/shard_map/convert_element_type | solution.py:146
  (93 shorter events, 10.7 us)
Async XLA Ops:
  0.0 14.0 %copy-start.8 = (s32[512]{0:T(512)S(1)}, s32[512]{0:T(512)}, u32[]{:S(2)}) copy-start(s32[512]{0:T(512)} %param.25) | copy-start | bytes 6148
  0.0 11.8 %copy-start.13 = (bf16[4,2,128]{2,1,0:T(2,128)(2,1)S(1)}, bf16[4,2,128]{2,1,0:T(2,128)(2,1)}, u32[]{:S(2)}) copy-start(bf16[4,2,128]{2,1,0:T(2,128)(2,1)} %param.18) | copy-start | bytes 6148
  0.0 11.9 %copy-start.17 = (f32[16]{0:T(128)S(1)}, f32[16]{0:T(128)}, u32[]{:S(2)}) copy-start(f32[16]{0:T(128)} %param.22) | copy-start | bytes 196
  0.0 11.9 %copy-start.6 = (f32[512,16]{0,1:T(8,128)S(1)}, f32[512,16]{0,1:T(8,128)}, u32[]{:S(2)}) copy-start(f32[512,16]{0,1:T(8,128)} %param.16) | copy-start | bytes 98308
  0.0 11.9 %copy-start.15 = (f32[16]{0:T(128)S(1)}, f32[16]{0:T(128)}, u32[]{:S(2)}) copy-start(f32[16]{0:T(128)} %param.21) | copy-start | bytes 196
  0.0 13.8 %copy-start.7 = (bf16[4,1024]{1,0:T(4,128)(2,1)S(1)}, bf16[4,1024]{1,0:T(4,128)(2,1)}, u32[]{:S(2)}) copy-start(bf16[4,1024]{1,0:T(4,128)(2,1)} %param.17) | copy-start | bytes 24580
  0.0 16.1 %copy-start.14 = (f32[2,128]{1,0:T(2,128)S(1)}, f32[2,128]{1,0:T(2,128)}, u32[]{:S(2)}) copy-start(f32[2,128]{1,0:T(2,128)} %param.20) | copy-start | bytes 3076
  1.1 15.0 %collective-permute-start.2 = (bf16[3,2,128]{2,0,1:T(4,128)(2,1)S(1)}, bf16[3,2,128]{2,0,1:T(4,128)(2,1)S(1)}, u32[]{:S(2)}, u32[]{:S(2)}) collective-permute-start(bf16[3,2,128]{2,0,1:T(4,128)(2,1)S(1)} %slice.140), channel_id=1, source_target_pairs={{0,8},{8,16},{16,24},{24,32},{32,40},{40,48},{48,56},{56,64},{64,7... | collective-permute-start | bytes 4616 | tf_op jit(solution)/shard_map/ppermute | solution.py:13
  3.9 10.0 %collective-permute-start = (bf16[3]{0:T(256)(128)(2,1)S(1)}, bf16[3]{0:T(256)(128)(2,1)S(1)}, u32[]{:S(2)}, u32[]{:S(2)}) collective-permute-start(bf16[3]{0:T(256)(128)(2,1)S(1)} %slice.105), channel_id=1, source_target_pairs={{0,8},{8,16},{16,24},{24,32},{32,40},{40,48},{48,56},{56,64},{64,7... | collective-permute-start | bytes 26 | tf_op jit(solution)/shard_map/ppermute | solution.py:13
  8.4 9.8 %copy-start.10 = (f32[1024]{0:T(1024)S(1)}, f32[1024]{0:T(1024)}, u32[]{:S(2)}) copy-start(f32[1024]{0:T(1024)} %param.19) | copy-start | bytes 12292
  8.4 9.8 %collective-permute-start.1 = (bf16[3,1024]{0,1:T(8,128)(2,1)S(1)}, bf16[3,1024]{0,1:T(8,128)(2,1)S(1)}, u32[]{:S(2)}, u32[]{:S(2)}) collective-permute-start(bf16[3,1024]{0,1:T(8,128)(2,1)S(1)} %copy.39), channel_id=1, source_target_pairs={{0,8},{8,16},{16,24},{24,32},{32,40},{40,48},{48,56},{56,64},{64,7... | collective-permute-start | bytes 18440 | tf_op jit(solution)/shard_map/ppermute | solution.py:13
  21.3 2.9 %copy-start.2 = (bf16[2,256,16,64]{1,0,3,2:T(2,128)(2,1)}, bf16[2,256,16,64]{1,0,3,2:T(2,128)(2,1)S(1)}, u32[]{:S(2)}) copy-start(bf16[2,256,16,64]{1,0,3,2:T(2,128)(2,1)S(1)} %reshape.281) | copy-start | bytes 3145732
  21.3 7.5 %copy-start.9 = (f32[16]{0:T(128)S(1)}, f32[16]{0:T(128)}, u32[]{:S(2)}) copy-start(f32[16]{0:T(128)} %get-tuple-element.34) | copy-start | bytes 196
  24.1 5.7 %copy-start.16 = (f32[1,16]{1,0:T(1,128)S(1)}, f32[1,16]{1,0:T(1,128)}, u32[]{:S(2)}) copy-start(f32[1,16]{1,0:T(1,128)} %get-tuple-element.31) | copy-start | bytes 196
  24.2 4.6 %collective-permute-start.6 = (f32[1,16,64,128]{3,2,1,0:T(8,128)S(1)}, f32[1,16,64,128]{3,2,1,0:T(8,128)S(1)}, u32[]{:S(2)}, u32[]{:S(2)}) collective-permute-start(f32[1,16,64,128]{3,2,1,0:T(8,128)S(1)} %slice_add_fusion), channel_id=1, source_target_pairs={{0,8},{16,24},{32,40},{48,56},{64,72},{80,88},{96,104},{112,120},{... | collective-permute-start | bytes 1572872 | tf_op jit(solution)/shard_map/ppermute | solution.py:17
  29.0 6.3 %collective-permute-start.7 = (f32[1,16,64,128]{3,2,1,0:T(8,128)S(1)}, f32[1,16,64,128]{3,2,1,0:T(8,128)S(1)}, u32[]{:S(2)}, u32[]{:S(2)}) collective-permute-start(f32[1,16,64,128]{3,2,1,0:T(8,128)S(1)} %multiply_add_fusion.4), channel_id=1, source_target_pairs={{8,24},{24,40},{40,56},{56,72},{72,88},{88,104},{104,120},{120,136... | collective-permute-start | bytes 1572872 | tf_op jit(solution)/shard_map/ppermute | solution.py:17
  29.8 5.6 %collective-permute-start.3 = (f32[1,16]{1,0:T(1,128)S(1)}, f32[1,16]{1,0:T(1,128)S(1)}, u32[]{:S(2)}, u32[]{:S(2)}) collective-permute-start(f32[1,16]{1,0:T(1,128)S(1)} %copy-done.16), channel_id=1, source_target_pairs={{0,8},{16,24},{32,40},{48,56},{64,72},{80,88},{96,104},{112,120},{... | collective-permute-start | bytes 200 | tf_op jit(solution)/shard_map/ppermute | solution.py:17
  35.5 1.4 %collective-permute-start.8 = (f32[1,16,64,128]{3,2,1,0:T(8,128)S(1)}, f32[1,16,64,128]{3,2,1,0:T(8,128)S(1)}, u32[]{:S(2)}, u32[]{:S(2)}) collective-permute-start(f32[1,16,64,128]{3,2,1,0:T(8,128)S(1)} %multiply_add_fusion.3), channel_id=1, source_target_pairs={{8,40},{24,56},{40,72},{56,88},{72,104},{88,120},{104,136},{120,15... | collective-permute-start | bytes 1572872 | tf_op jit(solution)/shard_map/ppermute | solution.py:17
  36.2 0.7 collective-permute-start.4
  37.0 1.4 %collective-permute-start.9 = (f32[1,16,64,128]{3,2,1,0:T(8,128)S(1)}, f32[1,16,64,128]{3,2,1,0:T(8,128)S(1)}, u32[]{:S(2)}, u32[]{:S(2)}) collective-permute-start(f32[1,16,64,128]{3,2,1,0:T(8,128)S(1)} %multiply_add_fusion.2), channel_id=1, source_target_pairs={{8,72},{24,88},{40,104},{56,120},{72,136},{88,152},{104,168},{120,... | collective-permute-start | bytes 1572872 | tf_op jit(solution)/shard_map/ppermute | solution.py:17
  37.7 0.7 collective-permute-start.5
  38.5 48.6 %collective-permute-start.10 = (f32[1,16,64,128]{3,2,1,0:T(8,128)S(1)}, f32[1,16,64,128]{3,2,1,0:T(8,128)S(1)}, u32[]{:S(2)}, u32[]{:S(2)}) collective-permute-start(f32[1,16,64,128]{3,2,1,0:T(8,128)S(1)} %multiply_add_fusion.1), channel_id=1, source_target_pairs={{8,16},{24,32},{40,48},{56,64},{72,80},{88,96},{104,112},{120,128}... | collective-permute-start | bytes 1572872 | tf_op jit(solution)/shard_map/ppermute | solution.py:17
  87.2 0.8 copy-start.1
  89.0 8.5 %collective-permute-start.11 = (f32[1,16,64,128]{3,2,1,0:T(8,128)}, f32[1,16,64,128]{3,2,1,0:T(8,128)}, u32[]{:S(2)}, u32[]{:S(2)}) collective-permute-start(f32[1,16,64,128]{3,2,1,0:T(8,128)} %multiply_add_fusion), channel_id=1, source_target_pairs={{0,8},{16,24},{32,40},{48,56},{64,72},{80,88},{96,104},{112,120},{... | collective-permute-start | bytes 1572872 | tf_op jit(solution)/shard_map/ppermute | solution.py:17
  93.4 4.1 %copy-start.12 = (f32[16]{0:T(128)S(1)}, f32[16]{0:T(128)}, u32[]{:S(2)}) copy-start(f32[16]{0:T(128)} %get-tuple-element.33) | copy-start | bytes 196
  97.4 2.3 %copy-start.4 = (f32[2,256,256]{2,1,0:T(8,128)S(1)}, f32[2,256,256]{2,1,0:T(8,128)}, u32[]{:S(2)}) copy-start(f32[2,256,256]{2,1,0:T(8,128)} %fusion.35) | copy-start | bytes 1572868
  98.7 1.6 %copy-start = (f32[2,256,1,16,64]{1,0,4,3,2:T(2,128)S(1)}, f32[2,256,1,16,64]{1,0,4,3,2:T(2,128)}, u32[]{:S(2)}) copy-start(f32[2,256,1,16,64]{1,0,4,3,2:T(2,128)} %reshape.299) | copy-start | bytes 6291460
  98.7 1.8 %copy-start.3 = (bf16[2,256,16,64]{1,0,3,2:T(2,128)(2,1)S(1)}, bf16[2,256,16,64]{1,0,3,2:T(2,128)(2,1)}, u32[]{:S(2)}) copy-start(bf16[2,256,16,64]{1,0,3,2:T(2,128)(2,1)} %copy-done.2) | copy-start | bytes 3145732
  98.7 1.8 %copy-start.5 = (pred[2,256,256]{2,1,0:T(8,128)(4,1)S(1)}, pred[2,256,256]{2,1,0:T(8,128)(4,1)}, u32[]{:S(2)}) copy-start(pred[2,256,256]{2,1,0:T(8,128)(4,1)} %compare_and_fusion) | copy-start | bytes 393220
  98.7 1.8 %copy-start.18 = (f32[16]{0:T(128)S(1)}, f32[16]{0:T(128)}, u32[]{:S(2)}) copy-start(f32[16]{0:T(128)} %param.23) | copy-start | bytes 196
  105.3 23.9 %copy-start.11 = (f32[1024]{0:T(1024)S(1)}, f32[1024]{0:T(1024)}, u32[]{:S(2)}) copy-start(f32[1024]{0:T(1024)} %param.24) | copy-start | bytes 12292

commit v2 on v1

--- a/solution.py
+++ b/solution.py
@@ -23,20 +23,48 @@
     return (gain_e * gain_l, gain_l[..., None, None] * state_e + state_l)
 
 
+def pack(gain, state):
+    lanes = state.shape[-1]
+    flat = state.reshape(-1, lanes)
+    row = jnp.zeros((8, lanes), state.dtype).at[0, : gain.size].set(gain.reshape(-1))
+    return jnp.concatenate([flat, row])
+
+
+def unpack(packed, gain_shape, state_shape):
+    rows = packed.shape[0] - 8
+    count = 1
+    for size in gain_shape:
+        count *= size
+    return (packed[rows, :count].reshape(gain_shape), packed[:rows].reshape(state_shape))
+
+
 def entering_state(gain, state, axis):
     count = lax.axis_size(axis)
     chips = count // 2
+    shapes = (gain.shape, state.shape)
     own = (gain, state)
-    pair = shifted(own, axis, [(2 * c, 2 * c + 1) for c in range(chips)])
+    pair = unpack(shifted(pack(*own), axis, [(2 * c, 2 * c + 1) for c in range(chips)]), *shapes)
     chip_total = fold(pair, own)
     for reach in (1, 2, 4):
         route = [(2 * c + 1, 2 * (c + reach) + 1) for c in range(chips - reach)]
-        chip_total = fold(shifted(chip_total, axis, route), chip_total)
-    behind = shifted(chip_total[1], axis, [(2 * c - 1, 2 * c) for c in range(1, chips)])
-    passed = gain[..., None, None] * behind + state
-    ahead = shifted(passed, axis, [(2 * c, 2 * c + 1) for c in range(chips)])
+        got = unpack(shifted(pack(*chip_total), axis, route), *shapes)
+        chip_total = fold(got, chip_total)
+    to_even = shifted(chip_total[1], axis, [(2 * c - 1, 2 * c) for c in range(1, chips)])
+    to_odd = shifted(chip_total[1], axis, [(2 * c - 1, 2 * c + 1) for c in range(1, chips)])
+    odd_entering = pair[0][..., None, None] * to_odd + pair[1]
     mine = lax.axis_index(axis)
-    return jnp.where(mine % 2 == 0, behind, ahead)
+    return jnp.where(mine % 2 == 0, to_even, odd_entering)
+
+
+def summed_over(value, axis):
+    count = lax.axis_size(axis)
+    if count & (count - 1):
+        return lax.psum(value, axis)
+    reach = 1
+    while reach < count:
+        value = value + lax.ppermute(value, axis, [(i, i ^ reach) for i in range(count)])
+        reach *= 2
+    return value
 
 
 def causal_conv(window, window_ids, weight, bias, rows):
@@ -141,7 +169,7 @@
     skip = d_skip.reshape(groups_local, heads_group)[..., None]
     mixed = y_intra + y_inter + skip * x_heads.astype(jnp.float32)
     gated = mixed.reshape(tok_rows, inner_local) * jax.nn.silu(z_proj.astype(jnp.float32))
-    squares = lax.psum(jnp.sum(gated * gated, axis=-1), "tp")
+    squares = summed_over(jnp.sum(gated * gated, axis=-1), "tp")
     scale = lax.rsqrt(squares / (inner_local * lax.axis_size("tp")) + 1e-05)
     return (gated * scale[:, None] * norm_gain).astype(jnp.bfloat16)
 

time: 134 us -> 128 us (0.955)
  the two profiles are of different devices: /device:TPU:6 before, /device:TPU:5 now
where the time goes in v2:
time: 128 us
  waiting for transfers between devices  47.9 us (37%)
  starting transfers between devices  43.7 us (34%)
  other arithmetic  14.5 us (11%)
  local copies, waits for them, and re-layouts  13.4 us (10%)
  matrix products  7.63 us (6%)
    ppermute x6, waiting for transfers between devices, shifted(): return lax.ppermute(block, axis, pairs)  45.1 us
    ppermute x3, starting transfers between devices, summed_over(): lax.ppermute(value, axis, [(i, i ^ reach) for i in range(count)])  18.2 us
    ppermute x6, starting transfers between devices, shifted(): return lax.ppermute(block, axis, pairs)  16.2 us
    ppermute x3, starting transfers between devices, from_behind(): return lax.ppermute(block, axis, route)  9.26 us
    unnamed x44, local copies, waits for them, and re-layouts  5.09 us
    convert_element_type x2, other arithmetic, causal_conv(): return jax.nn.silu(result).astype(jnp.bfloat16)  3.62 us
    dot_general x1, matrix products, on_device(): jnp.einsum('cghqs,csghp->cqghp', mixing, x_heads, preferred_element_type=...  2.91 us
    ppermute x3, waiting for transfers between devices, summed_over(): lax.ppermute(value, axis, [(i, i ^ reach) for i in range(count)])  2.88 us
  transfers between devices with their start and end apart: 12, of which 8 were waited for; matrix products, arithmetic and copies ran while one was open for 11% of the time, Pallas kernels for 0%

profile of v2, /device:TPU:5, one launch (start us, length us, event | category | flops | bytes accessed | tf_op | source)
XLA Modules:
  0.0 127.8 jit_solution(4988008287125730574)
XLA Ops:
  0.0 1.0 copy.42
  1.1 3.8 %collective-permute-start.2 = (bf16[3,2,128]{2,0,1:T(4,128)(2,1)S(1)}, bf16[3,2,128]{2,0,1:T(4,128)(2,1)S(1)}, u32[]{:S(2)}, u32[]{:S(2)}) collective-permute-start(bf16[3,2,128]{2,0,1:T(4,128)(2,1)S(1)} %slice.232), channel_id=1, source_target_pairs={{0,8},{8,16},{16,24},{24,32},{32,40},{40,48},{48,56},{56,64},{64,7... | collective-permute-start | bytes 4616 | tf_op jit(solution)/shard_map/ppermute | solution.py:13
  5.7 1.9 %collective-permute-start = (bf16[3]{0:T(256)(128)(2,1)S(1)}, bf16[3]{0:T(256)(128)(2,1)S(1)}, u32[]{:S(2)}, u32[]{:S(2)}) collective-permute-start(bf16[3]{0:T(256)(128)(2,1)S(1)} %slice.190), channel_id=1, source_target_pairs={{0,8},{8,16},{16,24},{24,32},{32,40},{40,48},{48,56},{56,64},{64,7... | collective-permute-start | bytes 26 | tf_op jit(solution)/shard_map/ppermute | solution.py:13
  8.6 3.6 %collective-permute-start.1 = (bf16[3,1024]{0,1:T(8,128)(2,1)S(1)}, bf16[3,1024]{0,1:T(8,128)(2,1)S(1)}, u32[]{:S(2)}, u32[]{:S(2)}) collective-permute-start(bf16[3,1024]{0,1:T(8,128)(2,1)S(1)} %copy.39), channel_id=1, source_target_pairs={{0,8},{8,16},{16,24},{24,32},{32,40},{40,48},{48,56},{56,64},{64,7... | collective-permute-start | bytes 18440 | tf_op jit(solution)/shard_map/ppermute | solution.py:13
  12.2 1.5 %copy.40 = bf16[512,1024]{0,1:T(8,128)(2,1)S(1)} copy(bf16[512,1024]{1,0:T(8,128)(2,1)} %param.21) | data formatting | bytes 2097152 | tf_op args[0]
  14.1 1.2 reduce-window.6
  19.0 2.8 %multiply_convert_fusion.5 = bf16[512,1024]{0,1:T(8,128)(2,1)S(1)} fusion(bf16[512,1024]{0,1:T(8,128)(2,1)S(1)} %copy.40, bf16[3,1024]{0,1:T(8,128)(2,1)S(1)} %collective-permute-done.1, f32[1024]{0:T(1024)S(1)} %bitcast.147, f32[1024]{0:T(1024)S(1)} %bitcast.148, f32[1024]{0:T(1024)S(1)} %bitcast.146, f32[1024]{0:T(1024)S(1)} %bitcast.145, ...), kind=kLoop, calls=%fused_computation.24 | loop fusion | flops 15728640 | bytes 2125824 | tf_op jit(solution)/shard_map/convert_element_type | solution.py:79
  22.1 2.7 %fusion.11 = f32[2,16,64,128]{3,2,1,0:T(8,128)S(1)} fusion(f32[2,16,256]{2,1,0:T(8,128)S(1)} %fusion.27, f32[2,256,128]{2,1,0:T(8,128)} %convert_element_type.125, bf16[2,256,16,64]{1,0,3,2:T(2,128)(2,1)S(1)} %reshape.468), kind=kOutput, calls=%fused_computation.15 | convolution fusion | flops 136314880 | bytes 2392064 | tf_op jit(solution)/shard_map/cghsn,csghp->cghpn/dot_general | solution.py:141
  25.1 1.3 %collective-permute-start.3 = (f32[1032,128]{1,0:T(8,128)S(1)}, f32[1032,128]{1,0:T(8,128)S(1)}, u32[]{:S(2)}, u32[]{:S(2)}) collective-permute-start(f32[1032,128]{1,0:T(8,128)S(1)} %select_maximum_fusion.3), channel_id=1, source_target_pairs={{0,8},{16,24},{32,40},{48,56},{64,72},{80,88},{96,104},{112,120},{... | collective-permute-start | bytes 1585160 | tf_op jit(solution)/shard_map/ppermute | solution.py:17
  26.4 2.5 %collective-permute-done.3 = f32[1032,128]{1,0:T(8,128)S(1)} collective-permute-done((f32[1032,128]{1,0:T(8,128)S(1)}, f32[1032,128]{1,0:T(8,128)S(1)}, u32[]{:S(2)}, u32[]{:S(2)}) %collective-permute-start.3) | collective-permute-done | bytes 528416 | tf_op jit(solution)/shard_map/ppermute | solution.py:17
  29.2 3.2 %collective-permute-start.4 = (f32[1032,128]{1,0:T(8,128)S(1)}, f32[1032,128]{1,0:T(8,128)S(1)}, u32[]{:S(2)}, u32[]{:S(2)}) collective-permute-start(f32[1032,128]{1,0:T(8,128)S(1)} %select_maximum_fusion.2), channel_id=1, source_target_pairs={{8,24},{24,40},{40,56},{56,72},{72,88},{88,104},{104,120},{120,136... | collective-permute-start | bytes 1585160 | tf_op jit(solution)/shard_map/ppermute | solution.py:17
  32.4 8.9 %collective-permute-done.4 = f32[1032,128]{1,0:T(8,128)S(1)} collective-permute-done((f32[1032,128]{1,0:T(8,128)S(1)}, f32[1032,128]{1,0:T(8,128)S(1)}, u32[]{:S(2)}, u32[]{:S(2)}) %collective-permute-start.4) | collective-permute-done | bytes 528416 | tf_op jit(solution)/shard_map/ppermute | solution.py:17
  41.5 3.3 %collective-permute-start.5 = (f32[1032,128]{1,0:T(8,128)S(1)}, f32[1032,128]{1,0:T(8,128)S(1)}, u32[]{:S(2)}, u32[]{:S(2)}) collective-permute-start(f32[1032,128]{1,0:T(8,128)S(1)} %select_maximum_fusion.1), channel_id=1, source_target_pairs={{8,40},{24,56},{40,72},{56,88},{72,104},{88,120},{104,136},{120,15... | collective-permute-start | bytes 1585160 | tf_op jit(solution)/shard_map/ppermute | solution.py:17
  44.8 14.5 %collective-permute-done.5 = f32[1032,128]{1,0:T(8,128)S(1)} collective-permute-done((f32[1032,128]{1,0:T(8,128)S(1)}, f32[1032,128]{1,0:T(8,128)S(1)}, u32[]{:S(2)}, u32[]{:S(2)}) %collective-permute-start.5) | collective-permute-done | bytes 528416 | tf_op jit(solution)/shard_map/ppermute | solution.py:17
  59.5 4.3 %collective-permute-start.6 = (f32[1032,128]{1,0:T(8,128)S(1)}, f32[1032,128]{1,0:T(8,128)S(1)}, u32[]{:S(2)}, u32[]{:S(2)}) collective-permute-start(f32[1032,128]{1,0:T(8,128)S(1)} %select_maximum_fusion), channel_id=1, source_target_pairs={{8,72},{24,88},{40,104},{56,120},{72,136},{88,152},{104,168},{120,... | collective-permute-start | bytes 1585160 | tf_op jit(solution)/shard_map/ppermute | solution.py:17
  63.8 14.7 %collective-permute-done.6 = f32[1032,128]{1,0:T(8,128)S(1)} collective-permute-done((f32[1032,128]{1,0:T(8,128)S(1)}, f32[1032,128]{1,0:T(8,128)S(1)}, u32[]{:S(2)}, u32[]{:S(2)}) %collective-permute-start.6) | collective-permute-done | bytes 528416 | tf_op jit(solution)/shard_map/ppermute | solution.py:17
  79.5 2.1 %collective-permute-start.7 = (f32[1,16,64,128]{3,2,1,0:T(8,128)}, f32[1,16,64,128]{3,2,1,0:T(8,128)}, u32[]{:S(2)}, u32[]{:S(2)}) collective-permute-start(f32[1,16,64,128]{3,2,1,0:T(8,128)} %multiply_add_fusion), channel_id=1, source_target_pairs={{8,16},{24,32},{40,48},{56,64},{72,80},{88,96},{104,112},{120,128}... | collective-permute-start | bytes 1572872 | tf_op jit(solution)/shard_map/ppermute | solution.py:17
  81.6 2.1 %collective-permute-start.8 = (f32[1,16,64,128]{3,2,1,0:T(8,128)}, f32[1,16,64,128]{3,2,1,0:T(8,128)}, u32[]{:S(2)}, u32[]{:S(2)}) collective-permute-start(f32[1,16,64,128]{3,2,1,0:T(8,128)} %multiply_add_fusion), channel_id=1, source_target_pairs={{8,24},{24,40},{40,56},{56,72},{72,88},{88,104},{104,120},{120,136... | collective-permute-start | bytes 1572872 | tf_op jit(solution)/shard_map/ppermute | solution.py:17
  84.5 1.5 %copy.53 = bf16[512,1024]{0,1:T(8,128)(2,1)S(1)} copy(bf16[512,1024]{1,0:T(8,128)(2,1)} %param.23) | data formatting | bytes 2097152 | tf_op args[2]
  86.1 1.0 fusion.34
  87.1 2.3 %reshape.494 = f32[2,256,1,16,64]{1,0,4,3,2:T(2,128)} reshape(bf16[512,1024]{0,1:T(8,128)(2,1)S(1)} %multiply_convert_fusion.5) | data formatting | bytes 3145728 | tf_op jit(solution)/shard_map/convert_element_type | solution.py:170
  89.4 4.5 %collective-permute-done.8 = f32[1,16,64,128]{3,2,1,0:T(8,128)} collective-permute-done((f32[1,16,64,128]{3,2,1,0:T(8,128)}, f32[1,16,64,128]{3,2,1,0:T(8,128)}, u32[]{:S(2)}, u32[]{:S(2)}) %collective-permute-start.8) | collective-permute-done | bytes 524320 | tf_op jit(solution)/shard_map/ppermute | solution.py:17
  93.9 1.5 %add_bitcast_fusion = (f32[1,1,16,64,128]{4,3,2,1,0:T(8,128)S(1)}, f32[1,16,64,128]{3,2,1,0:T(8,128)S(1)}) fusion(f32[2,16,64,128]{3,2,1,0:T(8,128)S(1)} %fusion.11, f32[16]{0:T(128)S(1)} %copy-done.13, f32[1,16,64,128]{3,2,1,0:T(8,128)} %collective-permute-done.7, f32[1,16,64,128]{3,2,1,0:T(8,128)} %bitcast.130, ...), kind=kLoop, calls=%fused_computation.44 | loop fusion | flops 655360 | bytes 3145857 | tf_op jit(solution)/shard_map/stack | solution.py:160
  95.4 1.0 fusion.18
  97.2 2.9 %fusion.13 = f32[2,256,1,16,64]{1,4,3,0,2:T(8,128)S(1)} fusion(f32[2,16,64,256]{3,2,1,0:T(8,128)S(1)} %fusion.18, f32[2,256,1,16,64]{1,0,4,3,2:T(2,128)S(1)} %copy-done.1, f32[2,16,256]{2,1,0:T(8,128)S(1)} %bitcast.144, f32[2,16,256]{2,1,0:T(8,128)S(1)} %get-tuple-element.63, f32[2,256,256]{2,1,0:T(8,128)S(1)} %copy-done.4, ...), kind=kOutput, calls=%fused_computation.18 | convolution fusion | flops 283115520 | bytes 8093760 | tf_op jit(solution)/shard_map/cghqs,csghp->cqghp/dot_general | solution.py:135
  100.1 1.6 %copy.52 = f32[2,256,1,16,64]{1,0,4,3,2:T(2,128)S(1)} copy(f32[2,256,1,16,64]{1,4,3,0,2:T(8,128)S(1)} %fusion.13) | data formatting | bytes 4194304 | tf_op jit(solution)/shard_map/add | solution.py:170
  102.6 4.0 %collective-permute-start.9 = (f32[512]{0:T(512)S(1)}, f32[512]{0:T(512)S(1)}, u32[]{:S(2)}, u32[]{:S(2)}) collective-permute-start(f32[512]{0:T(512)S(1)} %multiply_reduce_fusion), channel_id=1, source_target_pairs={{0,1},{1,0},{2,3},{3,2},{4,5},{5,4},{6,7},{7,6},{8,9},{9,8},{10,11... | collective-permute-start | bytes 6152 | tf_op jit(solution)/shard_map/ppermute | solution.py:65
  106.7 1.0 collective-permute-done.9
  107.6 5.8 %collective-permute-start.10 = (f32[512]{0:T(512)S(1)}, f32[512]{0:T(512)S(1)}, u32[]{:S(2)}, u32[]{:S(2)}) collective-permute-start(f32[512]{0:T(512)S(1)} %add.137), channel_id=1, source_target_pairs={{0,2},{1,3},{2,0},{3,1},{4,6},{5,7},{6,4},{7,5},{8,10},{9,11},{10,... | collective-permute-start | bytes 6152 | tf_op jit(solution)/shard_map/ppermute | solution.py:65
  114.4 8.4 %collective-permute-start.11 = (f32[512]{0:T(512)S(1)}, f32[512]{0:T(512)S(1)}, u32[]{:S(2)}, u32[]{:S(2)}) collective-permute-start(f32[512]{0:T(512)S(1)} %add.138), channel_id=1, source_target_pairs={{0,4},{1,5},{2,6},{3,7},{4,0},{5,1},{6,2},{7,3},{8,12},{9,13},{10,... | collective-permute-start | bytes 6152 | tf_op jit(solution)/shard_map/ppermute | solution.py:65
  123.8 1.7 %multiply_convert_fusion.4 = bf16[512,1024]{0,1:T(8,128)(2,1)} fusion(f32[1024]{0:T(1024)S(1)} %copy-done.12, f32[512]{0:T(512)S(1)} %add_rsqrt_fusion, f32[512,1024]{0,1:T(8,128)S(1)} %bitcast.127, bf16[512,1024]{0,1:T(8,128)(2,1)S(1)} %copy.53), kind=kLoop, calls=%fused_computation.20 | loop fusion | flops 4718592 | bytes 4200448 | tf_op jit(solution)/shard_map/convert_element_type | solution.py:174
  125.5 2.3 %copy.54 = bf16[512,1024]{1,0:T(8,128)(2,1)} copy(bf16[512,1024]{0,1:T(8,128)(2,1)} %multiply_convert_fusion.4) | data formatting | bytes 2097152 | tf_op jit(solution)/shard_map/convert_element_type | solution.py:174
  (103 shorter events, 12.5 us)
Async XLA Ops:
  0.0 15.8 %copy-start.8 = (s32[512]{0:T(512)S(1)}, s32[512]{0:T(512)}, u32[]{:S(2)}) copy-start(s32[512]{0:T(512)} %param.33) | copy-start | bytes 6148
  0.0 13.7 %copy-start.15 = (bf16[4,2,128]{2,1,0:T(2,128)(2,1)S(1)}, bf16[4,2,128]{2,1,0:T(2,128)(2,1)}, u32[]{:S(2)}) copy-start(bf16[4,2,128]{2,1,0:T(2,128)(2,1)} %param.26) | copy-start | bytes 6148
  0.0 13.7 %copy-start.18 = (f32[16]{0:T(128)S(1)}, f32[16]{0:T(128)}, u32[]{:S(2)}) copy-start(f32[16]{0:T(128)} %param.30) | copy-start | bytes 196
  0.0 13.7 %copy-start.6 = (f32[512,16]{0,1:T(8,128)S(1)}, f32[512,16]{0,1:T(8,128)}, u32[]{:S(2)}) copy-start(f32[512,16]{0,1:T(8,128)} %param.24) | copy-start | bytes 98308
  0.0 13.7 %copy-start.17 = (f32[16]{0:T(128)S(1)}, f32[16]{0:T(128)}, u32[]{:S(2)}) copy-start(f32[16]{0:T(128)} %param.29) | copy-start | bytes 196
  0.0 15.7 %copy-start.7 = (bf16[4,1024]{1,0:T(4,128)(2,1)S(1)}, bf16[4,1024]{1,0:T(4,128)(2,1)}, u32[]{:S(2)}) copy-start(bf16[4,1024]{1,0:T(4,128)(2,1)} %param.25) | copy-start | bytes 24580
  0.0 17.4 %copy-start.16 = (f32[2,128]{1,0:T(2,128)S(1)}, f32[2,128]{1,0:T(2,128)}, u32[]{:S(2)}) copy-start(f32[2,128]{1,0:T(2,128)} %param.28) | copy-start | bytes 3076
  1.1 16.3 %collective-permute-start.2 = (bf16[3,2,128]{2,0,1:T(4,128)(2,1)S(1)}, bf16[3,2,128]{2,0,1:T(4,128)(2,1)S(1)}, u32[]{:S(2)}, u32[]{:S(2)}) collective-permute-start(bf16[3,2,128]{2,0,1:T(4,128)(2,1)S(1)} %slice.232), channel_id=1, source_target_pairs={{0,8},{8,16},{16,24},{24,32},{32,40},{40,48},{48,56},{56,64},{64,7... | collective-permute-start | bytes 4616 | tf_op jit(solution)/shard_map/ppermute | solution.py:13
  5.7 10.0 %collective-permute-start = (bf16[3]{0:T(256)(128)(2,1)S(1)}, bf16[3]{0:T(256)(128)(2,1)S(1)}, u32[]{:S(2)}, u32[]{:S(2)}) collective-permute-start(bf16[3]{0:T(256)(128)(2,1)S(1)} %slice.190), channel_id=1, source_target_pairs={{0,8},{8,16},{16,24},{24,32},{32,40},{40,48},{48,56},{56,64},{64,7... | collective-permute-start | bytes 26 | tf_op jit(solution)/shard_map/ppermute | solution.py:13
  8.6 10.4 %copy-start.11 = (f32[1024]{0:T(1024)S(1)}, f32[1024]{0:T(1024)}, u32[]{:S(2)}) copy-start(f32[1024]{0:T(1024)} %param.27) | copy-start | bytes 12292
  8.6 10.4 %collective-permute-start.1 = (bf16[3,1024]{0,1:T(8,128)(2,1)S(1)}, bf16[3,1024]{0,1:T(8,128)(2,1)S(1)}, u32[]{:S(2)}, u32[]{:S(2)}) collective-permute-start(bf16[3,1024]{0,1:T(8,128)(2,1)S(1)} %copy.39), channel_id=1, source_target_pairs={{0,8},{8,16},{16,24},{24,32},{32,40},{40,48},{48,56},{56,64},{64,7... | collective-permute-start | bytes 18440 | tf_op jit(solution)/shard_map/ppermute | solution.py:13
  22.1 2.9 %copy-start.2 = (bf16[2,256,16,64]{1,0,3,2:T(2,128)(2,1)}, bf16[2,256,16,64]{1,0,3,2:T(2,128)(2,1)S(1)}, u32[]{:S(2)}) copy-start(bf16[2,256,16,64]{1,0,3,2:T(2,128)(2,1)S(1)} %reshape.468) | copy-start | bytes 3145732
  22.1 2.8 %copy-start.9 = (f32[16]{0:T(128)S(1)}, f32[16]{0:T(128)}, u32[]{:S(2)}) copy-start(f32[16]{0:T(128)} %get-tuple-element.82) | copy-start | bytes 196
  22.1 2.9 %copy-start.10 = (f32[1,16]{1,0:T(1,128)S(1)}, f32[1,16]{1,0:T(1,128)}, u32[]{:S(2)}) copy-start(f32[1,16]{1,0:T(1,128)} %get-tuple-element.83) | copy-start | bytes 196
  24.9 4.1 %copy-start.14 = (f32[16]{0:T(128)S(1)}, f32[16]{0:T(128)}, u32[]{:S(2)}) copy-start(f32[16]{0:T(128)} %get-tuple-element.81) | copy-start | bytes 196
  25.1 3.8 %collective-permute-start.3 = (f32[1032,128]{1,0:T(8,128)S(1)}, f32[1032,128]{1,0:T(8,128)S(1)}, u32[]{:S(2)}, u32[]{:S(2)}) collective-permute-start(f32[1032,128]{1,0:T(8,128)S(1)} %select_maximum_fusion.3), channel_id=1, source_target_pairs={{0,8},{16,24},{32,40},{48,56},{64,72},{80,88},{96,104},{112,120},{... | collective-permute-start | bytes 1585160 | tf_op jit(solution)/shard_map/ppermute | solution.py:17
  28.9 12.4 %copy-start = (f32[1024,128]{1,0:T(8,128)}, f32[1024,128]{1,0:T(8,128)S(1)}, u32[]{:S(2)}) copy-start(f32[1024,128]{1,0:T(8,128)S(1)} %slice.246) | copy-start | bytes 1572868
  29.2 12.1 %collective-permute-start.4 = (f32[1032,128]{1,0:T(8,128)S(1)}, f32[1032,128]{1,0:T(8,128)S(1)}, u32[]{:S(2)}, u32[]{:S(2)}) collective-permute-start(f32[1032,128]{1,0:T(8,128)S(1)} %select_maximum_fusion.2), channel_id=1, source_target_pairs={{8,24},{24,40},{40,56},{56,72},{72,88},{88,104},{104,120},{120,136... | collective-permute-start | bytes 1585160 | tf_op jit(solution)/shard_map/ppermute | solution.py:17
  41.5 17.8 %collective-permute-start.5 = (f32[1032,128]{1,0:T(8,128)S(1)}, f32[1032,128]{1,0:T(8,128)S(1)}, u32[]{:S(2)}, u32[]{:S(2)}) collective-permute-start(f32[1032,128]{1,0:T(8,128)S(1)} %select_maximum_fusion.1), channel_id=1, source_target_pairs={{8,40},{24,56},{40,72},{56,88},{72,104},{88,120},{104,136},{120,15... | collective-permute-start | bytes 1585160 | tf_op jit(solution)/shard_map/ppermute | solution.py:17
  59.5 19.0 %collective-permute-start.6 = (f32[1032,128]{1,0:T(8,128)S(1)}, f32[1032,128]{1,0:T(8,128)S(1)}, u32[]{:S(2)}, u32[]{:S(2)}) collective-permute-start(f32[1032,128]{1,0:T(8,128)S(1)} %select_maximum_fusion), channel_id=1, source_target_pairs={{8,72},{24,88},{40,104},{56,120},{72,136},{88,152},{104,168},{120,... | collective-permute-start | bytes 1585160 | tf_op jit(solution)/shard_map/ppermute | solution.py:17
  79.5 9.9 %collective-permute-start.7 = (f32[1,16,64,128]{3,2,1,0:T(8,128)}, f32[1,16,64,128]{3,2,1,0:T(8,128)}, u32[]{:S(2)}, u32[]{:S(2)}) collective-permute-start(f32[1,16,64,128]{3,2,1,0:T(8,128)} %multiply_add_fusion), channel_id=1, source_target_pairs={{8,16},{24,32},{40,48},{56,64},{72,80},{88,96},{104,112},{120,128}... | collective-permute-start | bytes 1572872 | tf_op jit(solution)/shard_map/ppermute | solution.py:17
  81.6 12.3 %collective-permute-start.8 = (f32[1,16,64,128]{3,2,1,0:T(8,128)}, f32[1,16,64,128]{3,2,1,0:T(8,128)}, u32[]{:S(2)}, u32[]{:S(2)}) collective-permute-start(f32[1,16,64,128]{3,2,1,0:T(8,128)} %multiply_add_fusion), channel_id=1, source_target_pairs={{8,24},{24,40},{40,56},{56,72},{72,88},{88,104},{104,120},{120,136... | collective-permute-start | bytes 1572872 | tf_op jit(solution)/shard_map/ppermute | solution.py:17
  86.0 7.9 %copy-start.13 = (f32[16]{0:T(128)S(1)}, f32[16]{0:T(128)}, u32[]{:S(2)}) copy-start(f32[16]{0:T(128)} %get-tuple-element.84) | copy-start | bytes 196
  93.9 2.5 %copy-start.4 = (f32[2,256,256]{2,1,0:T(8,128)S(1)}, f32[2,256,256]{2,1,0:T(8,128)}, u32[]{:S(2)}) copy-start(f32[2,256,256]{2,1,0:T(8,128)} %fusion.34) | copy-start | bytes 1572868
  95.4 1.6 %copy-start.1 = (f32[2,256,1,16,64]{1,0,4,3,2:T(2,128)S(1)}, f32[2,256,1,16,64]{1,0,4,3,2:T(2,128)}, u32[]{:S(2)}) copy-start(f32[2,256,1,16,64]{1,0,4,3,2:T(2,128)} %reshape.494) | copy-start | bytes 6291460
  95.4 1.8 %copy-start.3 = (bf16[2,256,16,64]{1,0,3,2:T(2,128)(2,1)S(1)}, bf16[2,256,16,64]{1,0,3,2:T(2,128)(2,1)}, u32[]{:S(2)}) copy-start(bf16[2,256,16,64]{1,0,3,2:T(2,128)(2,1)} %copy-done.2) | copy-start | bytes 3145732
  95.4 1.8 %copy-start.5 = (pred[2,256,256]{2,1,0:T(8,128)(4,1)S(1)}, pred[2,256,256]{2,1,0:T(8,128)(4,1)}, u32[]{:S(2)}) copy-start(pred[2,256,256]{2,1,0:T(8,128)(4,1)} %compare_and_fusion) | copy-start | bytes 393220
  95.4 1.8 %copy-start.19 = (f32[16]{0:T(128)S(1)}, f32[16]{0:T(128)}, u32[]{:S(2)}) copy-start(f32[16]{0:T(128)} %param.31) | copy-start | bytes 196
  102.0 21.8 %copy-start.12 = (f32[1024]{0:T(1024)S(1)}, f32[1024]{0:T(1024)}, u32[]{:S(2)}) copy-start(f32[1024]{0:T(1024)} %param.32) | copy-start | bytes 12292
  102.6 5.0 %collective-permute-start.9 = (f32[512]{0:T(512)S(1)}, f32[512]{0:T(512)S(1)}, u32[]{:S(2)}, u32[]{:S(2)}) collective-permute-start(f32[512]{0:T(512)S(1)} %multiply_reduce_fusion), channel_id=1, source_target_pairs={{0,1},{1,0},{2,3},{3,2},{4,5},{5,4},{6,7},{7,6},{8,9},{9,8},{10,11... | collective-permute-start | bytes 6152 | tf_op jit(solution)/shard_map/ppermute | solution.py:65
  107.6 6.8 %collective-permute-start.10 = (f32[512]{0:T(512)S(1)}, f32[512]{0:T(512)S(1)}, u32[]{:S(2)}, u32[]{:S(2)}) collective-permute-start(f32[512]{0:T(512)S(1)} %add.137), channel_id=1, source_target_pairs={{0,2},{1,3},{2,0},{3,1},{4,6},{5,7},{6,4},{7,5},{8,10},{9,11},{10,... | collective-permute-start | bytes 6152 | tf_op jit(solution)/shard_map/ppermute | solution.py:65
  114.4 9.4 %collective-permute-start.11 = (f32[512]{0:T(512)S(1)}, f32[512]{0:T(512)S(1)}, u32[]{:S(2)}, u32[]{:S(2)}) collective-permute-start(f32[512]{0:T(512)S(1)} %add.138), channel_id=1, source_target_pairs={{0,4},{1,5},{2,6},{3,7},{4,0},{5,1},{6,2},{7,3},{8,12},{9,13},{10,... | collective-permute-start | bytes 6152 | tf_op jit(solution)/shard_map/ppermute | solution.py:65

commit v3 on v2

--- a/solution.py
+++ b/solution.py
@@ -38,7 +38,7 @@
     return (packed[rows, :count].reshape(gain_shape), packed[:rows].reshape(state_shape))
 
 
-def entering_state(gain, state, axis):
+def entering_state(gain, state, axis, ride):
     count = lax.axis_size(axis)
     chips = count // 2
     shapes = (gain.shape, state.shape)
@@ -48,12 +48,14 @@
     for reach in (1, 2, 4):
         route = [(2 * c + 1, 2 * (c + reach) + 1) for c in range(chips - reach)]
         got = unpack(shifted(pack(*chip_total), axis, route), *shapes)
+        if reach == 4:
+            got, ride = lax.optimization_barrier((got, ride))
         chip_total = fold(got, chip_total)
     to_even = shifted(chip_total[1], axis, [(2 * c - 1, 2 * c) for c in range(1, chips)])
     to_odd = shifted(chip_total[1], axis, [(2 * c - 1, 2 * c + 1) for c in range(1, chips)])
     odd_entering = pair[0][..., None, None] * to_odd + pair[1]
     mine = lax.axis_index(axis)
-    return jnp.where(mine % 2 == 0, to_even, odd_entering)
+    return jnp.where(mine % 2 == 0, to_even, odd_entering), ride
 
 
 def summed_over(value, axis):
@@ -103,12 +105,19 @@
     block = STRETCH
     blocks = tok_rows // block
     margin = conv_x.shape[0] - 1
-    tails = (
-        x_proj[tok_rows - margin :],
-        bc_proj[tok_rows - margin :],
-        seg_ids[tok_rows - margin :].astype(jnp.bfloat16),
-    )
-    rim_x, rim_bc, rim_ids = from_behind((tails[0], tails[1], tails[2]), "seq", 1)
+    bc_width = bc_proj.shape[1] * bc_proj.shape[2]
+    rim = jnp.concatenate(
+        [
+            x_proj[tok_rows - margin :],
+            bc_proj[tok_rows - margin :].reshape(margin, bc_width),
+            jnp.broadcast_to(seg_ids[tok_rows - margin :, None].astype(jnp.bfloat16), (margin, 128)),
+        ],
+        axis=1,
+    )
+    rim = from_behind(rim, "seq", 1)
+    rim_x = rim[:, :inner_local]
+    rim_bc = rim[:, inner_local : inner_local + bc_width].reshape(margin, *bc_proj.shape[1:])
+    rim_ids = rim[:, inner_local + bc_width]
     own_ids = seg_ids.astype(jnp.float32)
     window_ids = jnp.concatenate([rim_ids.astype(jnp.float32), own_ids])
     x_conv = causal_conv(jnp.concatenate([rim_x, x_proj]), window_ids, conv_x, bias_x, tok_rows)
@@ -162,13 +171,17 @@
     empty = jnp.zeros((groups_local, heads_group, head_size, state_size), jnp.float32)
     zero_states, summary = recur(empty)
     device_gain = carry_gain[0] * carry_gain[1]
-    entering = entering_state(device_gain, summary, "seq")
+    skip = d_skip.reshape(groups_local, heads_group)[..., None]
+    base = (y_intra + skip * x_heads.astype(jnp.float32)).reshape(tok_rows, inner_local)
+    gate = jax.nn.silu(z_proj.astype(jnp.float32))
+    entering, (early, gate) = entering_state(device_gain, summary, "seq", (base * gate, gate))
     states, _ = recur(entering)
-    product = jnp.einsum("cqgn,cghpn->cqghp", c_float, states, precision=lax.Precision.HIGHEST)
-    y_inter = product * link.transpose(0, 3, 1, 2)[..., None]
-    skip = d_skip.reshape(groups_local, heads_group)[..., None]
-    mixed = y_intra + y_inter + skip * x_heads.astype(jnp.float32)
-    gated = mixed.reshape(tok_rows, inner_local) * jax.nn.silu(z_proj.astype(jnp.float32))
+    lanes = heads_group * head_size
+    states_t = states.transpose(0, 1, 4, 2, 3).reshape(blocks, groups_local, state_size, lanes)
+    product = jnp.einsum("cqgn,cgnk->cqgk", c_float, states_t, precision=lax.Precision.HIGHEST)
+    product = product.reshape(blocks, block, groups_local, heads_group, head_size)
+    y_inter = (product * link.transpose(0, 3, 1, 2)[..., None]).reshape(tok_rows, inner_local)
+    gated = early + y_inter * gate
     squares = summed_over(jnp.sum(gated * gated, axis=-1), "tp")
     scale = lax.rsqrt(squares / (inner_local * lax.axis_size("tp")) + 1e-05)
     return (gated * scale[:, None] * norm_gain).astype(jnp.bfloat16)

time: 128 us -> 137 us (1.070)
  the two profiles are of different devices: /device:TPU:5 before, /device:TPU:6 now
where the time goes in v3:
time: 137 us; the launch traced here: 136 us
  waiting for transfers between devices  54.5 us (40%)
  starting transfers between devices  29.1 us (21%)
  other arithmetic  23.1 us (17%)
  local copies, waits for them, and re-layouts  20.1 us (15%)
  matrix products  8.16 us (6%)
    ppermute x6, waiting for transfers between devices, shifted(): return lax.ppermute(block, axis, pairs)  48 us
    ppermute x3, starting transfers between devices, summed_over(): lax.ppermute(value, axis, [(i, i ^ reach) for i in range(count)])  19.6 us
    ppermute x6, starting transfers between devices, shifted(): return lax.ppermute(block, axis, pairs)  7.52 us
    unnamed x41, local copies, waits for them, and re-layouts  7.35 us
    ppermute x3, waiting for transfers between devices, summed_over(): lax.ppermute(value, axis, [(i, i ^ reach) for i in range(count)])  4.65 us
    reduce_sum x1, other arithmetic, on_device(): squares = summed_over(jnp.sum(gated * gated, axis=-1), 'tp')  3.72 us
    convert_element_type x2, other arithmetic, causal_conv(): return jax.nn.silu(result).astype(jnp.bfloat16)  3.68 us
    reshape x1, local copies, waits for them, and re-layouts, on_device(): product.reshape(blocks, block, groups_local, heads_group, head_size)  2.91 us
  transfers between devices with their start and end apart: 10, of which 6 were waited for; matrix products, arithmetic and copies ran while one was open for 16% of the time, Pallas kernels for 0%

profile of v3, /device:TPU:6, one launch (start us, length us, event | category | flops | bytes accessed | tf_op | source)
XLA Modules:
  0.0 135.5 jit_solution(1731282641454304379)
XLA Ops:
  2.7 1.9 %collective-permute-start = (bf16[3,1408]{0,1:T(8,128)(2,1)S(1)}, bf16[3,1408]{0,1:T(8,128)(2,1)S(1)}, u32[]{:S(2)}, u32[]{:S(2)}) collective-permute-start(bf16[3,1408]{0,1:T(8,128)(2,1)S(1)} %copy.67), channel_id=1, source_target_pairs={{0,8},{8,16},{16,24},{24,32},{32,40},{40,48},{48,56},{56,64},{64,7... | collective-permute-start | bytes 25352 | tf_op jit(solution)/shard_map/ppermute | solution.py:13
  7.8 1.2 reduce-window.6
  10.1 1.0 copy.72
  11.7 1.9 %collective-permute-done = bf16[3,1408]{0,1:T(8,128)(2,1)S(1)} collective-permute-done((bf16[3,1408]{0,1:T(8,128)(2,1)S(1)}, bf16[3,1408]{0,1:T(8,128)(2,1)S(1)}, u32[]{:S(2)}, u32[]{:S(2)}) %collective-permute-start) | collective-permute-done | bytes 8480 | tf_op jit(solution)/shard_map/ppermute | solution.py:13
  16.8 2.8 %multiply_convert_fusion.5 = bf16[512,1024]{0,1:T(8,128)(2,1)S(1)} fusion(bf16[512,1024]{0,1:T(8,128)(2,1)S(1)} %copy.68, bf16[3,1024]{0,1:T(8,128)(2,1)S(1)} %slice.246, f32[1024]{0:T(1024)S(1)} %bitcast.161, f32[1024]{0:T(1024)S(1)} %bitcast.162, f32[1024]{0:T(1024)S(1)} %bitcast.160, f32[1024]{0:T(1024)S(1)} %bitcast.159, f32[1024]{0:T(1024)S(1)} %copy-done.9, ...), kind=kLoop, calls=%fused_computation.22 | loop fusion | flops 15728640 | bytes 2125824 | tf_op jit(solution)/shard_map/convert_element_type | solution.py:81
  20.0 2.7 %fusion.10 = f32[2,16,64,128]{3,2,1,0:T(8,128)S(1)} fusion(f32[2,16,256]{2,1,0:T(8,128)S(1)} %fusion.20, f32[2,256,128]{2,1,0:T(8,128)} %convert_element_type.129, bf16[2,256,16,64]{1,0,3,2:T(2,128)(2,1)S(1)} %reshape.483), kind=kOutput, calls=%fused_computation.14 | convolution fusion | flops 136314880 | bytes 2392064 | tf_op jit(solution)/shard_map/cghsn,csghp->cghpn/dot_general | solution.py:150
  23.0 1.8 %collective-permute-start.1 = (f32[1032,128]{1,0:T(8,128)S(1)}, f32[1032,128]{1,0:T(8,128)S(1)}, u32[]{:S(2)}, u32[]{:S(2)}) collective-permute-start(f32[1032,128]{1,0:T(8,128)S(1)} %select_maximum_fusion.3), channel_id=1, source_target_pairs={{0,8},{16,24},{32,40},{48,56},{64,72},{80,88},{96,104},{112,120},{... | collective-permute-start | bytes 1585160 | tf_op jit(solution)/shard_map/ppermute | solution.py:17
  24.7 1.5 %collective-permute-done.1 = f32[1032,128]{1,0:T(8,128)S(1)} collective-permute-done((f32[1032,128]{1,0:T(8,128)S(1)}, f32[1032,128]{1,0:T(8,128)S(1)}, u32[]{:S(2)}, u32[]{:S(2)}) %collective-permute-start.1) | collective-permute-done | bytes 528416 | tf_op jit(solution)/shard_map/ppermute | solution.py:17
  28.8 1.5 %collective-permute-start.3 = (f32[1032,128]{1,0:T(8,128)}, f32[1032,128]{1,0:T(8,128)}, u32[]{:S(2)}, u32[]{:S(2)}) collective-permute-start(f32[1032,128]{1,0:T(8,128)} %select_maximum_fusion.1), channel_id=1, source_target_pairs={{8,40},{24,56},{40,72},{56,88},{72,104},{88,120},{104,136},{120,15... | collective-permute-start | bytes 1585160 | tf_op jit(solution)/shard_map/ppermute | solution.py:17
  30.3 2.3 %copy.79 = bf16[512,1024]{0,1:T(8,128)(2,1)} copy(bf16[512,1024]{1,0:T(8,128)(2,1)} %param.23) | data formatting | bytes 2097152 | tf_op args[2]
  33.4 2.3 %reshape.507 = f32[2,256,1,16,64]{1,0,4,3,2:T(2,128)} reshape(bf16[512,1024]{0,1:T(8,128)(2,1)S(1)} %multiply_convert_fusion.5) | data formatting | bytes 3145728 | tf_op jit(solution)/shard_map/convert_element_type | solution.py:175
  35.9 1.2 slice.263
  38.7 2.8 %bitcast_add_fusion = f32[2,256,1,16,64]{1,4,3,0,2:T(8,128)S(1)} fusion(f32[2,256,1,16,64]{1,0,4,3,2:T(2,128)S(1)} %copy-done.3, f32[2,16,256]{2,1,0:T(8,128)S(1)} %bitcast.158, f32[2,16,256]{2,1,0:T(8,128)S(1)} %get-tuple-element.73, f32[2,256,256]{2,1,0:T(8,128)S(1)} %fusion.29, pred[2,256,256]{2,1,0:T(8,128)(4,1)S(1)} %copy-done.7, ...), kind=kOutput, calls=%fused_computation.15 | convolution fusion | flops 282066944 | bytes 5963840 | tf_op jit(solution)/shard_map/cghqs,csghp->cqghp/dot_general | solution.py:144
  41.5 1.6 %copy.78 = f32[2,256,1,16,64]{1,0,4,3,2:T(2,128)S(1)} copy(f32[2,256,1,16,64]{1,4,3,0,2:T(8,128)S(1)} %bitcast_add_fusion) | data formatting | bytes 4194304 | tf_op jit(solution)/shard_map/add | solution.py:175
  43.4 1.0 copy-done.2
  44.4 2.1 %convert_multiply_fusion = (f32[512,1024]{0,1:T(8,128)S(1)}, f32[512,1024]{0,1:T(8,128)}) fusion(bf16[512,1024]{0,1:T(8,128)(2,1)S(1)} %copy-done.2, f32[512,1024]{0,1:T(8,128)S(1)} %bitcast.136), kind=kLoop, calls=%fused_computation.9 | loop fusion | flops 3145728 | bytes 7340032 | tf_op jit(solution)/shard_map/jit(silu)/mul | solution.py:176
  46.5 0.9 multiply_add_fusion.1
  47.5 1.5 %collective-permute-start.6 = (f32[1,16,64,128]{3,2,1,0:T(8,128)}, f32[1,16,64,128]{3,2,1,0:T(8,128)}, u32[]{:S(2)}, u32[]{:S(2)}) collective-permute-start(f32[1,16,64,128]{3,2,1,0:T(8,128)} %multiply_add_fusion.1), channel_id=1, source_target_pairs={{8,24},{24,40},{40,56},{56,72},{72,88},{88,104},{104,120},{120,136... | collective-permute-start | bytes 1572872 | tf_op jit(solution)/shard_map/ppermute | solution.py:17
  48.9 1.5 %collective-permute-start.5 = (f32[1,16,64,128]{3,2,1,0:T(8,128)}, f32[1,16,64,128]{3,2,1,0:T(8,128)}, u32[]{:S(2)}, u32[]{:S(2)}) collective-permute-start(f32[1,16,64,128]{3,2,1,0:T(8,128)} %multiply_add_fusion.1), channel_id=1, source_target_pairs={{8,16},{24,32},{40,48},{56,64},{72,80},{88,96},{104,112},{120,128}... | collective-permute-start | bytes 1572872 | tf_op jit(solution)/shard_map/ppermute | solution.py:17
  51.1 1.5 %copy.92 = f32[128,8,2,256]{3,1,2,0:T(8,128)} copy(f32[128,8,2,256]{3,2,1,0:T(2,128)S(1)} %bitcast.139) | data formatting | bytes 4194304
  52.6 46.5 %collective-permute-done.5 = f32[1,16,64,128]{3,2,1,0:T(8,128)} collective-permute-done((f32[1,16,64,128]{3,2,1,0:T(8,128)}, f32[1,16,64,128]{3,2,1,0:T(8,128)}, u32[]{:S(2)}, u32[]{:S(2)}) %collective-permute-start.5) | collective-permute-done | bytes 524320 | tf_op jit(solution)/shard_map/ppermute | solution.py:17
  99.1 1.4 %add_bitcast_fusion = (f32[1,1,16,64,128]{4,3,2,1,0:T(8,128)S(1)}, f32[1,16,64,128]{3,2,1,0:T(8,128)S(1)}) fusion(f32[2,16,64,128]{3,2,1,0:T(8,128)S(1)} %fusion.10, f32[16]{0:T(128)S(1)} %copy-done.12, f32[1,16,64,128]{3,2,1,0:T(8,128)} %collective-permute-done.5, f32[1,16,64,128]{3,2,1,0:T(8,128)S(1)} %bitcast.142, ...), kind=kLoop, calls=%fused_computation.39 | loop fusion | flops 655360 | bytes 3145857 | tf_op jit(solution)/shard_map/stack | solution.py:169
  100.6 2.4 %fusion.30 = f32[2,1024,256]{1,2,0:T(8,128)} fusion(f32[2,128,1024]{1,2,0:T(8,128)S(1)} %bitcast.146, bf16[2,256,128]{2,1,0:T(8,128)(2,1)S(1)} %bitcast.153), kind=kOutput, calls=%fused_computation.108 | convolution fusion | flops 805306368 | bytes 3276800 | tf_op jit(solution)/shard_map/cqgn,cgnk->cqgk/dot_general | solution.py:181
  103.0 2.9 %copy.82 = f32[512,1024]{0,1:T(8,128)} copy(f32[512,1024]{1,0:T(8,128)} %bitcast.137) | data formatting | bytes 4194304 | tf_op jit(solution)/shard_map/reshape | solution.py:182
  105.9 3.7 %multiply_reduce_fusion = (f32[512]{0:T(512)S(1)}, f32[512,1024]{0,1:T(8,128)S(1)}) fusion(f32[512,1024]{0,1:T(8,128)} %get-tuple-element.56, f32[512,1024]{0,1:T(8,128)S(1)} %get-tuple-element.58, f32[512,1024]{0,1:T(8,128)} %copy.82, f32[512,1024]{0,1:T(8,128)} %bitcast.140), kind=kLoop, calls=%fused_computation.18 | loop fusion | flops 2620928 | bytes 10487808 | tf_op jit(solution)/shard_map/reduce_sum | solution.py:185
  109.6 4.3 %collective-permute-start.7 = (f32[512]{0:T(512)S(1)}, f32[512]{0:T(512)S(1)}, u32[]{:S(2)}, u32[]{:S(2)}) collective-permute-start(f32[512]{0:T(512)S(1)} %get-tuple-element.61), channel_id=1, source_target_pairs={{0,1},{1,0},{2,3},{3,2},{4,5},{5,4},{6,7},{7,6},{8,9},{9,8},{10,11... | collective-permute-start | bytes 6152 | tf_op jit(solution)/shard_map/ppermute | solution.py:67
  113.9 1.5 %collective-permute-done.7 = f32[512]{0:T(512)S(1)} collective-permute-done((f32[512]{0:T(512)S(1)}, f32[512]{0:T(512)S(1)}, u32[]{:S(2)}, u32[]{:S(2)}) %collective-permute-start.7) | collective-permute-done | bytes 2080 | tf_op jit(solution)/shard_map/ppermute | solution.py:67
  115.4 6.1 %collective-permute-start.8 = (f32[512]{0:T(512)S(1)}, f32[512]{0:T(512)S(1)}, u32[]{:S(2)}, u32[]{:S(2)}) collective-permute-start(f32[512]{0:T(512)S(1)} %add.137), channel_id=1, source_target_pairs={{0,2},{1,3},{2,0},{3,1},{4,6},{5,7},{6,4},{7,5},{8,10},{9,11},{10,... | collective-permute-start | bytes 6152 | tf_op jit(solution)/shard_map/ppermute | solution.py:67
  121.5 1.5 %collective-permute-done.8 = f32[512]{0:T(512)S(1)} collective-permute-done((f32[512]{0:T(512)S(1)}, f32[512]{0:T(512)S(1)}, u32[]{:S(2)}, u32[]{:S(2)}) %collective-permute-start.8) | collective-permute-done | bytes 2080 | tf_op jit(solution)/shard_map/ppermute | solution.py:67
  123.1 9.3 %collective-permute-start.9 = (f32[512]{0:T(512)S(1)}, f32[512]{0:T(512)S(1)}, u32[]{:S(2)}, u32[]{:S(2)}) collective-permute-start(f32[512]{0:T(512)S(1)} %add.138), channel_id=1, source_target_pairs={{0,4},{1,5},{2,6},{3,7},{4,0},{5,1},{6,2},{7,3},{8,12},{9,13},{10,... | collective-permute-start | bytes 6152 | tf_op jit(solution)/shard_map/ppermute | solution.py:67
  132.4 1.5 %collective-permute-done.9 = f32[512]{0:T(512)S(1)} collective-permute-done((f32[512]{0:T(512)S(1)}, f32[512]{0:T(512)S(1)}, u32[]{:S(2)}, u32[]{:S(2)}) %collective-permute-start.9) | collective-permute-done | bytes 2080 | tf_op jit(solution)/shard_map/ppermute | solution.py:67
  134.2 1.3 copy.83
  (105 shorter events, 17.6 us)
Async XLA Ops:
  0.0 13.8 %copy-start.8 = (s32[512]{0:T(512)S(1)}, s32[512]{0:T(512)}, u32[]{:S(2)}) copy-start(s32[512]{0:T(512)} %param.33) | copy-start | bytes 6148
  0.0 11.1 %copy-start.4 = (bf16[512,1024]{1,0:T(8,128)(2,1)S(1)}, bf16[512,1024]{1,0:T(8,128)(2,1)}, u32[]{:S(2)}) copy-start(bf16[512,1024]{1,0:T(8,128)(2,1)} %param.21) | copy-start | bytes 3145732
  0.0 15.1 %copy-start.15 = (f32[2,128]{1,0:T(2,128)S(1)}, f32[2,128]{1,0:T(2,128)}, u32[]{:S(2)}) copy-start(f32[2,128]{1,0:T(2,128)} %param.28) | copy-start | bytes 3076
  2.7 10.9 %collective-permute-start = (bf16[3,1408]{0,1:T(8,128)(2,1)S(1)}, bf16[3,1408]{0,1:T(8,128)(2,1)S(1)}, u32[]{:S(2)}, u32[]{:S(2)}) collective-permute-start(bf16[3,1408]{0,1:T(8,128)(2,1)S(1)} %copy.67), channel_id=1, source_target_pairs={{0,8},{8,16},{16,24},{24,32},{32,40},{40,48},{48,56},{56,64},{64,7... | collective-permute-start | bytes 25352 | tf_op jit(solution)/shard_map/ppermute | solution.py:13
  11.1 5.6 %copy-start.9 = (f32[1024]{0:T(1024)S(1)}, f32[1024]{0:T(1024)}, u32[]{:S(2)}) copy-start(f32[1024]{0:T(1024)} %param.27) | copy-start | bytes 12292
  16.7 3.2 %copy-start.11 = (f32[2,16]{1,0:T(2,128)S(1)}, f32[2,16]{1,0:T(2,128)}, u32[]{:S(2)}) copy-start(f32[2,16]{1,0:T(2,128)} %get-tuple-element.59) | copy-start | bytes 388
  19.9 2.9 %copy-start.5 = (bf16[2,256,16,64]{1,0,3,2:T(2,128)(2,1)}, bf16[2,256,16,64]{1,0,3,2:T(2,128)(2,1)S(1)}, u32[]{:S(2)}) copy-start(bf16[2,256,16,64]{1,0,3,2:T(2,128)(2,1)S(1)} %reshape.483) | copy-start | bytes 3145732
  22.7 3.5 %copy-start.14 = (f32[16]{0:T(128)S(1)}, f32[16]{0:T(128)}, u32[]{:S(2)}) copy-start(f32[16]{0:T(128)} %get-tuple-element.94) | copy-start | bytes 196
  23.0 3.3 %collective-permute-start.1 = (f32[1032,128]{1,0:T(8,128)S(1)}, f32[1032,128]{1,0:T(8,128)S(1)}, u32[]{:S(2)}, u32[]{:S(2)}) collective-permute-start(f32[1032,128]{1,0:T(8,128)S(1)} %select_maximum_fusion.3), channel_id=1, source_target_pairs={{0,8},{16,24},{32,40},{48,56},{64,72},{80,88},{96,104},{112,120},{... | collective-permute-start | bytes 1585160 | tf_op jit(solution)/shard_map/ppermute | solution.py:17
  26.3 1.5 %copy-start = (f32[1024,128]{1,0:T(8,128)}, f32[1024,128]{1,0:T(8,128)S(1)}, u32[]{:S(2)}) copy-start(f32[1024,128]{1,0:T(8,128)S(1)} %slice.259) | copy-start | bytes 1572868
  27.0 0.7 collective-permute-start.2
  28.8 7.1 %collective-permute-start.3 = (f32[1032,128]{1,0:T(8,128)}, f32[1032,128]{1,0:T(8,128)}, u32[]{:S(2)}, u32[]{:S(2)}) collective-permute-start(f32[1032,128]{1,0:T(8,128)} %select_maximum_fusion.1), channel_id=1, source_target_pairs={{8,40},{24,56},{40,72},{56,88},{72,104},{88,120},{104,136},{120,15... | collective-permute-start | bytes 1585160 | tf_op jit(solution)/shard_map/ppermute | solution.py:17
  35.6 3.0 %copy-start.3 = (f32[2,256,1,16,64]{1,0,4,3,2:T(2,128)S(1)}, f32[2,256,1,16,64]{1,0,4,3,2:T(2,128)}, u32[]{:S(2)}) copy-start(f32[2,256,1,16,64]{1,0,4,3,2:T(2,128)} %reshape.507) | copy-start | bytes 6291460
  35.6 3.0 %copy-start.6 = (bf16[2,256,16,64]{1,0,3,2:T(2,128)(2,1)S(1)}, bf16[2,256,16,64]{1,0,3,2:T(2,128)(2,1)}, u32[]{:S(2)}) copy-start(bf16[2,256,16,64]{1,0,3,2:T(2,128)(2,1)} %copy-done.5) | copy-start | bytes 3145732
  35.6 3.1 %copy-start.7 = (pred[2,256,256]{2,1,0:T(8,128)(4,1)S(1)}, pred[2,256,256]{2,1,0:T(8,128)(4,1)}, u32[]{:S(2)}) copy-start(pred[2,256,256]{2,1,0:T(8,128)(4,1)} %compare_and_fusion) | copy-start | bytes 393220
  35.6 3.1 %copy-start.16 = (f32[16]{0:T(128)S(1)}, f32[16]{0:T(128)}, u32[]{:S(2)}) copy-start(f32[16]{0:T(128)} %param.31) | copy-start | bytes 196
  38.0 8.5 %collective-permute-start.4 = (f32[1032,128]{1,0:T(8,128)S(1)}, f32[1032,128]{1,0:T(8,128)S(1)}, u32[]{:S(2)}, u32[]{:S(2)}) collective-permute-start(f32[1032,128]{1,0:T(8,128)S(1)} %select_maximum_fusion), channel_id=1, source_target_pairs={{8,72},{24,88},{40,104},{56,120},{72,136},{88,152},{104,168},{120,... | collective-permute-start | bytes 1585160 | tf_op jit(solution)/shard_map/ppermute | solution.py:17
  43.2 1.2 copy-start.2
  47.5 5.1 %collective-permute-start.6 = (f32[1,16,64,128]{3,2,1,0:T(8,128)}, f32[1,16,64,128]{3,2,1,0:T(8,128)}, u32[]{:S(2)}, u32[]{:S(2)}) collective-permute-start(f32[1,16,64,128]{3,2,1,0:T(8,128)} %multiply_add_fusion.1), channel_id=1, source_target_pairs={{8,24},{24,40},{40,56},{56,72},{72,88},{88,104},{104,120},{120,136... | collective-permute-start | bytes 1572872 | tf_op jit(solution)/shard_map/ppermute | solution.py:17
  48.9 50.2 %collective-permute-start.5 = (f32[1,16,64,128]{3,2,1,0:T(8,128)}, f32[1,16,64,128]{3,2,1,0:T(8,128)}, u32[]{:S(2)}, u32[]{:S(2)}) collective-permute-start(f32[1,16,64,128]{3,2,1,0:T(8,128)} %multiply_add_fusion.1), channel_id=1, source_target_pairs={{8,16},{24,32},{40,48},{56,64},{72,80},{88,96},{104,112},{120,128}... | collective-permute-start | bytes 1572872 | tf_op jit(solution)/shard_map/ppermute | solution.py:17
  51.1 48.0 %copy-start.1 = (f32[1024,128]{1,0:T(8,128)S(1)}, f32[1024,128]{1,0:T(8,128)}, u32[]{:S(2)}) copy-start(f32[1024,128]{1,0:T(8,128)} %copy-done) | copy-start | bytes 1572868
  51.1 48.0 %copy-start.12 = (f32[16]{0:T(128)S(1)}, f32[16]{0:T(128)}, u32[]{:S(2)}) copy-start(f32[16]{0:T(128)} %get-tuple-element.91) | copy-start | bytes 196
  51.1 48.0 %copy-start.13 = (f32[16]{0:T(128)S(1)}, f32[16]{0:T(128)}, u32[]{:S(2)}) copy-start(f32[16]{0:T(128)} %get-tuple-element.69) | copy-start | bytes 196
  105.9 28.0 %copy-start.10 = (f32[1024]{0:T(1024)S(1)}, f32[1024]{0:T(1024)}, u32[]{:S(2)}) copy-start(f32[1024]{0:T(1024)} %param.32) | copy-start | bytes 12292
  109.6 5.8 %collective-permute-start.7 = (f32[512]{0:T(512)S(1)}, f32[512]{0:T(512)S(1)}, u32[]{:S(2)}, u32[]{:S(2)}) collective-permute-start(f32[512]{0:T(512)S(1)} %get-tuple-element.61), channel_id=1, source_target_pairs={{0,1},{1,0},{2,3},{3,2},{4,5},{5,4},{6,7},{7,6},{8,9},{9,8},{10,11... | collective-permute-start | bytes 6152 | tf_op jit(solution)/shard_map/ppermute | solution.py:67
  115.4 7.6 %collective-permute-start.8 = (f32[512]{0:T(512)S(1)}, f32[512]{0:T(512)S(1)}, u32[]{:S(2)}, u32[]{:S(2)}) collective-permute-start(f32[512]{0:T(512)S(1)} %add.137), channel_id=1, source_target_pairs={{0,2},{1,3},{2,0},{3,1},{4,6},{5,7},{6,4},{7,5},{8,10},{9,11},{10,... | collective-permute-start | bytes 6152 | tf_op jit(solution)/shard_map/ppermute | solution.py:67
  123.1 10.8 %collective-permute-start.9 = (f32[512]{0:T(512)S(1)}, f32[512]{0:T(512)S(1)}, u32[]{:S(2)}, u32[]{:S(2)}) collective-permute-start(f32[512]{0:T(512)S(1)} %add.138), channel_id=1, source_target_pairs={{0,4},{1,5},{2,6},{3,7},{4,0},{5,1},{6,2},{7,3},{8,12},{9,13},{10,... | collective-permute-start | bytes 6152 | tf_op jit(solution)/shard_map/ppermute | solution.py:67

commit v4 on v2

--- a/solution.py
+++ b/solution.py
@@ -49,22 +49,28 @@
         route = [(2 * c + 1, 2 * (c + reach) + 1) for c in range(chips - reach)]
         got = unpack(shifted(pack(*chip_total), axis, route), *shapes)
         chip_total = fold(got, chip_total)
-    to_even = shifted(chip_total[1], axis, [(2 * c - 1, 2 * c) for c in range(1, chips)])
-    to_odd = shifted(chip_total[1], axis, [(2 * c - 1, 2 * c + 1) for c in range(1, chips)])
-    odd_entering = pair[0][..., None, None] * to_odd + pair[1]
     mine = lax.axis_index(axis)
-    return jnp.where(mine % 2 == 0, to_even, odd_entering)
+    even = mine % 2 == 0
+    split = state.shape[1] // 2
+    prefix = chip_total[1]
+    to_even = shifted(prefix[:, :split], axis, [(2 * c - 1, 2 * c) for c in range(1, chips)])
+    to_odd = shifted(prefix[:, split:], axis, [(2 * c - 1, 2 * c + 1) for c in range(1, chips)])
+    held = jnp.where(even, to_even, to_odd)
+    swap = [(2 * c, 2 * c + 1) for c in range(chips)] + [(2 * c + 1, 2 * c) for c in range(chips)]
+    other = shifted(held, axis, swap)
+    behind = jnp.where(
+        even,
+        jnp.concatenate([held, other], axis=1),
+        jnp.concatenate([other, held], axis=1),
+    )
+    odd_entering = pair[0][..., None, None] * behind + pair[1]
+    return jnp.where(even, behind, odd_entering)
 
 
 def summed_over(value, axis):
     count = lax.axis_size(axis)
-    if count & (count - 1):
-        return lax.psum(value, axis)
-    reach = 1
-    while reach < count:
-        value = value + lax.ppermute(value, axis, [(i, i ^ reach) for i in range(count)])
-        reach *= 2
-    return value
+    spread = jnp.broadcast_to(value[None], (count,) + value.shape)
+    return lax.all_to_all(spread, axis, 0, 0, tiled=False).sum(0)
 
 
 def causal_conv(window, window_ids, weight, bias, rows):
@@ -103,12 +109,19 @@
     block = STRETCH
     blocks = tok_rows // block
     margin = conv_x.shape[0] - 1
-    tails = (
-        x_proj[tok_rows - margin :],
-        bc_proj[tok_rows - margin :],
-        seg_ids[tok_rows - margin :].astype(jnp.bfloat16),
-    )
-    rim_x, rim_bc, rim_ids = from_behind((tails[0], tails[1], tails[2]), "seq", 1)
+    bc_width = bc_proj.shape[1] * bc_proj.shape[2]
+    rim = jnp.concatenate(
+        [
+            x_proj[tok_rows - margin :],
+            bc_proj[tok_rows - margin :].reshape(margin, bc_width),
+            jnp.broadcast_to(seg_ids[tok_rows - margin :, None].astype(jnp.bfloat16), (margin, 128)),
+        ],
+        axis=1,
+    )
+    rim = from_behind(rim, "seq", 1)
+    rim_x = rim[:, :inner_local]
+    rim_bc = rim[:, inner_local : inner_local + bc_width].reshape(margin, *bc_proj.shape[1:])
+    rim_ids = rim[:, inner_local + bc_width]
     own_ids = seg_ids.astype(jnp.float32)
     window_ids = jnp.concatenate([rim_ids.astype(jnp.float32), own_ids])
     x_conv = causal_conv(jnp.concatenate([rim_x, x_proj]), window_ids, conv_x, bias_x, tok_rows)

time: 128 us -> 123 us (0.961)
  the two profiles are of different devices: /device:TPU:5 before, /device:TPU:6 now
where the time goes in v4:
time: 123 us; the launch traced here: 122 us
  waiting for transfers between devices  49.8 us (40%)
  blocking collectives  17.9 us (15%)
  starting transfers between devices  17.8 us (14%)
  other arithmetic  15.4 us (13%)
  local copies, waits for them, and re-layouts  14.9 us (12%)
  matrix products  5.8 us (5%)
    ppermute x7, waiting for transfers between devices, shifted(): return lax.ppermute(block, axis, pairs)  47.4 us
    all_to_all x1, blocking collectives, summed_over(): return lax.all_to_all(spread, axis, 0, 0, tiled=False).sum(0)  17.9 us
    ppermute x7, starting transfers between devices, shifted(): return lax.ppermute(block, axis, pairs)  15.9 us
    unnamed x32, local copies, waits for them, and re-layouts  5.58 us
    convert_element_type x2, other arithmetic, causal_conv(): return jax.nn.silu(result).astype(jnp.bfloat16)  3.67 us
    dot_general x1, matrix products, on_device(): jnp.einsum('cghqs,csghp->cqghp', mixing, x_heads, preferred_element_type=...  2.94 us
  transfers between devices with their start and end apart: 8, of which 3 were waited for; matrix products, arithmetic and copies ran while one was open for 9% of the time, Pallas kernels for 0%

profile of v4, /device:TPU:6, one launch (start us, length us, event | category | flops | bytes accessed | tf_op | source)
XLA Modules:
  0.0 122.3 jit_solution(9601175073768688042)
XLA Ops:
  0.0 0.8 fusion.35
  1.6 0.7 slice.205
  2.7 1.9 %collective-permute-start = (bf16[3,1408]{0,1:T(8,128)(2,1)S(1)}, bf16[3,1408]{0,1:T(8,128)(2,1)S(1)}, u32[]{:S(2)}, u32[]{:S(2)}) collective-permute-start(bf16[3,1408]{0,1:T(8,128)(2,1)S(1)} %copy.91), channel_id=1, source_target_pairs={{0,8},{8,16},{16,24},{24,32},{32,40},{40,48},{48,56},{56,64},{64,7... | collective-permute-start | bytes 25352 | tf_op jit(solution)/shard_map/ppermute | solution.py:13
  4.6 0.7 bitcast_convert_fusion.3
  6.0 0.9 broadcast_multiply_fusion
  6.9 1.2 reduce-window.6
  8.5 0.9 slice_convert_fusion.3
  9.6 1.0 copy.96
  11.1 2.4 %collective-permute-done = bf16[3,1408]{0,1:T(8,128)(2,1)S(1)} collective-permute-done((bf16[3,1408]{0,1:T(8,128)(2,1)S(1)}, bf16[3,1408]{0,1:T(8,128)(2,1)S(1)}, u32[]{:S(2)}, u32[]{:S(2)}) %collective-permute-start) | collective-permute-done | bytes 8480 | tf_op jit(solution)/shard_map/ppermute | solution.py:13
  14.6 0.8 multiply_convert_fusion.8
  15.6 2.8 %multiply_convert_fusion.5 = bf16[512,1024]{0,1:T(8,128)(2,1)S(1)} fusion(bf16[512,1024]{0,1:T(8,128)(2,1)S(1)} %copy.92, bf16[3,1024]{0,1:T(8,128)(2,1)S(1)} %slice.249, f32[1024]{0:T(1024)S(1)} %bitcast.163, f32[1024]{0:T(1024)S(1)} %bitcast.164, f32[1024]{0:T(1024)S(1)} %bitcast.162, f32[1024]{0:T(1024)S(1)} %bitcast.161, f32[1024]{0:T(1024)S(1)} %copy-done.8, ...), kind=kLoop, calls=%fused_computation.24 | loop fusion | flops 15728640 | bytes 2125824 | tf_op jit(solution)/shard_map/convert_element_type | solution.py:85
  18.8 1.7 %fusion.11 = f32[2,16,64,128]{3,2,1,0:T(8,128)S(1)} fusion(f32[2,16,256]{2,1,0:T(8,128)S(1)} %fusion.27, f32[2,256,128]{2,1,0:T(8,128)S(1)} %convert_element_type.130, bf16[2,256,16,64]{1,0,3,2:T(2,128)(2,1)S(1)} %reshape.651), kind=kOutput, calls=%fused_computation.15 | convolution fusion | flops 136314880 | bytes 2392064 | tf_op jit(solution)/shard_map/cghsn,csghp->cghpn/dot_general | solution.py:154
  20.7 1.3 %collective-permute-start.1 = (f32[1032,128]{1,0:T(8,128)S(1)}, f32[1032,128]{1,0:T(8,128)S(1)}, u32[]{:S(2)}, u32[]{:S(2)}) collective-permute-start(f32[1032,128]{1,0:T(8,128)S(1)} %select_maximum_fusion.3), channel_id=1, source_target_pairs={{0,8},{16,24},{32,40},{48,56},{64,72},{80,88},{96,104},{112,120},{... | collective-permute-start | bytes 1585160 | tf_op jit(solution)/shard_map/ppermute | solution.py:17
  22.0 1.5 %collective-permute-done.1 = f32[1032,128]{1,0:T(8,128)S(1)} collective-permute-done((f32[1032,128]{1,0:T(8,128)S(1)}, f32[1032,128]{1,0:T(8,128)S(1)}, u32[]{:S(2)}, u32[]{:S(2)}) %collective-permute-start.1) | collective-permute-done | bytes 528416 | tf_op jit(solution)/shard_map/ppermute | solution.py:17
  24.7 0.7 collective-permute-start.3
  25.7 0.7 collective-permute-start.4
  26.6 0.8 fusion.33
  27.3 1.3 %collective-permute-start.5 = (f32[1,8,64,128]{3,2,1,0:T(8,128)}, f32[1,8,64,128]{3,2,1,0:T(8,128)}, u32[]{:S(2)}, u32[]{:S(2)}) collective-permute-start(f32[1,8,64,128]{3,2,1,0:T(8,128)} %get-tuple-element.60), channel_id=1, source_target_pairs={{8,16},{24,32},{40,48},{56,64},{72,80},{88,96},{104,112},{120,128}... | collective-permute-start | bytes 786440 | tf_op jit(solution)/shard_map/ppermute | solution.py:17
  28.6 1.4 %collective-permute-start.6 = (f32[1,8,64,128]{3,2,1,0:T(8,128)S(1)}, f32[1,8,64,128]{3,2,1,0:T(8,128)}, u32[]{:S(2)}, u32[]{:S(2)}) collective-permute-start(f32[1,8,64,128]{3,2,1,0:T(8,128)S(1)} %get-tuple-element.59), channel_id=1, source_target_pairs={{8,24},{24,40},{40,56},{56,72},{72,88},{88,104},{104,120},{120,136... | collective-permute-start | bytes 786440 | tf_op jit(solution)/shard_map/ppermute | solution.py:17
  30.0 1.5 %copy.106 = bf16[512,1024]{0,1:T(8,128)(2,1)S(1)} copy(bf16[512,1024]{1,0:T(8,128)(2,1)} %param.23) | data formatting | bytes 2097152 | tf_op args[2]
  31.5 0.8 compare_and_fusion
  32.4 45.9 %collective-permute-done.5 = f32[1,8,64,128]{3,2,1,0:T(8,128)} collective-permute-done((f32[1,8,64,128]{3,2,1,0:T(8,128)}, f32[1,8,64,128]{3,2,1,0:T(8,128)}, u32[]{:S(2)}, u32[]{:S(2)}) %collective-permute-start.5) | collective-permute-done | bytes 262176 | tf_op jit(solution)/shard_map/ppermute | solution.py:17
  78.3 1.0 broadcast_select_fusion
  79.3 9.9 %collective-permute-start.7 = (f32[1,8,64,128]{3,2,1,0:T(8,128)S(1)}, f32[1,8,64,128]{3,2,1,0:T(8,128)S(1)}, u32[]{:S(2)}, u32[]{:S(2)}) collective-permute-start(f32[1,8,64,128]{3,2,1,0:T(8,128)S(1)} %broadcast_select_fusion), channel_id=1, source_target_pairs={{0,8},{16,24},{32,40},{48,56},{64,72},{80,88},{96,104},{112,120},{... | collective-permute-start | bytes 786440 | tf_op jit(solution)/shard_map/ppermute | solution.py:17
  89.3 2.3 %reshape.680 = f32[2,256,1,16,64]{1,0,4,3,2:T(2,128)} reshape(bf16[512,1024]{0,1:T(8,128)(2,1)S(1)} %multiply_convert_fusion.5) | data formatting | bytes 3145728 | tf_op jit(solution)/shard_map/convert_element_type | solution.py:183
  92.0 0.8 copy-done.1
  93.1 1.0 fusion.18
  94.9 2.9 %fusion.13 = f32[2,256,1,16,64]{1,4,3,0,2:T(8,128)S(1)} fusion(f32[2,16,64,256]{3,2,1,0:T(8,128)S(1)} %fusion.18, f32[2,256,1,16,64]{1,0,4,3,2:T(2,128)S(1)} %copy-done.2, f32[2,16,256]{2,1,0:T(8,128)S(1)} %bitcast.160, f32[2,16,256]{2,1,0:T(8,128)S(1)} %get-tuple-element.63, f32[2,256,256]{2,1,0:T(8,128)S(1)} %fusion.36, ...), kind=kOutput, calls=%fused_computation.18 | convolution fusion | flops 283115520 | bytes 8093760 | tf_op jit(solution)/shard_map/cghqs,csghp->cqghp/dot_general | solution.py:148
  97.8 1.6 %copy.105 = f32[2,256,1,16,64]{1,0,4,3,2:T(2,128)S(1)} copy(f32[2,256,1,16,64]{1,4,3,0,2:T(8,128)S(1)} %fusion.13) | data formatting | bytes 4194304 | tf_op jit(solution)/shard_map/add | solution.py:183
  100.4 17.9 %all_to_all.6 = f32[8,1,512]{2,1,0:T(1,128)S(1)} all-to-all(f32[8,1,512]{2,1,0:T(1,128)S(1)} %broadcast_in_dim.144), channel_id=1, replica_groups=mesh['seq'=64,'tp'=8] {'tp'}, dimensions={0} | all-to-all | bytes 32768 | tf_op jit(solution)/shard_map/all_to_all | solution.py:73
  118.3 1.7 %multiply_convert_fusion.4 = bf16[512,1024]{0,1:T(8,128)(2,1)} fusion(f32[1024]{0:T(1024)S(1)} %copy-done.9, f32[512]{0:T(512)S(1)} %add_rsqrt_fusion, f32[512,1024]{0,1:T(8,128)S(1)} %bitcast.140, bf16[512,1024]{0,1:T(8,128)(2,1)S(1)} %copy.106), kind=kLoop, calls=%fused_computation.20 | loop fusion | flops 4718592 | bytes 4200448 | tf_op jit(solution)/shard_map/convert_element_type | solution.py:187
  120.0 2.3 %copy.108 = bf16[512,1024]{1,0:T(8,128)(2,1)} copy(bf16[512,1024]{0,1:T(8,128)(2,1)} %multiply_convert_fusion.4) | data formatting | bytes 2097152 | tf_op jit(solution)/shard_map/convert_element_type | solution.py:187
  (91 shorter events, 8.7 us)
Async XLA Ops:
  0.0 13.6 %copy-start.7 = (s32[512]{0:T(512)S(1)}, s32[512]{0:T(512)}, u32[]{:S(2)}) copy-start(s32[512]{0:T(512)} %param.33) | copy-start | bytes 6148
  0.0 10.5 %copy-start.3 = (bf16[512,1024]{1,0:T(8,128)(2,1)S(1)}, bf16[512,1024]{1,0:T(8,128)(2,1)}, u32[]{:S(2)}) copy-start(bf16[512,1024]{1,0:T(8,128)(2,1)} %param.21) | copy-start | bytes 3145732
  0.0 14.6 %copy-start.11 = (f32[2,128]{1,0:T(2,128)S(1)}, f32[2,128]{1,0:T(2,128)}, u32[]{:S(2)}) copy-start(f32[2,128]{1,0:T(2,128)} %param.28) | copy-start | bytes 3076
  2.7 10.9 %collective-permute-start = (bf16[3,1408]{0,1:T(8,128)(2,1)S(1)}, bf16[3,1408]{0,1:T(8,128)(2,1)S(1)}, u32[]{:S(2)}, u32[]{:S(2)}) collective-permute-start(bf16[3,1408]{0,1:T(8,128)(2,1)S(1)} %copy.91), channel_id=1, source_target_pairs={{0,8},{8,16},{16,24},{24,32},{32,40},{40,48},{48,56},{56,64},{64,7... | collective-permute-start | bytes 25352 | tf_op jit(solution)/shard_map/ppermute | solution.py:13
  10.6 5.0 %copy-start.8 = (f32[1024]{0:T(1024)S(1)}, f32[1024]{0:T(1024)}, u32[]{:S(2)}) copy-start(f32[1024]{0:T(1024)} %param.27) | copy-start | bytes 12292
  18.7 1.9 %copy-start.4 = (bf16[2,256,16,64]{1,0,3,2:T(2,128)(2,1)}, bf16[2,256,16,64]{1,0,3,2:T(2,128)(2,1)S(1)}, u32[]{:S(2)}) copy-start(bf16[2,256,16,64]{1,0,3,2:T(2,128)(2,1)S(1)} %reshape.651) | copy-start | bytes 3145732
  20.5 3.3 %copy-start = (f32[2,16,64,128]{3,2,1,0:T(8,128)}, f32[2,16,64,128]{3,2,1,0:T(8,128)S(1)}, u32[]{:S(2)}) copy-start(f32[2,16,64,128]{3,2,1,0:T(8,128)S(1)} %fusion.11) | copy-start | bytes 3145732
  20.7 2.8 %collective-permute-start.1 = (f32[1032,128]{1,0:T(8,128)S(1)}, f32[1032,128]{1,0:T(8,128)S(1)}, u32[]{:S(2)}, u32[]{:S(2)}) collective-permute-start(f32[1032,128]{1,0:T(8,128)S(1)} %select_maximum_fusion.3), channel_id=1, source_target_pairs={{0,8},{16,24},{32,40},{48,56},{64,72},{80,88},{96,104},{112,120},{... | collective-permute-start | bytes 1585160 | tf_op jit(solution)/shard_map/ppermute | solution.py:17
  23.8 0.7 collective-permute-start.2
  24.7 0.7 collective-permute-start.3
  25.7 0.7 collective-permute-start.4
  27.3 51.0 %collective-permute-start.5 = (f32[1,8,64,128]{3,2,1,0:T(8,128)}, f32[1,8,64,128]{3,2,1,0:T(8,128)}, u32[]{:S(2)}, u32[]{:S(2)}) collective-permute-start(f32[1,8,64,128]{3,2,1,0:T(8,128)} %get-tuple-element.60), channel_id=1, source_target_pairs={{8,16},{24,32},{40,48},{56,64},{72,80},{88,96},{104,112},{120,128}... | collective-permute-start | bytes 786440 | tf_op jit(solution)/shard_map/ppermute | solution.py:17
  28.6 49.7 %collective-permute-start.6 = (f32[1,8,64,128]{3,2,1,0:T(8,128)S(1)}, f32[1,8,64,128]{3,2,1,0:T(8,128)}, u32[]{:S(2)}, u32[]{:S(2)}) collective-permute-start(f32[1,8,64,128]{3,2,1,0:T(8,128)S(1)} %get-tuple-element.59), channel_id=1, source_target_pairs={{8,24},{24,40},{40,56},{56,72},{72,88},{88,104},{104,120},{120,136... | collective-permute-start | bytes 786440 | tf_op jit(solution)/shard_map/ppermute | solution.py:17
  79.3 12.5 %collective-permute-start.7 = (f32[1,8,64,128]{3,2,1,0:T(8,128)S(1)}, f32[1,8,64,128]{3,2,1,0:T(8,128)S(1)}, u32[]{:S(2)}, u32[]{:S(2)}) collective-permute-start(f32[1,8,64,128]{3,2,1,0:T(8,128)S(1)} %broadcast_select_fusion), channel_id=1, source_target_pairs={{0,8},{16,24},{32,40},{48,56},{64,72},{80,88},{96,104},{112,120},{... | collective-permute-start | bytes 786440 | tf_op jit(solution)/shard_map/ppermute | solution.py:17
  89.3 2.7 %copy-start.10 = (f32[16]{0:T(128)S(1)}, f32[16]{0:T(128)}, u32[]{:S(2)}) copy-start(f32[16]{0:T(128)} %get-tuple-element.81) | copy-start | bytes 196
  91.6 1.2 %copy-start.1 = (f32[2,16,64,128]{3,2,1,0:T(8,128)S(1)}, f32[2,16,64,128]{3,2,1,0:T(8,128)}, u32[]{:S(2)}) copy-start(f32[2,16,64,128]{3,2,1,0:T(8,128)} %copy-done) | copy-start | bytes 3145732
  93.0 1.6 %copy-start.2 = (f32[2,256,1,16,64]{1,0,4,3,2:T(2,128)S(1)}, f32[2,256,1,16,64]{1,0,4,3,2:T(2,128)}, u32[]{:S(2)}) copy-start(f32[2,256,1,16,64]{1,0,4,3,2:T(2,128)} %reshape.680) | copy-start | bytes 6291460
  93.0 1.8 %copy-start.5 = (bf16[2,256,16,64]{1,0,3,2:T(2,128)(2,1)S(1)}, bf16[2,256,16,64]{1,0,3,2:T(2,128)(2,1)}, u32[]{:S(2)}) copy-start(bf16[2,256,16,64]{1,0,3,2:T(2,128)(2,1)} %copy-done.4) | copy-start | bytes 3145732
  93.1 1.8 %copy-start.6 = (pred[2,256,256]{2,1,0:T(8,128)(4,1)S(1)}, pred[2,256,256]{2,1,0:T(8,128)(4,1)}, u32[]{:S(2)}) copy-start(pred[2,256,256]{2,1,0:T(8,128)(4,1)} %compare_and_fusion) | copy-start | bytes 393220
  93.1 1.8 %copy-start.12 = (f32[16]{0:T(128)S(1)}, f32[16]{0:T(128)}, u32[]{:S(2)}) copy-start(f32[16]{0:T(128)} %param.31) | copy-start | bytes 196
  99.7 18.6 %copy-start.9 = (f32[1024]{0:T(1024)S(1)}, f32[1024]{0:T(1024)}, u32[]{:S(2)}) copy-start(f32[1024]{0:T(1024)} %param.32) | copy-start | bytes 12292

commit v5 on v4

--- a/solution.py
+++ b/solution.py
@@ -2,6 +2,7 @@
 import jax.numpy as jnp
 from jax import lax
 from jax.sharding import PartitionSpec as P
+from jax.experimental import pallas as pl
 
 STATE = 128
 STRETCH = 256
@@ -71,6 +72,61 @@
     count = lax.axis_size(axis)
     spread = jnp.broadcast_to(value[None], (count,) + value.shape)
     return lax.all_to_all(spread, axis, 0, 0, tiled=False).sum(0)
+
+
+def tail_kernel(base_ref, z_ref, c_ref, s_ref, link_ref, expand_ref, gated_ref, ss_ref):
+    state = s_ref[0]
+    s_hi = state.astype(jnp.bfloat16)
+    s_lo = (state - s_hi.astype(jnp.float32)).astype(jnp.bfloat16)
+    c_row = c_ref[...]
+    nt = (((1,), (1,)), ((), ()))
+    product = lax.dot_general(c_row, s_hi, nt, preferred_element_type=jnp.float32)
+    product = product + lax.dot_general(c_row, s_lo, nt, preferred_element_type=jnp.float32)
+    link = link_ref[...]
+    expand = expand_ref[...]
+    l_hi = link.astype(jnp.bfloat16)
+    rest = link - l_hi.astype(jnp.float32)
+    l_mid = rest.astype(jnp.bfloat16)
+    l_lo = (rest - l_mid.astype(jnp.float32)).astype(jnp.bfloat16)
+    spread = jnp.dot(l_hi, expand, preferred_element_type=jnp.float32)
+    spread = spread + jnp.dot(l_mid, expand, preferred_element_type=jnp.float32)
+    spread = spread + jnp.dot(l_lo, expand, preferred_element_type=jnp.float32)
+    z = z_ref[...].astype(jnp.float32)
+    gate = z * (1.0 / (1.0 + jnp.exp(-z)))
+    gated = (base_ref[...] + product * spread) * gate
+    gated_ref[...] = gated
+    ss_ref[...] = jnp.sum(gated * gated, axis=1, keepdims=True)
+
+
+def gated_tail(base, z_proj, c_rows, states, link_rows, block):
+    rows, width = base.shape
+    heads = link_rows.shape[1]
+    state_size = c_rows.shape[1]
+    expand = jnp.repeat(jnp.eye(heads, dtype=jnp.bfloat16), width // heads, axis=1)
+    flops = 2 * rows * width * (2 * state_size + 3 * heads)
+    return pl.pallas_call(
+        tail_kernel,
+        grid=(rows // block,),
+        in_specs=[
+            pl.BlockSpec((block, width), lambda i: (i, 0)),
+            pl.BlockSpec((block, width), lambda i: (i, 0)),
+            pl.BlockSpec((block, state_size), lambda i: (i, 0)),
+            pl.BlockSpec((1, width, state_size), lambda i: (i, 0, 0)),
+            pl.BlockSpec((block, heads), lambda i: (i, 0)),
+            pl.BlockSpec((heads, width), lambda i: (0, 0)),
+        ],
+        out_specs=[
+            pl.BlockSpec((block, width), lambda i: (i, 0)),
+            pl.BlockSpec((block, 1), lambda i: (i, 0)),
+        ],
+        out_shape=[
+            jax.ShapeDtypeStruct((rows, width), jnp.float32),
+            jax.ShapeDtypeStruct((rows, 1), jnp.float32),
+        ],
+        cost_estimate=pl.CostEstimate(
+            flops=flops, transcendentals=rows * width, bytes_accessed=rows * width * 10
+        ),
+    )(base, z_proj, c_rows, states, link_rows, expand)
 
 
 def causal_conv(window, window_ids, weight, bias, rows):
@@ -162,7 +218,6 @@
         jnp.exp(cum_heads)
         * (block_ids == before_ids[:, None]).astype(jnp.float32)[:, None, None, :]
     )
-    c_float = c_out.astype(jnp.float32)
 
     def recur(start_state):
         stacked = []
@@ -177,12 +232,18 @@
     device_gain = carry_gain[0] * carry_gain[1]
     entering = entering_state(device_gain, summary, "seq")
     states, _ = recur(entering)
-    product = jnp.einsum("cqgn,cghpn->cqghp", c_float, states, precision=lax.Precision.HIGHEST)
-    y_inter = product * link.transpose(0, 3, 1, 2)[..., None]
     skip = d_skip.reshape(groups_local, heads_group)[..., None]
-    mixed = y_intra + y_inter + skip * x_heads.astype(jnp.float32)
-    gated = mixed.reshape(tok_rows, inner_local) * jax.nn.silu(z_proj.astype(jnp.float32))
-    squares = summed_over(jnp.sum(gated * gated, axis=-1), "tp")
+    base = (y_intra + skip * x_heads.astype(jnp.float32)).reshape(tok_rows, inner_local)
+    link_rows = link.transpose(0, 3, 1, 2).reshape(tok_rows, heads_local)
+    gated, sums = gated_tail(
+        base,
+        z_proj,
+        c_out.reshape(tok_rows, state_size),
+        states.reshape(blocks, heads_local * head_size, state_size),
+        link_rows,
+        block,
+    )
+    squares = summed_over(sums[:, 0], "tp")
     scale = lax.rsqrt(squares / (inner_local * lax.axis_size("tp")) + 1e-05)
     return (gated * scale[:, None] * norm_gain).astype(jnp.bfloat16)
 

time: 123 us -> 147 us (1.20)
  local copies, waits for them, and re-layouts: 14.9 us -> 27.9 us
  waiting for transfers between devices: 49.8 us -> 40.9 us
  other arithmetic: 15.4 us -> 23.9 us
  Pallas kernels: 0 us -> 5.09 us
  starting transfers between devices: 17.8 us -> 21 us
  matrix products: 5.8 us -> 8.23 us
    reshape x0 -> x3, local copies, waits for them, and re-layouts: none -> 10.4 us  [the longest x2 9.69 us: on_device(): (y_intra + skip * x_heads.astype(jnp.float32)).reshape(tok_rows, inner_lo...]
    ppermute x7, waiting for transfers between devices: 47.4 us -> 40.9 us  [shifted(): return lax.ppermute(block, axis, pairs)]
    pallas_call x0 -> x1, Pallas kernels: none -> 5.09 us  [gated_tail(): pl.pallas_call(tail_kernel, grid=(rows // block,), in_specs=[pl.BlockSpec...]
    another operation x4 -> x6, local copies, waits for them, and re-layouts: 0.45 us -> 4.75 us
    unnamed x32 -> x17, local copies, waits for them, and re-layouts: 5.58 us -> 1.7 us
    convert_element_type x2, other arithmetic: 3.67 us -> 7.05 us  [causal_conv(): return jax.nn.silu(result).astype(jnp.bfloat16)]
    ppermute x7, starting transfers between devices: 15.9 us -> 19.1 us  [shifted(): return lax.ppermute(block, axis, pairs)]
    convert_element_type x2, local copies, waits for them, and re-layouts: 4.6 us -> 7.09 us  [on_device(): x_heads.astype(jnp.float32)]
  transfers between devices with their start and end apart: 8 -> 8, of which waited for: 3 -> 2; matrix products, arithmetic and copies ran while one was open for 9% -> 22% of each run, Pallas kernels for 0% -> 0%
where the time goes in v5:
time: 147 us; the launch traced here: 145 us
  waiting for transfers between devices  40.9 us (28%)
  local copies, waits for them, and re-layouts  27.9 us (19%)
  other arithmetic  23.9 us (16%)
  starting transfers between devices  21 us (14%)
  blocking collectives  17.9 us (12%)
  matrix products  8.23 us (6%)
  Pallas kernels  5.09 us (3%)
    ppermute x7, waiting for transfers between devices, shifted(): return lax.ppermute(block, axis, pairs)  40.9 us
    ppermute x7, starting transfers between devices, shifted(): return lax.ppermute(block, axis, pairs)  19.1 us
    all_to_all x1, blocking collectives, summed_over(): return lax.all_to_all(spread, axis, 0, 0, tiled=False).sum(0)  17.9 us
    reshape x2, local copies, waits for them, and re-layouts, on_device(): (y_intra + skip * x_heads.astype(jnp.float32)).reshape(tok_rows, inner_lo...  9.69 us
    convert_element_type x2, local copies, waits for them, and re-layouts, on_device(): x_heads.astype(jnp.float32)  7.09 us
    convert_element_type x2, other arithmetic, causal_conv(): return jax.nn.silu(result).astype(jnp.bfloat16)  7.05 us
    dot_general x1, matrix products, on_device(): jnp.einsum('cghqs,csghp->cqghp', mixing, x_heads, preferred_element_type=...  5.32 us
    pallas_call x1, Pallas kernels, gated_tail(): pl.pallas_call(tail_kernel, grid=(rows // block,), in_specs=[pl.BlockSpec...  5.09 us
  transfers between devices with their start and end apart: 8, of which 2 were waited for; matrix products, arithmetic and copies ran while one was open for 22% of the time, Pallas kernels for 0%

profile of v5, /device:TPU:6, one launch (start us, length us, event | category | flops | bytes accessed | tf_op | source)
XLA Modules:
  0.0 145.4 jit_solution(18355633687083503047)
XLA Ops:
  2.3 1.9 %collective-permute-start = (bf16[3,1408]{1,0:T(4,128)(2,1)S(1)}, bf16[3,1408]{1,0:T(4,128)(2,1)S(1)}, u32[]{:S(2)}, u32[]{:S(2)}) collective-permute-start(bf16[3,1408]{1,0:T(4,128)(2,1)S(1)} %pad_maximum_fusion.3), channel_id=1, source_target_pairs={{0,8},{8,16},{16,24},{24,32},{32,40},{40,48},{48,56},{56,64},{64,7... | collective-permute-start | bytes 25352 | tf_op jit(solution)/shard_map/ppermute | solution.py:14
  4.3 0.9 slice_convert_fusion.3
  5.8 0.9 broadcast_multiply_fusion
  6.7 1.2 reduce-window.6
  8.1 1.3 bitcast_convert_fusion.3
  10.3 1.0 copy.69
  11.5 0.8 slice_compare_fusion.2
  13.7 5.4 %multiply_convert_fusion.5 = bf16[512,1024]{1,0:T(8,128)(2,1)S(1)} fusion(bf16[512,1024]{1,0:T(8,128)(2,1)} %param.21, bf16[3,1024]{1,0:T(4,128)(2,1)S(1)} %slice.249, f32[1024]{0:T(1024)S(1)} %bitcast.146, f32[1024]{0:T(1024)S(1)} %bitcast.147, f32[1024]{0:T(1024)S(1)} %bitcast.145, f32[1024]{0:T(1024)S(1)} %bitcast.144, f32[1024]{0:T(1024)} %param.27, ...), kind=kLoop, calls=%fused_computation.14 | loop fusion | flops 15728640 | bytes 2125824 | tf_op jit(solution)/shard_map/convert_element_type | solution.py:141
  19.1 1.3 reshape.630
  20.4 2.5 %copy.75 = bf16[2,256,16,64]{1,3,2,0:T(8,128)(2,1)} copy(bf16[2,256,16,64]{3,2,1,0:T(8,128)(2,1)S(1)} %reshape.630) | data formatting | bytes 2097152 | tf_op jit(solution)/shard_map/reshape.124
  22.9 1.6 %multiply_convert_fusion.8 = bf16[512,2,128]{2,0,1:T(8,128)(2,1)S(1)} fusion(bf16[512,2,128]{2,0,1:T(8,128)(2,1)S(1)} %copy.69, bf16[3,2,128]{2,0,1:T(4,128)(2,1)S(1)} %slice_bitcast_fusion, f32[2,128]{1,0:T(2,128)} %get-tuple-element.81, f32[2,128]{1,0:T(2,128)} %get-tuple-element.82, f32[2,128]{1,0:T(2,128)} %get-tuple-element.80, ...), kind=kLoop, calls=%fused_computation.37 | loop fusion | flops 3932160 | bytes 532992 | tf_op jit(solution)/shard_map/convert_element_type | solution.py:141
  26.1 2.7 %fusion.7 = f32[2,16,64,128]{3,2,1,0:T(8,128)S(1)} fusion(bf16[2,256,16,64]{1,3,2,0:T(8,128)(2,1)} %copy.75, f32[2,16,256]{2,1,0:T(8,128)S(1)} %fusion.17, f32[2,256,128]{2,1,0:T(8,128)S(1)} %convert_element_type.131), kind=kOutput, calls=%fused_computation.9 | convolution fusion | flops 136314880 | bytes 2392064 | tf_op jit(solution)/shard_map/cghsn,csghp->cghpn/dot_general | solution.py:210
  29.0 3.6 %collective-permute-start.1 = (f32[1032,128]{1,0:T(8,128)S(1)}, f32[1032,128]{1,0:T(8,128)S(1)}, u32[]{:S(2)}, u32[]{:S(2)}) collective-permute-start(f32[1032,128]{1,0:T(8,128)S(1)} %select_maximum_fusion.3), channel_id=1, source_target_pairs={{0,8},{16,24},{32,40},{48,56},{64,72},{80,88},{96,104},{112,120},{... | collective-permute-start | bytes 1585160 | tf_op jit(solution)/shard_map/ppermute | solution.py:18
  32.6 1.5 %collective-permute-done.1 = f32[1032,128]{1,0:T(8,128)S(1)} collective-permute-done((f32[1032,128]{1,0:T(8,128)S(1)}, f32[1032,128]{1,0:T(8,128)S(1)}, u32[]{:S(2)}, u32[]{:S(2)}) %collective-permute-start.1) | collective-permute-done | bytes 528416 | tf_op jit(solution)/shard_map/ppermute | solution.py:18
  37.0 0.8 compare_and_fusion
  38.0 0.9 fusion.22
  38.8 1.3 collective-permute-start.5
  40.1 1.4 collective-permute-start.6
  42.4 2.5 %reshape.628 = f32[2,256,1,16,64]{4,3,1,0,2:T(8,128)} reshape(bf16[512,1024]{1,0:T(8,128)(2,1)S(1)} %multiply_convert_fusion.5) | data formatting | bytes 3145728 | tf_op jit(solution)/shard_map/convert_element_type | solution.py:236
  44.9 4.6 %copy.77 = f32[2,256,1,16,64]{1,4,3,0,2:T(8,128)} copy(f32[2,256,1,16,64]{4,3,1,0,2:T(8,128)} %reshape.628) | data formatting | bytes 4194304 | tf_op jit(solution)/shard_map/convert_element_type | solution.py:236
  49.7 39.4 %collective-permute-done.5 = f32[1,8,64,128]{3,2,1,0:T(8,128)} collective-permute-done((f32[1,8,64,128]{3,2,1,0:T(8,128)}, f32[1,8,64,128]{3,2,1,0:T(8,128)}, u32[]{:S(2)}, u32[]{:S(2)}) %collective-permute-start.5) | collective-permute-done | bytes 262176 | tf_op jit(solution)/shard_map/ppermute | solution.py:18
  89.1 1.0 broadcast_select_fusion
  90.1 10.7 %collective-permute-start.7 = (f32[1,8,64,128]{3,2,1,0:T(8,128)S(1)}, f32[1,8,64,128]{3,2,1,0:T(8,128)S(1)}, u32[]{:S(2)}, u32[]{:S(2)}) collective-permute-start(f32[1,8,64,128]{3,2,1,0:T(8,128)S(1)} %broadcast_select_fusion), channel_id=1, source_target_pairs={{0,8},{16,24},{32,40},{48,56},{64,72},{80,88},{96,104},{112,120},{... | collective-permute-start | bytes 786440 | tf_op jit(solution)/shard_map/ppermute | solution.py:18
  100.8 5.3 %bitcast_add_fusion = f32[2,256,1,16,64]{1,4,3,0,2:T(8,128)} fusion(f32[2,256,1,16,64]{1,4,3,0,2:T(8,128)} %copy.77, bf16[2,256,16,64]{1,3,2,0:T(8,128)(2,1)} %copy.75, f32[2,16,256]{2,1,0:T(8,128)S(1)} %bitcast.143, f32[2,16,256]{2,1,0:T(8,128)S(1)} %get-tuple-element.69, f32[2,256,256]{2,1,0:T(8,128)S(1)} %fusion.24, ...), kind=kOutput, calls=%fused_computation.10 | convolution fusion | flops 282066944 | bytes 5963840 | tf_op jit(solution)/shard_map/cghqs,csghp->cqghp/dot_general | solution.py:204
  106.1 4.8 %copy.85 = f32[2,256,1,16,64]{4,3,1,0,2:T(8,128)} copy(f32[2,256,1,16,64]{1,4,3,0,2:T(8,128)} %bitcast_add_fusion) | data formatting | bytes 4194304 | tf_op jit(solution)/shard_map/reshape | solution.py:236
  111.0 4.8 %reshape.629.base_ref = f32[512,1024]{1,0:T(8,128)} reshape(f32[2,256,1,16,64]{4,3,1,0,2:T(8,128)} %copy.85) | data formatting | bytes 4194304 | tf_op jit(solution)/shard_map/reshape | solution.py:236
  115.9 0.9 copy.80
  117.4 1.0 pad_maximum_fusion.1.s_ref
  118.4 5.1 %shard_map.127 = (f32[512,1024]{1,0:T(8,128)}, f32[512,1]{1,0:T(8,128)}) custom-call(f32[512,1024]{1,0:T(8,128)} %reshape.629.base_ref, bf16[512,1024]{1,0:T(8,128)(2,1)} %z_ref.1, bf16[512,128]{1,0:T(8,128)(2,1)} %get-tuple-element.65.c_ref, f32[2,1024,128]{2,1,0:T(8,128)} %pad_maximum_fusion.1.s_ref, f32[512,16]{1,0:T(8,128)} %bitcast.139, ...), custom_call_target="tpu_custom_call" | custom-call | flops 318767104 | bytes 5242880 | tf_op jit(solution)/shard_map/pallas_call | solution.py:107
  123.5 1.1 reduce.14
  124.6 17.9 %all_to_all.6 = f32[8,1,512]{2,1,0:T(1,128)S(1)} all-to-all(f32[8,1,512]{2,1,0:T(1,128)S(1)} %broadcast_in_dim.149), channel_id=1, replica_groups=mesh['seq'=64,'tp'=8] {'tp'}, dimensions={0} | all-to-all | bytes 32768 | tf_op jit(solution)/shard_map/all_to_all | solution.py:74
  142.6 2.8 %multiply_convert_fusion.4 = bf16[512,1024]{1,0:T(8,128)(2,1)} fusion(f32[512,1024]{1,0:T(8,128)} %get-tuple-element.55, f32[1024]{0:T(1024)S(1)} %copy-done.3, f32[512]{0:T(512)S(1)} %add_rsqrt_fusion), kind=kLoop, calls=%fused_computation.11 | loop fusion | flops 1572864 | bytes 3151872 | tf_op jit(solution)/shard_map/convert_element_type | solution.py:248
  (84 shorter events, 12.1 us)
Async XLA Ops:
  2.3 9.0 %collective-permute-start = (bf16[3,1408]{1,0:T(4,128)(2,1)S(1)}, bf16[3,1408]{1,0:T(4,128)(2,1)S(1)}, u32[]{:S(2)}, u32[]{:S(2)}) collective-permute-start(bf16[3,1408]{1,0:T(4,128)(2,1)S(1)} %pad_maximum_fusion.3), channel_id=1, source_target_pairs={{0,8},{8,16},{16,24},{24,32},{32,40},{40,48},{48,56},{56,64},{64,7... | collective-permute-start | bytes 25352 | tf_op jit(solution)/shard_map/ppermute | solution.py:14
  12.3 1.4 copy-start.1
  12.3 1.4 copy-start.2
  28.8 5.4 %copy-start.5 = (f32[16]{0:T(128)S(1)}, f32[16]{0:T(128)}, u32[]{:S(2)}) copy-start(f32[16]{0:T(128)} %get-tuple-element.89) | copy-start | bytes 196
  29.0 5.1 %collective-permute-start.1 = (f32[1032,128]{1,0:T(8,128)S(1)}, f32[1032,128]{1,0:T(8,128)S(1)}, u32[]{:S(2)}, u32[]{:S(2)}) collective-permute-start(f32[1032,128]{1,0:T(8,128)S(1)} %select_maximum_fusion.3), channel_id=1, source_target_pairs={{0,8},{16,24},{32,40},{48,56},{64,72},{80,88},{96,104},{112,120},{... | collective-permute-start | bytes 1585160 | tf_op jit(solution)/shard_map/ppermute | solution.py:18
  34.4 0.7 collective-permute-start.2
  35.3 0.7 collective-permute-start.3
  36.3 1.6 %collective-permute-start.4 = (f32[1032,128]{1,0:T(8,128)S(1)}, f32[1032,128]{1,0:T(8,128)S(1)}, u32[]{:S(2)}, u32[]{:S(2)}) collective-permute-start(f32[1032,128]{1,0:T(8,128)S(1)} %select_maximum_fusion), channel_id=1, source_target_pairs={{8,72},{24,88},{40,104},{56,120},{72,136},{88,152},{104,168},{120,... | collective-permute-start | bytes 1585160 | tf_op jit(solution)/shard_map/ppermute | solution.py:18
  38.8 50.2 %collective-permute-start.5 = (f32[1,8,64,128]{3,2,1,0:T(8,128)}, f32[1,8,64,128]{3,2,1,0:T(8,128)}, u32[]{:S(2)}, u32[]{:S(2)}) collective-permute-start(f32[1,8,64,128]{3,2,1,0:T(8,128)} %get-tuple-element.64), channel_id=1, source_target_pairs={{8,16},{24,32},{40,48},{56,64},{72,80},{88,96},{104,112},{120,128}... | collective-permute-start | bytes 786440 | tf_op jit(solution)/shard_map/ppermute | solution.py:18
  40.1 48.9 %collective-permute-start.6 = (f32[1,8,64,128]{3,2,1,0:T(8,128)}, f32[1,8,64,128]{3,2,1,0:T(8,128)}, u32[]{:S(2)}, u32[]{:S(2)}) collective-permute-start(f32[1,8,64,128]{3,2,1,0:T(8,128)} %get-tuple-element.63), channel_id=1, source_target_pairs={{8,24},{24,40},{40,56},{56,72},{72,88},{88,104},{104,120},{120,136... | collective-permute-start | bytes 786440 | tf_op jit(solution)/shard_map/ppermute | solution.py:18
  44.9 4.6 %copy-start = (bf16[512,1,128]{2,0,1:T(8,128)(2,1)S(1)}, bf16[512,1,128]{2,0,1:T(8,128)(2,1)}, u32[]{:S(2)}) copy-start(bf16[512,1,128]{2,0,1:T(8,128)(2,1)} %get-tuple-element.67) | copy-start | bytes 393220
  44.9 55.9 %copy-start.6 = (f32[16]{0:T(128)S(1)}, f32[16]{0:T(128)}, u32[]{:S(2)}) copy-start(f32[16]{0:T(128)} %param.31) | copy-start | bytes 196
  90.1 26.9 %collective-permute-start.7 = (f32[1,8,64,128]{3,2,1,0:T(8,128)S(1)}, f32[1,8,64,128]{3,2,1,0:T(8,128)S(1)}, u32[]{:S(2)}, u32[]{:S(2)}) collective-permute-start(f32[1,8,64,128]{3,2,1,0:T(8,128)S(1)} %broadcast_select_fusion), channel_id=1, source_target_pairs={{0,8},{16,24},{32,40},{48,56},{64,72},{80,88},{96,104},{112,120},{... | collective-permute-start | bytes 786440 | tf_op jit(solution)/shard_map/ppermute | solution.py:18
  111.0 6.0 %copy-start.4 = (f32[16]{0:T(128)S(1)}, f32[16]{0:T(128)}, u32[]{:S(2)}) copy-start(f32[16]{0:T(128)} %get-tuple-element.86) | copy-start | bytes 196
  118.4 24.1 %copy-start.3 = (f32[1024]{0:T(1024)S(1)}, f32[1024]{0:T(1024)}, u32[]{:S(2)}) copy-start(f32[1024]{0:T(1024)} %param.32) | copy-start | bytes 12292

commit v6 on v4

--- a/solution.py
+++ b/solution.py
@@ -45,17 +45,30 @@
     own = (gain, state)
     pair = unpack(shifted(pack(*own), axis, [(2 * c, 2 * c + 1) for c in range(chips)]), *shapes)
     chip_total = fold(pair, own)
-    for reach in (1, 2, 4):
+    for reach in (1, 2):
         route = [(2 * c + 1, 2 * (c + reach) + 1) for c in range(chips - reach)]
         got = unpack(shifted(pack(*chip_total), axis, route), *shapes)
         chip_total = fold(got, chip_total)
+    far = 5
     mine = lax.axis_index(axis)
     even = mine % 2 == 0
     split = state.shape[1] // 2
-    prefix = chip_total[1]
-    to_even = shifted(prefix[:, :split], axis, [(2 * c - 1, 2 * c) for c in range(1, chips)])
-    to_odd = shifted(prefix[:, split:], axis, [(2 * c - 1, 2 * c + 1) for c in range(1, chips)])
-    held = jnp.where(even, to_even, to_odd)
+    gain_t, state_t = chip_total
+    halves = ((gain.shape[0], split), (state.shape[0], split) + state.shape[2:])
+    near_lo = shifted(
+        pack(gain_t[:, :split], state_t[:, :split]), axis, [(2 * c - 1, 2 * c) for c in range(1, chips)]
+    )
+    near_hi = shifted(
+        pack(gain_t[:, split:], state_t[:, split:]), axis, [(2 * c - 1, 2 * c + 1) for c in range(1, chips)]
+    )
+    far_lo = shifted(
+        state_t[:, :split], axis, [(2 * (c - far) + 1, 2 * c) for c in range(far, chips)]
+    )
+    far_hi = shifted(
+        state_t[:, split:], axis, [(2 * (c - far) + 1, 2 * c + 1) for c in range(far, chips)]
+    )
+    near_gain, near_state = unpack(jnp.where(even, near_lo, near_hi), *halves)
+    held = near_gain[..., None, None] * jnp.where(even, far_lo, far_hi) + near_state
     swap = [(2 * c, 2 * c + 1) for c in range(chips)] + [(2 * c + 1, 2 * c) for c in range(chips)]
     other = shifted(held, axis, swap)
     behind = jnp.where(

time: 123 us -> 124 us (level)
  waiting for transfers between devices: 49.8 us -> 45.8 us
  other arithmetic: 15.4 us -> 18 us
  starting transfers between devices: 17.8 us -> 20 us
    ppermute x7 -> x8, waiting for transfers between devices: 47.4 us -> 43.4 us  [shifted(): return lax.ppermute(block, axis, pairs)]
    concatenate x4 -> x5, other arithmetic: 0.15 us -> 2.76 us  [pack(): return jnp.concatenate([flat, row])]
    ppermute x7 -> x8, starting transfers between devices: 15.9 us -> 18.1 us  [shifted(): return lax.ppermute(block, axis, pairs)]
  transfers between devices with their start and end apart: 8 -> 9, of which waited for: 3 -> 4; matrix products, arithmetic and copies ran while one was open for 9% -> 11% of each run, Pallas kernels for 0% -> 0%
where the time goes in v6:
time: 124 us; the launch traced here: 123 us
  waiting for transfers between devices  45.8 us (37%)
  starting transfers between devices  20 us (16%)
  other arithmetic  18 us (15%)
  blocking collectives  17.9 us (14%)
  local copies, waits for them, and re-layouts  15.1 us (12%)
  matrix products  5.79 us (5%)
    ppermute x8, waiting for transfers between devices, shifted(): return lax.ppermute(block, axis, pairs)  43.4 us
    ppermute x8, starting transfers between devices, shifted(): return lax.ppermute(block, axis, pairs)  18.1 us
    all_to_all x1, blocking collectives, summed_over(): return lax.all_to_all(spread, axis, 0, 0, tiled=False).sum(0)  17.9 us
    unnamed x32, local copies, waits for them, and re-layouts  5.59 us
    convert_element_type x2, other arithmetic, causal_conv(): return jax.nn.silu(result).astype(jnp.bfloat16)  3.67 us
    dot_general x1, matrix products, on_device(): jnp.einsum('cghqs,csghp->cqghp', mixing, x_heads, preferred_element_type=...  2.94 us
    concatenate x5, other arithmetic, pack(): return jnp.concatenate([flat, row])  2.76 us
  transfers between devices with their start and end apart: 9, of which 4 were waited for; matrix products, arithmetic and copies ran while one was open for 11% of the time, Pallas kernels for 0%

profile of v6, /device:TPU:6, one launch (start us, length us, event | category | flops | bytes accessed | tf_op | source)
XLA Modules:
  0.0 123.1 jit_solution(9536004537325607542)
XLA Ops:
  0.0 0.8 fusion.35
  2.7 1.9 %collective-permute-start = (bf16[3,1408]{0,1:T(8,128)(2,1)S(1)}, bf16[3,1408]{0,1:T(8,128)(2,1)S(1)}, u32[]{:S(2)}, u32[]{:S(2)}) collective-permute-start(bf16[3,1408]{0,1:T(8,128)(2,1)S(1)} %copy.91), channel_id=1, source_target_pairs={{0,8},{8,16},{16,24},{24,32},{32,40},{40,48},{48,56},{56,64},{64,7... | collective-permute-start | bytes 25352 | tf_op jit(solution)/shard_map/ppermute | solution.py:13
  6.0 0.9 broadcast_multiply_fusion
  6.9 1.2 reduce-window.6
  8.5 0.9 slice_convert_fusion.3
  9.6 1.0 copy.96
  11.1 2.4 %collective-permute-done = bf16[3,1408]{0,1:T(8,128)(2,1)S(1)} collective-permute-done((bf16[3,1408]{0,1:T(8,128)(2,1)S(1)}, bf16[3,1408]{0,1:T(8,128)(2,1)S(1)}, u32[]{:S(2)}, u32[]{:S(2)}) %collective-permute-start) | collective-permute-done | bytes 8480 | tf_op jit(solution)/shard_map/ppermute | solution.py:13
  14.6 0.8 multiply_convert_fusion.8
  15.6 2.8 %multiply_convert_fusion.5 = bf16[512,1024]{0,1:T(8,128)(2,1)S(1)} fusion(bf16[512,1024]{0,1:T(8,128)(2,1)S(1)} %copy.92, bf16[3,1024]{0,1:T(8,128)(2,1)S(1)} %slice.279, f32[1024]{0:T(1024)S(1)} %bitcast.164, f32[1024]{0:T(1024)S(1)} %bitcast.165, f32[1024]{0:T(1024)S(1)} %bitcast.163, f32[1024]{0:T(1024)S(1)} %bitcast.162, f32[1024]{0:T(1024)S(1)} %copy-done.8, ...), kind=kLoop, calls=%fused_computation.24 | loop fusion | flops 15728640 | bytes 2125824 | tf_op jit(solution)/shard_map/convert_element_type | solution.py:98
  18.8 1.7 %fusion.11 = f32[2,16,64,128]{3,2,1,0:T(8,128)S(1)} fusion(f32[2,16,256]{2,1,0:T(8,128)S(1)} %fusion.27, f32[2,256,128]{2,1,0:T(8,128)S(1)} %convert_element_type.130, bf16[2,256,16,64]{1,0,3,2:T(2,128)(2,1)S(1)} %reshape.668), kind=kOutput, calls=%fused_computation.15 | convolution fusion | flops 136314880 | bytes 2392064 | tf_op jit(solution)/shard_map/cghsn,csghp->cghpn/dot_general | solution.py:167
  20.7 1.3 %collective-permute-start.1 = (f32[1032,128]{1,0:T(8,128)S(1)}, f32[1032,128]{1,0:T(8,128)S(1)}, u32[]{:S(2)}, u32[]{:S(2)}) collective-permute-start(f32[1032,128]{1,0:T(8,128)S(1)} %select_maximum_fusion.2), channel_id=1, source_target_pairs={{0,8},{16,24},{32,40},{48,56},{64,72},{80,88},{96,104},{112,120},{... | collective-permute-start | bytes 1585160 | tf_op jit(solution)/shard_map/ppermute | solution.py:17
  22.0 1.5 %collective-permute-done.1 = f32[1032,128]{1,0:T(8,128)S(1)} collective-permute-done((f32[1032,128]{1,0:T(8,128)S(1)}, f32[1032,128]{1,0:T(8,128)S(1)}, u32[]{:S(2)}, u32[]{:S(2)}) %collective-permute-start.1) | collective-permute-done | bytes 528416 | tf_op jit(solution)/shard_map/ppermute | solution.py:17
  25.7 0.9 fusion.33
  26.6 1.0 select_maximum_fusion.4
  27.6 1.3 %collective-permute-start.4 = (f32[520,128]{1,0:T(8,128)S(1)}, f32[520,128]{1,0:T(8,128)}, u32[]{:S(2)}, u32[]{:S(2)}) collective-permute-start(f32[520,128]{1,0:T(8,128)S(1)} %select_maximum_fusion.4), channel_id=1, source_target_pairs={{8,16},{24,32},{40,48},{56,64},{72,80},{88,96},{104,112},{120,128}... | collective-permute-start | bytes 798728 | tf_op jit(solution)/shard_map/ppermute | solution.py:17
  28.9 1.7 %select_maximum_fusion.3 = f32[520,128]{1,0:T(8,128)} fusion(f32[1,8]{1,0:T(1,128)S(1)} %get-tuple-element.98, f32[512,128]{1,0:T(8,128)} %bitcast.35), kind=kLoop, calls=%fused_computation.54 | loop fusion | flops 199680 | bytes 528416 | tf_op jit(solution)/shard_map/concatenate | solution.py:30
  30.5 1.4 %collective-permute-start.5 = (f32[520,128]{1,0:T(8,128)}, f32[520,128]{1,0:T(8,128)}, u32[]{:S(2)}, u32[]{:S(2)}) collective-permute-start(f32[520,128]{1,0:T(8,128)} %select_maximum_fusion.3), channel_id=1, source_target_pairs={{8,24},{24,40},{40,56},{56,72},{72,88},{88,104},{104,120},{120,136... | collective-permute-start | bytes 798728 | tf_op jit(solution)/shard_map/ppermute | solution.py:17
  32.0 1.5 %copy.106 = bf16[512,1024]{0,1:T(8,128)(2,1)S(1)} copy(bf16[512,1024]{1,0:T(8,128)(2,1)} %param.25) | data formatting | bytes 2097152 | tf_op args[2]
  33.5 0.8 compare_and_fusion
  34.3 1.3 %collective-permute-start.6 = (f32[1,8,64,128]{3,2,1,0:T(8,128)}, f32[1,8,64,128]{3,2,1,0:T(8,128)S(1)}, u32[]{:S(2)}, u32[]{:S(2)}) collective-permute-start(f32[1,8,64,128]{3,2,1,0:T(8,128)} %get-tuple-element.72), channel_id=1, source_target_pairs={{8,80},{24,96},{40,112},{56,128},{72,144},{88,160},{104,176},{120,... | collective-permute-start | bytes 786440 | tf_op jit(solution)/shard_map/ppermute | solution.py:17
  36.3 20.0 %collective-permute-done.4 = f32[520,128]{1,0:T(8,128)} collective-permute-done((f32[520,128]{1,0:T(8,128)S(1)}, f32[520,128]{1,0:T(8,128)}, u32[]{:S(2)}, u32[]{:S(2)}) %collective-permute-start.4) | collective-permute-done | bytes 266272 | tf_op jit(solution)/shard_map/ppermute | solution.py:17
  56.3 1.0 broadcast_select_fusion
  57.3 21.8 %collective-permute-done.6 = f32[1,8,64,128]{3,2,1,0:T(8,128)S(1)} collective-permute-done((f32[1,8,64,128]{3,2,1,0:T(8,128)}, f32[1,8,64,128]{3,2,1,0:T(8,128)S(1)}, u32[]{:S(2)}, u32[]{:S(2)}) %collective-permute-start.6) | collective-permute-done | bytes 262176 | tf_op jit(solution)/shard_map/ppermute | solution.py:17
  79.2 10.8 %collective-permute-start.8 = (f32[1,8,64,128]{3,2,1,0:T(8,128)S(1)}, f32[1,8,64,128]{3,2,1,0:T(8,128)S(1)}, u32[]{:S(2)}, u32[]{:S(2)}) collective-permute-start(f32[1,8,64,128]{3,2,1,0:T(8,128)S(1)} %multiply_add_fusion.3), channel_id=1, source_target_pairs={{0,8},{16,24},{32,40},{48,56},{64,72},{80,88},{96,104},{112,120},{... | collective-permute-start | bytes 786440 | tf_op jit(solution)/shard_map/ppermute | solution.py:17
  90.1 2.3 %reshape.698 = f32[2,256,1,16,64]{1,0,4,3,2:T(2,128)} reshape(bf16[512,1024]{0,1:T(8,128)(2,1)S(1)} %multiply_convert_fusion.5) | data formatting | bytes 3145728 | tf_op jit(solution)/shard_map/convert_element_type | solution.py:196
  92.8 0.8 copy-done.1
  93.9 1.0 fusion.18
  95.8 2.9 %fusion.13 = f32[2,256,1,16,64]{1,4,3,0,2:T(8,128)S(1)} fusion(f32[2,16,64,256]{3,2,1,0:T(8,128)S(1)} %fusion.18, f32[2,256,1,16,64]{1,0,4,3,2:T(2,128)S(1)} %copy-done.2, f32[2,16,256]{2,1,0:T(8,128)S(1)} %bitcast.161, f32[2,16,256]{2,1,0:T(8,128)S(1)} %get-tuple-element.75, f32[2,256,256]{2,1,0:T(8,128)S(1)} %fusion.37, ...), kind=kOutput, calls=%fused_computation.18 | convolution fusion | flops 283115520 | bytes 8093760 | tf_op jit(solution)/shard_map/cghqs,csghp->cqghp/dot_general | solution.py:161
  98.7 1.6 %copy.105 = f32[2,256,1,16,64]{1,0,4,3,2:T(2,128)S(1)} copy(f32[2,256,1,16,64]{1,4,3,0,2:T(8,128)S(1)} %fusion.13) | data formatting | bytes 4194304 | tf_op jit(solution)/shard_map/add | solution.py:196
  101.2 17.9 %all_to_all.6 = f32[8,1,512]{2,1,0:T(1,128)S(1)} all-to-all(f32[8,1,512]{2,1,0:T(1,128)S(1)} %broadcast_in_dim.143), channel_id=1, replica_groups=mesh['seq'=64,'tp'=8] {'tp'}, dimensions={0} | all-to-all | bytes 32768 | tf_op jit(solution)/shard_map/all_to_all | solution.py:86
  119.2 1.7 %multiply_convert_fusion.4 = bf16[512,1024]{0,1:T(8,128)(2,1)} fusion(f32[1024]{0:T(1024)S(1)} %copy-done.9, f32[512]{0:T(512)S(1)} %add_rsqrt_fusion, f32[512,1024]{0,1:T(8,128)S(1)} %bitcast.142, bf16[512,1024]{0,1:T(8,128)(2,1)S(1)} %copy.106), kind=kLoop, calls=%fused_computation.20 | loop fusion | flops 4718592 | bytes 4200448 | tf_op jit(solution)/shard_map/convert_element_type | solution.py:200
  120.9 2.3 %copy.108 = bf16[512,1024]{1,0:T(8,128)(2,1)} copy(bf16[512,1024]{0,1:T(8,128)(2,1)} %multiply_convert_fusion.4) | data formatting | bytes 2097152 | tf_op jit(solution)/shard_map/convert_element_type | solution.py:200
  (96 shorter events, 11.5 us)
Async XLA Ops:
  0.0 13.6 %copy-start.7 = (s32[512]{0:T(512)S(1)}, s32[512]{0:T(512)}, u32[]{:S(2)}) copy-start(s32[512]{0:T(512)} %param.35) | copy-start | bytes 6148
  0.0 10.5 %copy-start.3 = (bf16[512,1024]{1,0:T(8,128)(2,1)S(1)}, bf16[512,1024]{1,0:T(8,128)(2,1)}, u32[]{:S(2)}) copy-start(bf16[512,1024]{1,0:T(8,128)(2,1)} %param.23) | copy-start | bytes 3145732
  0.0 14.6 %copy-start.11 = (f32[2,128]{1,0:T(2,128)S(1)}, f32[2,128]{1,0:T(2,128)}, u32[]{:S(2)}) copy-start(f32[2,128]{1,0:T(2,128)} %param.30) | copy-start | bytes 3076
  2.7 10.9 %collective-permute-start = (bf16[3,1408]{0,1:T(8,128)(2,1)S(1)}, bf16[3,1408]{0,1:T(8,128)(2,1)S(1)}, u32[]{:S(2)}, u32[]{:S(2)}) collective-permute-start(bf16[3,1408]{0,1:T(8,128)(2,1)S(1)} %copy.91), channel_id=1, source_target_pairs={{0,8},{8,16},{16,24},{24,32},{32,40},{40,48},{48,56},{56,64},{64,7... | collective-permute-start | bytes 25352 | tf_op jit(solution)/shard_map/ppermute | solution.py:13
  10.6 5.0 %copy-start.8 = (f32[1024]{0:T(1024)S(1)}, f32[1024]{0:T(1024)}, u32[]{:S(2)}) copy-start(f32[1024]{0:T(1024)} %param.29) | copy-start | bytes 12292
  18.7 1.9 %copy-start.4 = (bf16[2,256,16,64]{1,0,3,2:T(2,128)(2,1)}, bf16[2,256,16,64]{1,0,3,2:T(2,128)(2,1)S(1)}, u32[]{:S(2)}) copy-start(bf16[2,256,16,64]{1,0,3,2:T(2,128)(2,1)S(1)} %reshape.668) | copy-start | bytes 3145732
  20.5 3.3 %copy-start = (f32[2,16,64,128]{3,2,1,0:T(8,128)}, f32[2,16,64,128]{3,2,1,0:T(8,128)S(1)}, u32[]{:S(2)}) copy-start(f32[2,16,64,128]{3,2,1,0:T(8,128)S(1)} %fusion.11) | copy-start | bytes 3145732
  20.7 2.8 %collective-permute-start.1 = (f32[1032,128]{1,0:T(8,128)S(1)}, f32[1032,128]{1,0:T(8,128)S(1)}, u32[]{:S(2)}, u32[]{:S(2)}) collective-permute-start(f32[1032,128]{1,0:T(8,128)S(1)} %select_maximum_fusion.2), channel_id=1, source_target_pairs={{0,8},{16,24},{32,40},{48,56},{64,72},{80,88},{96,104},{112,120},{... | collective-permute-start | bytes 1585160 | tf_op jit(solution)/shard_map/ppermute | solution.py:17
  23.8 0.7 collective-permute-start.2
  24.8 0.7 collective-permute-start.3
  27.6 28.7 %collective-permute-start.4 = (f32[520,128]{1,0:T(8,128)S(1)}, f32[520,128]{1,0:T(8,128)}, u32[]{:S(2)}, u32[]{:S(2)}) collective-permute-start(f32[520,128]{1,0:T(8,128)S(1)} %select_maximum_fusion.4), channel_id=1, source_target_pairs={{8,16},{24,32},{40,48},{56,64},{72,80},{88,96},{104,112},{120,128}... | collective-permute-start | bytes 798728 | tf_op jit(solution)/shard_map/ppermute | solution.py:17
  30.5 25.8 %collective-permute-start.5 = (f32[520,128]{1,0:T(8,128)}, f32[520,128]{1,0:T(8,128)}, u32[]{:S(2)}, u32[]{:S(2)}) collective-permute-start(f32[520,128]{1,0:T(8,128)} %select_maximum_fusion.3), channel_id=1, source_target_pairs={{8,24},{24,40},{40,56},{56,72},{72,88},{88,104},{104,120},{120,136... | collective-permute-start | bytes 798728 | tf_op jit(solution)/shard_map/ppermute | solution.py:17
  34.3 44.9 %collective-permute-start.6 = (f32[1,8,64,128]{3,2,1,0:T(8,128)}, f32[1,8,64,128]{3,2,1,0:T(8,128)S(1)}, u32[]{:S(2)}, u32[]{:S(2)}) collective-permute-start(f32[1,8,64,128]{3,2,1,0:T(8,128)} %get-tuple-element.72), channel_id=1, source_target_pairs={{8,80},{24,96},{40,112},{56,128},{72,144},{88,160},{104,176},{120,... | collective-permute-start | bytes 786440 | tf_op jit(solution)/shard_map/ppermute | solution.py:17
  35.6 43.6 %collective-permute-start.7 = (f32[1,8,64,128]{3,2,1,0:T(8,128)}, f32[1,8,64,128]{3,2,1,0:T(8,128)S(1)}, u32[]{:S(2)}, u32[]{:S(2)}) collective-permute-start(f32[1,8,64,128]{3,2,1,0:T(8,128)} %get-tuple-element.71), channel_id=1, source_target_pairs={{8,88},{24,104},{40,120},{56,136},{72,152},{88,168},{104,184},{120... | collective-permute-start | bytes 786440 | tf_op jit(solution)/shard_map/ppermute | solution.py:17
  79.2 13.4 %collective-permute-start.8 = (f32[1,8,64,128]{3,2,1,0:T(8,128)S(1)}, f32[1,8,64,128]{3,2,1,0:T(8,128)S(1)}, u32[]{:S(2)}, u32[]{:S(2)}) collective-permute-start(f32[1,8,64,128]{3,2,1,0:T(8,128)S(1)} %multiply_add_fusion.3), channel_id=1, source_target_pairs={{0,8},{16,24},{32,40},{48,56},{64,72},{80,88},{96,104},{112,120},{... | collective-permute-start | bytes 786440 | tf_op jit(solution)/shard_map/ppermute | solution.py:17
  90.1 2.7 %copy-start.10 = (f32[16]{0:T(128)S(1)}, f32[16]{0:T(128)}, u32[]{:S(2)}) copy-start(f32[16]{0:T(128)} %get-tuple-element.93) | copy-start | bytes 196
  92.4 1.2 copy-start.1
  93.9 1.6 %copy-start.2 = (f32[2,256,1,16,64]{1,0,4,3,2:T(2,128)S(1)}, f32[2,256,1,16,64]{1,0,4,3,2:T(2,128)}, u32[]{:S(2)}) copy-start(f32[2,256,1,16,64]{1,0,4,3,2:T(2,128)} %reshape.698) | copy-start | bytes 6291460
  93.9 1.8 %copy-start.5 = (bf16[2,256,16,64]{1,0,3,2:T(2,128)(2,1)S(1)}, bf16[2,256,16,64]{1,0,3,2:T(2,128)(2,1)}, u32[]{:S(2)}) copy-start(bf16[2,256,16,64]{1,0,3,2:T(2,128)(2,1)} %copy-done.4) | copy-start | bytes 3145732
  93.9 1.8 %copy-start.6 = (pred[2,256,256]{2,1,0:T(8,128)(4,1)S(1)}, pred[2,256,256]{2,1,0:T(8,128)(4,1)}, u32[]{:S(2)}) copy-start(pred[2,256,256]{2,1,0:T(8,128)(4,1)} %compare_and_fusion) | copy-start | bytes 393220
  93.9 1.8 %copy-start.12 = (f32[16]{0:T(128)S(1)}, f32[16]{0:T(128)}, u32[]{:S(2)}) copy-start(f32[16]{0:T(128)} %param.33) | copy-start | bytes 196
  100.5 18.6 %copy-start.9 = (f32[1024]{0:T(1024)S(1)}, f32[1024]{0:T(1024)}, u32[]{:S(2)}) copy-start(f32[1024]{0:T(1024)} %param.34) | copy-start | bytes 12292

commit v7 on v4

--- a/solution.py
+++ b/solution.py
@@ -45,24 +45,22 @@
     own = (gain, state)
     pair = unpack(shifted(pack(*own), axis, [(2 * c, 2 * c + 1) for c in range(chips)]), *shapes)
     chip_total = fold(pair, own)
-    for reach in (1, 2, 4):
+    for reach in (1, 2):
         route = [(2 * c + 1, 2 * (c + reach) + 1) for c in range(chips - reach)]
         got = unpack(shifted(pack(*chip_total), axis, route), *shapes)
         chip_total = fold(got, chip_total)
+    far = 5
     mine = lax.axis_index(axis)
     even = mine % 2 == 0
-    split = state.shape[1] // 2
-    prefix = chip_total[1]
-    to_even = shifted(prefix[:, :split], axis, [(2 * c - 1, 2 * c) for c in range(1, chips)])
-    to_odd = shifted(prefix[:, split:], axis, [(2 * c - 1, 2 * c + 1) for c in range(1, chips)])
-    held = jnp.where(even, to_even, to_odd)
+    gain_t, state_t = chip_total
+    far_state = shifted(state_t, axis, [(2 * (c - far) + 1, 2 * c + 1) for c in range(far, chips)])
+    near = shifted(pack(*chip_total), axis, [(2 * c - 1, 2 * c) for c in range(1, chips)])
+    held = jnp.where(even, near, pack(gain_t, far_state))
     swap = [(2 * c, 2 * c + 1) for c in range(chips)] + [(2 * c + 1, 2 * c) for c in range(chips)]
     other = shifted(held, axis, swap)
-    behind = jnp.where(
-        even,
-        jnp.concatenate([held, other], axis=1),
-        jnp.concatenate([other, held], axis=1),
-    )
+    near_gain, near_state = unpack(jnp.where(even, held, other), *shapes)
+    _, far_got = unpack(jnp.where(even, other, held), *shapes)
+    behind = near_gain[..., None, None] * far_got + near_state
     odd_entering = pair[0][..., None, None] * behind + pair[1]
     return jnp.where(even, behind, odd_entering)
 

time: 123 us -> 121 us (0.984)
  the two profiles are of different devices: /device:TPU:6 before, /device:TPU:4 now
where the time goes in v7:
time: 121 us; the launch traced here: 120 us
  waiting for transfers between devices  34.8 us (29%)
  starting transfers between devices  29.8 us (25%)
  other arithmetic  18.2 us (15%)
  blocking collectives  17.9 us (15%)
  local copies, waits for them, and re-layouts  13.4 us (11%)
  matrix products  5.78 us (5%)
    ppermute x6, waiting for transfers between devices, shifted(): return lax.ppermute(block, axis, pairs)  32.4 us
    ppermute x6, starting transfers between devices, shifted(): return lax.ppermute(block, axis, pairs)  27.9 us
    all_to_all x1, blocking collectives, summed_over(): return lax.all_to_all(spread, axis, 0, 0, tiled=False).sum(0)  17.9 us
    unnamed x30, local copies, waits for them, and re-layouts  4.76 us
    convert_element_type x2, other arithmetic, causal_conv(): return jax.nn.silu(result).astype(jnp.bfloat16)  3.67 us
    dot_general x1, matrix products, on_device(): jnp.einsum('cghqs,csghp->cqghp', mixing, x_heads, preferred_element_type=...  2.92 us
  transfers between devices with their start and end apart: 7, of which 3 were waited for; matrix products, arithmetic and copies ran while one was open for 9% of the time, Pallas kernels for 0%

profile of v7, /device:TPU:4, one launch (start us, length us, event | category | flops | bytes accessed | tf_op | source)
XLA Modules:
  0.0 120.4 jit_solution(13159967527974895811)
XLA Ops:
  0.0 0.8 fusion.37
  1.6 0.7 slice.215
  2.7 1.9 %collective-permute-start = (bf16[3,1408]{0,1:T(8,128)(2,1)S(1)}, bf16[3,1408]{0,1:T(8,128)(2,1)S(1)}, u32[]{:S(2)}, u32[]{:S(2)}) collective-permute-start(bf16[3,1408]{0,1:T(8,128)(2,1)S(1)} %copy.91), channel_id=1, source_target_pairs={{0,8},{8,16},{16,24},{24,32},{32,40},{40,48},{48,56},{56,64},{64,7... | collective-permute-start | bytes 25352 | tf_op jit(solution)/shard_map/ppermute | solution.py:13
  4.6 0.7 bitcast_convert_fusion.3
  6.0 0.9 broadcast_multiply_fusion
  6.9 1.2 reduce-window.6
  8.5 0.9 slice_convert_fusion.3
  9.6 1.0 copy.96
  11.1 2.4 %collective-permute-done = bf16[3,1408]{0,1:T(8,128)(2,1)S(1)} collective-permute-done((bf16[3,1408]{0,1:T(8,128)(2,1)S(1)}, bf16[3,1408]{0,1:T(8,128)(2,1)S(1)}, u32[]{:S(2)}, u32[]{:S(2)}) %collective-permute-start) | collective-permute-done | bytes 8480 | tf_op jit(solution)/shard_map/ppermute | solution.py:13
  14.1 0.8 multiply_convert_fusion.8
  15.0 2.8 %multiply_convert_fusion.5 = bf16[512,1024]{0,1:T(8,128)(2,1)S(1)} fusion(bf16[512,1024]{0,1:T(8,128)(2,1)S(1)} %copy.92, bf16[3,1024]{0,1:T(8,128)(2,1)S(1)} %slice.259, f32[1024]{0:T(1024)S(1)} %bitcast.167, f32[1024]{0:T(1024)S(1)} %bitcast.168, f32[1024]{0:T(1024)S(1)} %bitcast.166, f32[1024]{0:T(1024)S(1)} %bitcast.165, f32[1024]{0:T(1024)S(1)} %copy-done.8, ...), kind=kLoop, calls=%fused_computation.24 | loop fusion | flops 15728640 | bytes 2125824 | tf_op jit(solution)/shard_map/convert_element_type | solution.py:83
  18.2 1.7 %fusion.11 = f32[2,16,64,128]{3,2,1,0:T(8,128)S(1)} fusion(f32[2,16,256]{2,1,0:T(8,128)S(1)} %fusion.30, f32[2,256,128]{2,1,0:T(8,128)S(1)} %convert_element_type.130, bf16[2,256,16,64]{1,0,3,2:T(2,128)(2,1)S(1)} %reshape.590), kind=kOutput, calls=%fused_computation.15 | convolution fusion | flops 136314880 | bytes 2392064 | tf_op jit(solution)/shard_map/cghsn,csghp->cghpn/dot_general | solution.py:152
  20.1 1.3 %collective-permute-start.1 = (f32[1032,128]{1,0:T(8,128)S(1)}, f32[1032,128]{1,0:T(8,128)S(1)}, u32[]{:S(2)}, u32[]{:S(2)}) collective-permute-start(f32[1032,128]{1,0:T(8,128)S(1)} %select_maximum_fusion.2), channel_id=1, source_target_pairs={{0,8},{16,24},{32,40},{48,56},{64,72},{80,88},{96,104},{112,120},{... | collective-permute-start | bytes 1585160 | tf_op jit(solution)/shard_map/ppermute | solution.py:17
  21.5 1.5 %collective-permute-done.1 = f32[1032,128]{1,0:T(8,128)S(1)} collective-permute-done((f32[1032,128]{1,0:T(8,128)S(1)}, f32[1032,128]{1,0:T(8,128)S(1)}, u32[]{:S(2)}, u32[]{:S(2)}) %collective-permute-start.1) | collective-permute-done | bytes 528416 | tf_op jit(solution)/shard_map/ppermute | solution.py:17
  23.2 0.7 collective-permute-start.2
  24.2 0.7 collective-permute-start.3
  25.1 1.3 %collective-permute-start.4 = (f32[1032,128]{1,0:T(8,128)S(1)}, f32[1032,128]{1,0:T(8,128)}, u32[]{:S(2)}, u32[]{:S(2)}) collective-permute-start(f32[1032,128]{1,0:T(8,128)S(1)} %fusion.23), channel_id=1, source_target_pairs={{8,16},{24,32},{40,48},{56,64},{72,80},{88,96},{104,112},{120,128}... | collective-permute-start | bytes 1585160 | tf_op jit(solution)/shard_map/ppermute | solution.py:17
  26.4 1.5 %collective-permute-start.5 = (f32[1,16,64,128]{3,2,1,0:T(8,128)S(1)}, f32[1,16,64,128]{3,2,1,0:T(8,128)}, u32[]{:S(2)}, u32[]{:S(2)}) collective-permute-start(f32[1,16,64,128]{3,2,1,0:T(8,128)S(1)} %multiply_add_fusion), channel_id=1, source_target_pairs={{8,88},{24,104},{40,120},{56,136},{72,152},{88,168},{104,184},{120... | collective-permute-start | bytes 1572872 | tf_op jit(solution)/shard_map/ppermute | solution.py:17
  27.9 30.9 %collective-permute-done.4 = f32[1032,128]{1,0:T(8,128)} collective-permute-done((f32[1032,128]{1,0:T(8,128)S(1)}, f32[1032,128]{1,0:T(8,128)}, u32[]{:S(2)}, u32[]{:S(2)}) %collective-permute-start.4) | collective-permute-done | bytes 528416 | tf_op jit(solution)/shard_map/ppermute | solution.py:17
  58.8 2.0 %fusion.25 = f32[1032,128]{1,0:T(8,128)} fusion(f32[1032,128]{1,0:T(8,128)} %collective-permute-done.4, f32[1,16]{1,0:T(1,128)S(1)} %slice_multiply_fusion, f32[1024,128]{1,0:T(8,128)} %bitcast.35, pred[]{:T(512)S(6)} %eq.75), kind=kLoop, calls=%fused_computation.41 | loop fusion | flops 528384 | bytes 1581121 | tf_op jit(solution)/shard_map/jit(_where)/select_n | solution.py:58
  60.9 22.4 %collective-permute-start.6 = (f32[1032,128]{1,0:T(8,128)}, f32[1032,128]{1,0:T(8,128)}, u32[]{:S(2)}, u32[]{:S(2)}) collective-permute-start(f32[1032,128]{1,0:T(8,128)} %fusion.25), channel_id=1, source_target_pairs={{0,8},{16,24},{32,40},{48,56},{64,72},{80,88},{96,104},{112,120},{... | collective-permute-start | bytes 1585160 | tf_op jit(solution)/shard_map/ppermute | solution.py:17
  83.3 0.8 compare_and_fusion
  84.1 1.5 %copy.106 = bf16[512,1024]{0,1:T(8,128)(2,1)S(1)} copy(bf16[512,1024]{1,0:T(8,128)(2,1)} %param.25) | data formatting | bytes 2097152 | tf_op args[2]
  85.6 2.3 %reshape.623 = f32[2,256,1,16,64]{1,0,4,3,2:T(2,128)} reshape(bf16[512,1024]{0,1:T(8,128)(2,1)S(1)} %multiply_convert_fusion.5) | data formatting | bytes 3145728 | tf_op jit(solution)/shard_map/convert_element_type | solution.py:181
  88.3 1.2 broadcast_select_fusion
  89.5 1.3 %slice_select_fusion = f32[1024,128]{1,0:T(8,128)S(1)} fusion(f32[1032,128]{1,0:T(8,128)} %fusion.25, f32[1032,128]{1,0:T(8,128)} %collective-permute-done.6, pred[]{:T(512)S(6)} %eq.75), kind=kLoop, calls=%fused_computation.46 | loop fusion | flops 131072 | bytes 1572865 | tf_op jit(solution)/shard_map/jit(_where)/select_n | solution.py:62
  91.3 1.0 fusion.18
  93.1 2.9 %fusion.13 = f32[2,256,1,16,64]{1,4,3,0,2:T(8,128)S(1)} fusion(f32[2,16,64,256]{3,2,1,0:T(8,128)S(1)} %fusion.18, f32[2,256,1,16,64]{1,0,4,3,2:T(2,128)S(1)} %copy-done.2, f32[2,16,256]{2,1,0:T(8,128)S(1)} %bitcast.164, f32[2,16,256]{2,1,0:T(8,128)S(1)} %get-tuple-element.69, f32[2,256,256]{2,1,0:T(8,128)S(1)} %fusion.38, ...), kind=kOutput, calls=%fused_computation.18 | convolution fusion | flops 283115520 | bytes 8093760 | tf_op jit(solution)/shard_map/cghqs,csghp->cqghp/dot_general | solution.py:146
  96.0 1.6 %copy.105 = f32[2,256,1,16,64]{1,0,4,3,2:T(2,128)S(1)} copy(f32[2,256,1,16,64]{1,4,3,0,2:T(8,128)S(1)} %fusion.13) | data formatting | bytes 4194304 | tf_op jit(solution)/shard_map/add | solution.py:181
  98.5 17.9 %all_to_all.6 = f32[8,1,512]{2,1,0:T(1,128)S(1)} all-to-all(f32[8,1,512]{2,1,0:T(1,128)S(1)} %broadcast_in_dim.143), channel_id=1, replica_groups=mesh['seq'=64,'tp'=8] {'tp'}, dimensions={0} | all-to-all | bytes 32768 | tf_op jit(solution)/shard_map/all_to_all | solution.py:71
  116.5 1.7 %multiply_convert_fusion.4 = bf16[512,1024]{0,1:T(8,128)(2,1)} fusion(f32[1024]{0:T(1024)S(1)} %copy-done.9, f32[512]{0:T(512)S(1)} %add_rsqrt_fusion, f32[512,1024]{0,1:T(8,128)S(1)} %bitcast.143, bf16[512,1024]{0,1:T(8,128)(2,1)S(1)} %copy.106), kind=kLoop, calls=%fused_computation.20 | loop fusion | flops 4718592 | bytes 4200448 | tf_op jit(solution)/shard_map/convert_element_type | solution.py:185
  118.2 2.3 %copy.108 = bf16[512,1024]{1,0:T(8,128)(2,1)} copy(bf16[512,1024]{0,1:T(8,128)(2,1)} %multiply_convert_fusion.4) | data formatting | bytes 2097152 | tf_op jit(solution)/shard_map/convert_element_type | solution.py:185
  (88 shorter events, 7.3 us)
Async XLA Ops:
  0.0 13.6 %copy-start.7 = (s32[512]{0:T(512)S(1)}, s32[512]{0:T(512)}, u32[]{:S(2)}) copy-start(s32[512]{0:T(512)} %param.35) | copy-start | bytes 6148
  0.0 10.5 %copy-start.3 = (bf16[512,1024]{1,0:T(8,128)(2,1)S(1)}, bf16[512,1024]{1,0:T(8,128)(2,1)}, u32[]{:S(2)}) copy-start(bf16[512,1024]{1,0:T(8,128)(2,1)} %param.23) | copy-start | bytes 3145732
  0.0 14.1 %copy-start.10 = (f32[2,128]{1,0:T(2,128)S(1)}, f32[2,128]{1,0:T(2,128)}, u32[]{:S(2)}) copy-start(f32[2,128]{1,0:T(2,128)} %param.30) | copy-start | bytes 3076
  2.7 10.9 %collective-permute-start = (bf16[3,1408]{0,1:T(8,128)(2,1)S(1)}, bf16[3,1408]{0,1:T(8,128)(2,1)S(1)}, u32[]{:S(2)}, u32[]{:S(2)}) collective-permute-start(bf16[3,1408]{0,1:T(8,128)(2,1)S(1)} %copy.91), channel_id=1, source_target_pairs={{0,8},{8,16},{16,24},{24,32},{32,40},{40,48},{48,56},{56,64},{64,7... | collective-permute-start | bytes 25352 | tf_op jit(solution)/shard_map/ppermute | solution.py:13
  10.6 4.4 %copy-start.8 = (f32[1024]{0:T(1024)S(1)}, f32[1024]{0:T(1024)}, u32[]{:S(2)}) copy-start(f32[1024]{0:T(1024)} %param.29) | copy-start | bytes 12292
  18.1 1.9 %copy-start.4 = (bf16[2,256,16,64]{1,0,3,2:T(2,128)(2,1)}, bf16[2,256,16,64]{1,0,3,2:T(2,128)(2,1)S(1)}, u32[]{:S(2)}) copy-start(bf16[2,256,16,64]{1,0,3,2:T(2,128)(2,1)S(1)} %reshape.590) | copy-start | bytes 3145732
  19.9 3.3 %copy-start = (f32[2,16,64,128]{3,2,1,0:T(8,128)}, f32[2,16,64,128]{3,2,1,0:T(8,128)S(1)}, u32[]{:S(2)}) copy-start(f32[2,16,64,128]{3,2,1,0:T(8,128)S(1)} %fusion.11) | copy-start | bytes 3145732
  20.1 2.8 %collective-permute-start.1 = (f32[1032,128]{1,0:T(8,128)S(1)}, f32[1032,128]{1,0:T(8,128)S(1)}, u32[]{:S(2)}, u32[]{:S(2)}) collective-permute-start(f32[1032,128]{1,0:T(8,128)S(1)} %select_maximum_fusion.2), channel_id=1, source_target_pairs={{0,8},{16,24},{32,40},{48,56},{64,72},{80,88},{96,104},{112,120},{... | collective-permute-start | bytes 1585160 | tf_op jit(solution)/shard_map/ppermute | solution.py:17
  23.2 0.7 collective-permute-start.2
  24.2 0.7 collective-permute-start.3
  25.1 33.7 %collective-permute-start.4 = (f32[1032,128]{1,0:T(8,128)S(1)}, f32[1032,128]{1,0:T(8,128)}, u32[]{:S(2)}, u32[]{:S(2)}) collective-permute-start(f32[1032,128]{1,0:T(8,128)S(1)} %fusion.23), channel_id=1, source_target_pairs={{8,16},{24,32},{40,48},{56,64},{72,80},{88,96},{104,112},{120,128}... | collective-permute-start | bytes 1585160 | tf_op jit(solution)/shard_map/ppermute | solution.py:17
  26.4 1.5 %collective-permute-start.5 = (f32[1,16,64,128]{3,2,1,0:T(8,128)S(1)}, f32[1,16,64,128]{3,2,1,0:T(8,128)}, u32[]{:S(2)}, u32[]{:S(2)}) collective-permute-start(f32[1,16,64,128]{3,2,1,0:T(8,128)S(1)} %multiply_add_fusion), channel_id=1, source_target_pairs={{8,88},{24,104},{40,120},{56,136},{72,152},{88,168},{104,184},{120... | collective-permute-start | bytes 1572872 | tf_op jit(solution)/shard_map/ppermute | solution.py:17
  60.9 27.4 %collective-permute-start.6 = (f32[1032,128]{1,0:T(8,128)}, f32[1032,128]{1,0:T(8,128)}, u32[]{:S(2)}, u32[]{:S(2)}) collective-permute-start(f32[1032,128]{1,0:T(8,128)} %fusion.25), channel_id=1, source_target_pairs={{0,8},{16,24},{32,40},{48,56},{64,72},{80,88},{96,104},{112,120},{... | collective-permute-start | bytes 1585160 | tf_op jit(solution)/shard_map/ppermute | solution.py:17
  88.3 2.5 %copy-start.1 = (f32[2,16,64,128]{3,2,1,0:T(8,128)S(1)}, f32[2,16,64,128]{3,2,1,0:T(8,128)}, u32[]{:S(2)}) copy-start(f32[2,16,64,128]{3,2,1,0:T(8,128)} %copy-done) | copy-start | bytes 3145732
  91.2 1.6 %copy-start.2 = (f32[2,256,1,16,64]{1,0,4,3,2:T(2,128)S(1)}, f32[2,256,1,16,64]{1,0,4,3,2:T(2,128)}, u32[]{:S(2)}) copy-start(f32[2,256,1,16,64]{1,0,4,3,2:T(2,128)} %reshape.623) | copy-start | bytes 6291460
  91.2 1.8 %copy-start.5 = (bf16[2,256,16,64]{1,0,3,2:T(2,128)(2,1)S(1)}, bf16[2,256,16,64]{1,0,3,2:T(2,128)(2,1)}, u32[]{:S(2)}) copy-start(bf16[2,256,16,64]{1,0,3,2:T(2,128)(2,1)} %copy-done.4) | copy-start | bytes 3145732
  91.2 1.8 %copy-start.6 = (pred[2,256,256]{2,1,0:T(8,128)(4,1)S(1)}, pred[2,256,256]{2,1,0:T(8,128)(4,1)}, u32[]{:S(2)}) copy-start(pred[2,256,256]{2,1,0:T(8,128)(4,1)} %compare_and_fusion) | copy-start | bytes 393220
  91.3 1.8 %copy-start.11 = (f32[16]{0:T(128)S(1)}, f32[16]{0:T(128)}, u32[]{:S(2)}) copy-start(f32[16]{0:T(128)} %param.33) | copy-start | bytes 196
  97.8 18.6 %copy-start.9 = (f32[1024]{0:T(1024)S(1)}, f32[1024]{0:T(1024)}, u32[]{:S(2)}) copy-start(f32[1024]{0:T(1024)} %param.34) | copy-start | bytes 12292

commit v8 on v7

--- a/solution.py
+++ b/solution.py
@@ -45,22 +45,27 @@
     own = (gain, state)
     pair = unpack(shifted(pack(*own), axis, [(2 * c, 2 * c + 1) for c in range(chips)]), *shapes)
     chip_total = fold(pair, own)
-    for reach in (1, 2):
-        route = [(2 * c + 1, 2 * (c + reach) + 1) for c in range(chips - reach)]
-        got = unpack(shifted(pack(*chip_total), axis, route), *shapes)
-        chip_total = fold(got, chip_total)
-    far = 5
+    route = [(2 * c + 1, 2 * (c + 1) + 1) for c in range(chips - 1)]
+    chip_total = fold(unpack(shifted(pack(*chip_total), axis, route), *shapes), chip_total)
     mine = lax.axis_index(axis)
     even = mine % 2 == 0
-    gain_t, state_t = chip_total
-    far_state = shifted(state_t, axis, [(2 * (c - far) + 1, 2 * c + 1) for c in range(far, chips)])
-    near = shifted(pack(*chip_total), axis, [(2 * c - 1, 2 * c) for c in range(1, chips)])
-    held = jnp.where(even, near, pack(gain_t, far_state))
+    packed = pack(*chip_total)
+
+    def fetch(value, back, core):
+        return shifted(value, axis, [(2 * (c - back) + 1, 2 * c + core) for c in range(back, chips)])
+
+    far_last = unpack(fetch(packed, 7, 1), *shapes)
+    far_next = unpack(fetch(packed, 5, 1), *shapes)
+    near_last = unpack(fetch(packed, 3, 0), *shapes)
+    near_next = unpack(fetch(packed, 1, 0), *shapes)
+    near = fold(near_last, near_next)
+    far = fold(far_last, far_next)
+    held = jnp.where(even, pack(*near), pack(*far))
     swap = [(2 * c, 2 * c + 1) for c in range(chips)] + [(2 * c + 1, 2 * c) for c in range(chips)]
     other = shifted(held, axis, swap)
     near_gain, near_state = unpack(jnp.where(even, held, other), *shapes)
-    _, far_got = unpack(jnp.where(even, other, held), *shapes)
-    behind = near_gain[..., None, None] * far_got + near_state
+    _, far_state = unpack(jnp.where(even, other, held), *shapes)
+    behind = near_gain[..., None, None] * far_state + near_state
     odd_entering = pair[0][..., None, None] * behind + pair[1]
     return jnp.where(even, behind, odd_entering)
 

time: 121 us -> 114 us (0.942)
  the two profiles are of different devices: /device:TPU:4 before, /device:TPU:2 now
where the time goes in v8:
time: 114 us; the launch traced here: 113 us
  waiting for transfers between devices  37.2 us (33%)
  other arithmetic  21 us (18%)
  blocking collectives  18.5 us (16%)
  starting transfers between devices  16.6 us (15%)
  local copies, waits for them, and re-layouts  13.6 us (12%)
  matrix products  5.78 us (5%)
    ppermute x7, waiting for transfers between devices, shifted(): return lax.ppermute(block, axis, pairs)  34.8 us
    all_to_all x1, blocking collectives, summed_over(): return lax.all_to_all(spread, axis, 0, 0, tiled=False).sum(0)  18.5 us
    ppermute x7, starting transfers between devices, shifted(): return lax.ppermute(block, axis, pairs)  14.7 us
    unnamed x30, local copies, waits for them, and re-layouts  4.76 us
    convert_element_type x2, other arithmetic, causal_conv(): return jax.nn.silu(result).astype(jnp.bfloat16)  3.67 us
    add x4, other arithmetic, fold(): return (gain_e * gain_l, gain_l[..., None, None] * state_e + state_l)  2.94 us
    dot_general x1, matrix products, on_device(): jnp.einsum('cghqs,csghp->cqghp', mixing, x_heads, preferred_element_type=...  2.92 us
    ppermute x1, waiting for transfers between devices, from_behind(): return lax.ppermute(block, axis, route)  2.4 us
  transfers between devices with their start and end apart: 8, of which 4 were waited for; matrix products, arithmetic and copies ran while one was open for 11% of the time, Pallas kernels for 0%

profile of v8, /device:TPU:2, one launch (start us, length us, event | category | flops | bytes accessed | tf_op | source)
XLA Modules:
  0.0 113.2 jit_solution(9771423602808795806)
XLA Ops:
  0.0 0.8 fusion.35
  2.7 1.9 %collective-permute-start = (bf16[3,1408]{0,1:T(8,128)(2,1)S(1)}, bf16[3,1408]{0,1:T(8,128)(2,1)S(1)}, u32[]{:S(2)}, u32[]{:S(2)}) collective-permute-start(bf16[3,1408]{0,1:T(8,128)(2,1)S(1)} %copy.91), channel_id=1, source_target_pairs={{0,8},{8,16},{16,24},{24,32},{32,40},{40,48},{48,56},{56,64},{64,7... | collective-permute-start | bytes 25352 | tf_op jit(solution)/shard_map/ppermute | solution.py:13
  6.0 0.9 broadcast_multiply_fusion
  6.9 1.2 %reduce-window.6 = f32[2,16,2,128]{3,1,2,0:T(8,128)S(1)} reduce-window(f32[2,16,2,128]{3,1,2,0:T(8,128)S(1)} %copy_bitcast_fusion.1, f32[]{:T(128)} %constant.131.clone.1), window={size=1x1x1x128 pad=0_0x0_0x0_0x127_0}, to_apply=%region_0.1 | reduce-window | flops 1040384 | bytes 65540 | tf_op jit(solution)/shard_map/reduce-window
  8.5 0.9 slice_convert_fusion.3
  9.6 1.0 copy.96
  11.1 2.4 %collective-permute-done = bf16[3,1408]{0,1:T(8,128)(2,1)S(1)} collective-permute-done((bf16[3,1408]{0,1:T(8,128)(2,1)S(1)}, bf16[3,1408]{0,1:T(8,128)(2,1)S(1)}, u32[]{:S(2)}, u32[]{:S(2)}) %collective-permute-start) | collective-permute-done | bytes 8480 | tf_op jit(solution)/shard_map/ppermute | solution.py:13
  14.1 0.8 multiply_convert_fusion.8
  15.0 2.8 %multiply_convert_fusion.5 = bf16[512,1024]{0,1:T(8,128)(2,1)S(1)} fusion(bf16[512,1024]{0,1:T(8,128)(2,1)S(1)} %copy.92, bf16[3,1024]{0,1:T(8,128)(2,1)S(1)} %slice.289, f32[1024]{0:T(1024)S(1)} %bitcast.165, f32[1024]{0:T(1024)S(1)} %bitcast.166, f32[1024]{0:T(1024)S(1)} %bitcast.164, f32[1024]{0:T(1024)S(1)} %bitcast.163, f32[1024]{0:T(1024)S(1)} %copy-done.8, ...), kind=kLoop, calls=%fused_computation.24 | loop fusion | flops 15728640 | bytes 2125824 | tf_op jit(solution)/shard_map/convert_element_type | solution.py:88
  18.2 1.7 %fusion.11 = f32[2,16,64,128]{3,2,1,0:T(8,128)S(1)} fusion(f32[2,16,256]{2,1,0:T(8,128)S(1)} %fusion.28, f32[2,256,128]{2,1,0:T(8,128)S(1)} %convert_element_type.130, bf16[2,256,16,64]{1,0,3,2:T(2,128)(2,1)S(1)} %reshape.604), kind=kOutput, calls=%fused_computation.15 | convolution fusion | flops 136314880 | bytes 2392064 | tf_op jit(solution)/shard_map/cghsn,csghp->cghpn/dot_general | solution.py:157
  20.1 1.3 %collective-permute-start.1 = (f32[1032,128]{1,0:T(8,128)S(1)}, f32[1032,128]{1,0:T(8,128)S(1)}, u32[]{:S(2)}, u32[]{:S(2)}) collective-permute-start(f32[1032,128]{1,0:T(8,128)S(1)} %select_maximum_fusion.4), channel_id=1, source_target_pairs={{0,8},{16,24},{32,40},{48,56},{64,72},{80,88},{96,104},{112,120},{... | collective-permute-start | bytes 1585160 | tf_op jit(solution)/shard_map/ppermute | solution.py:17
  21.5 1.5 %collective-permute-done.1 = f32[1032,128]{1,0:T(8,128)S(1)} collective-permute-done((f32[1032,128]{1,0:T(8,128)S(1)}, f32[1032,128]{1,0:T(8,128)S(1)}, u32[]{:S(2)}, u32[]{:S(2)}) %collective-permute-start.1) | collective-permute-done | bytes 528416 | tf_op jit(solution)/shard_map/ppermute | solution.py:17
  24.2 1.3 %collective-permute-start.3 = (f32[1032,128]{1,0:T(8,128)S(1)}, f32[1032,128]{1,0:T(8,128)S(1)}, u32[]{:S(2)}, u32[]{:S(2)}) collective-permute-start(f32[1032,128]{1,0:T(8,128)S(1)} %select_maximum_fusion.2), channel_id=1, source_target_pairs={{8,16},{24,32},{40,48},{56,64},{72,80},{88,96},{104,112},{120,128}... | collective-permute-start | bytes 1585160 | tf_op jit(solution)/shard_map/ppermute | solution.py:17
  25.5 1.3 %collective-permute-start.4 = (f32[1032,128]{1,0:T(8,128)S(1)}, f32[1032,128]{1,0:T(8,128)}, u32[]{:S(2)}, u32[]{:S(2)}) collective-permute-start(f32[1032,128]{1,0:T(8,128)S(1)} %select_maximum_fusion.2), channel_id=1, source_target_pairs={{8,48},{24,64},{40,80},{56,96},{72,112},{88,128},{104,144},{120,16... | collective-permute-start | bytes 1585160 | tf_op jit(solution)/shard_map/ppermute | solution.py:17
  26.8 1.5 %collective-permute-start.5 = (f32[1032,128]{1,0:T(8,128)S(1)}, f32[1032,128]{1,0:T(8,128)}, u32[]{:S(2)}, u32[]{:S(2)}) collective-permute-start(f32[1032,128]{1,0:T(8,128)S(1)} %select_maximum_fusion.2), channel_id=1, source_target_pairs={{8,88},{24,104},{40,120},{56,136},{72,152},{88,168},{104,184},{120... | collective-permute-start | bytes 1585160 | tf_op jit(solution)/shard_map/ppermute | solution.py:17
  28.2 1.4 %collective-permute-start.6 = (f32[1032,128]{1,0:T(8,128)S(1)}, f32[1032,128]{1,0:T(8,128)}, u32[]{:S(2)}, u32[]{:S(2)}) collective-permute-start(f32[1032,128]{1,0:T(8,128)S(1)} %select_maximum_fusion.2), channel_id=1, source_target_pairs={{8,120},{24,136},{40,152},{56,168},{72,184},{88,200},{104,216},{12... | collective-permute-start | bytes 1585160 | tf_op jit(solution)/shard_map/ppermute | solution.py:17
  29.7 14.3 %collective-permute-done.3 = f32[1032,128]{1,0:T(8,128)S(1)} collective-permute-done((f32[1032,128]{1,0:T(8,128)S(1)}, f32[1032,128]{1,0:T(8,128)S(1)}, u32[]{:S(2)}, u32[]{:S(2)}) %collective-permute-start.3) | collective-permute-done | bytes 528416 | tf_op jit(solution)/shard_map/ppermute | solution.py:17
  44.1 19.0 %collective-permute-done.4 = f32[1032,128]{1,0:T(8,128)} collective-permute-done((f32[1032,128]{1,0:T(8,128)S(1)}, f32[1032,128]{1,0:T(8,128)}, u32[]{:S(2)}, u32[]{:S(2)}) %collective-permute-start.4) | collective-permute-done | bytes 528416 | tf_op jit(solution)/shard_map/ppermute | solution.py:17
  64.8 1.2 %slice_add_fusion.1 = f32[1024,128]{1,0:T(8,128)S(1)} fusion(f32[1032,128]{1,0:T(8,128)S(1)} %collective-permute-done.3, f32[1032,128]{1,0:T(8,128)} %collective-permute-done.4, f32[1024]{0:T(1024)S(1)} %mul.520), kind=kLoop, calls=%fused_computation.48 | loop fusion | flops 262144 | bytes 1576960 | tf_op jit(solution)/shard_map/add | solution.py:23
  66.0 1.4 %slice_add_fusion = f32[1024,128]{1,0:T(8,128)S(1)} fusion(f32[1032,128]{1,0:T(8,128)} %collective-permute-done.5, f32[1032,128]{1,0:T(8,128)} %collective-permute-done.6, f32[1024]{0:T(1024)S(1)} %mul.526), kind=kLoop, calls=%fused_computation.46 | loop fusion | flops 262144 | bytes 1576960 | tf_op jit(solution)/shard_map/add | solution.py:23
  67.4 0.9 fusion.23
  68.3 7.2 %collective-permute-start.7 = (f32[1032,128]{1,0:T(8,128)}, f32[1032,128]{1,0:T(8,128)}, u32[]{:S(2)}, u32[]{:S(2)}) collective-permute-start(f32[1032,128]{1,0:T(8,128)} %fusion.23), channel_id=1, source_target_pairs={{0,8},{16,24},{32,40},{48,56},{64,72},{80,88},{96,104},{112,120},{... | collective-permute-start | bytes 1585160 | tf_op jit(solution)/shard_map/ppermute | solution.py:17
  76.3 1.5 %copy.106 = bf16[512,1024]{0,1:T(8,128)(2,1)S(1)} copy(bf16[512,1024]{1,0:T(8,128)(2,1)} %param.25) | data formatting | bytes 2097152 | tf_op args[2]
  77.8 2.3 %reshape.634 = f32[2,256,1,16,64]{1,0,4,3,2:T(2,128)} reshape(bf16[512,1024]{0,1:T(8,128)(2,1)S(1)} %multiply_convert_fusion.5) | data formatting | bytes 3145728 | tf_op jit(solution)/shard_map/convert_element_type | solution.py:186
  80.4 1.2 %broadcast_select_fusion = f32[1032,128]{1,0:T(8,128)S(1)} fusion(f32[1032,128]{1,0:T(8,128)} %fusion.23, f32[1032,128]{1,0:T(8,128)} %collective-permute-done.7, pred[]{:T(512)S(6)} %eq.75), kind=kLoop, calls=%fused_computation.59 | loop fusion | flops 132096 | bytes 1585153 | tf_op jit(solution)/shard_map/jit(_where)/select_n | solution.py:66
  81.7 1.3 %slice_select_fusion = f32[1024,128]{1,0:T(8,128)S(1)} fusion(f32[1032,128]{1,0:T(8,128)} %fusion.23, f32[1032,128]{1,0:T(8,128)} %collective-permute-done.7, pred[]{:T(512)S(6)} %eq.75), kind=kLoop, calls=%fused_computation.45 | loop fusion | flops 131072 | bytes 1572865 | tf_op jit(solution)/shard_map/jit(_where)/select_n | solution.py:67
  83.4 1.0 fusion.18
  85.2 2.9 %fusion.13 = f32[2,256,1,16,64]{1,4,3,0,2:T(8,128)S(1)} fusion(f32[2,16,64,256]{3,2,1,0:T(8,128)S(1)} %fusion.18, f32[2,256,1,16,64]{1,0,4,3,2:T(2,128)S(1)} %copy-done.2, f32[2,16,256]{2,1,0:T(8,128)S(1)} %bitcast.162, f32[2,16,256]{2,1,0:T(8,128)S(1)} %get-tuple-element.77, f32[2,256,256]{2,1,0:T(8,128)S(1)} %fusion.36, ...), kind=kOutput, calls=%fused_computation.18 | convolution fusion | flops 283115520 | bytes 8093760 | tf_op jit(solution)/shard_map/cghqs,csghp->cqghp/dot_general | solution.py:151
  88.2 1.6 %copy.105 = f32[2,256,1,16,64]{1,0,4,3,2:T(2,128)S(1)} copy(f32[2,256,1,16,64]{1,4,3,0,2:T(8,128)S(1)} %fusion.13) | data formatting | bytes 4194304 | tf_op jit(solution)/shard_map/add | solution.py:186
  90.7 18.5 %all_to_all.6 = f32[8,1,512]{2,1,0:T(1,128)S(1)} all-to-all(f32[8,1,512]{2,1,0:T(1,128)S(1)} %broadcast_in_dim.142), channel_id=1, replica_groups=mesh['seq'=64,'tp'=8] {'tp'}, dimensions={0} | all-to-all | bytes 32768 | tf_op jit(solution)/shard_map/all_to_all | solution.py:76
  109.3 1.7 %multiply_convert_fusion.4 = bf16[512,1024]{0,1:T(8,128)(2,1)} fusion(f32[1024]{0:T(1024)S(1)} %copy-done.9, f32[512]{0:T(512)S(1)} %add_rsqrt_fusion, f32[512,1024]{0,1:T(8,128)S(1)} %bitcast.143, bf16[512,1024]{0,1:T(8,128)(2,1)S(1)} %copy.106), kind=kLoop, calls=%fused_computation.20 | loop fusion | flops 4718592 | bytes 4200448 | tf_op jit(solution)/shard_map/convert_element_type | solution.py:190
  111.0 2.3 %copy.108 = bf16[512,1024]{1,0:T(8,128)(2,1)} copy(bf16[512,1024]{0,1:T(8,128)(2,1)} %multiply_convert_fusion.4) | data formatting | bytes 2097152 | tf_op jit(solution)/shard_map/convert_element_type | solution.py:190
  (94 shorter events, 11.8 us)
Async XLA Ops:
  0.0 13.6 %copy-start.7 = (s32[512]{0:T(512)S(1)}, s32[512]{0:T(512)}, u32[]{:S(2)}) copy-start(s32[512]{0:T(512)} %param.35) | copy-start | bytes 6148
  0.0 10.5 %copy-start.3 = (bf16[512,1024]{1,0:T(8,128)(2,1)S(1)}, bf16[512,1024]{1,0:T(8,128)(2,1)}, u32[]{:S(2)}) copy-start(bf16[512,1024]{1,0:T(8,128)(2,1)} %param.23) | copy-start | bytes 3145732
  0.0 14.1 %copy-start.10 = (f32[2,128]{1,0:T(2,128)S(1)}, f32[2,128]{1,0:T(2,128)}, u32[]{:S(2)}) copy-start(f32[2,128]{1,0:T(2,128)} %param.30) | copy-start | bytes 3076
  2.7 10.9 %collective-permute-start = (bf16[3,1408]{0,1:T(8,128)(2,1)S(1)}, bf16[3,1408]{0,1:T(8,128)(2,1)S(1)}, u32[]{:S(2)}, u32[]{:S(2)}) collective-permute-start(bf16[3,1408]{0,1:T(8,128)(2,1)S(1)} %copy.91), channel_id=1, source_target_pairs={{0,8},{8,16},{16,24},{24,32},{32,40},{40,48},{48,56},{56,64},{64,7... | collective-permute-start | bytes 25352 | tf_op jit(solution)/shard_map/ppermute | solution.py:13
  10.6 4.4 %copy-start.8 = (f32[1024]{0:T(1024)S(1)}, f32[1024]{0:T(1024)}, u32[]{:S(2)}) copy-start(f32[1024]{0:T(1024)} %param.29) | copy-start | bytes 12292
  18.1 1.9 %copy-start.4 = (bf16[2,256,16,64]{1,0,3,2:T(2,128)(2,1)}, bf16[2,256,16,64]{1,0,3,2:T(2,128)(2,1)S(1)}, u32[]{:S(2)}) copy-start(bf16[2,256,16,64]{1,0,3,2:T(2,128)(2,1)S(1)} %reshape.604) | copy-start | bytes 3145732
  19.9 3.3 %copy-start = (f32[2,16,64,128]{3,2,1,0:T(8,128)}, f32[2,16,64,128]{3,2,1,0:T(8,128)S(1)}, u32[]{:S(2)}) copy-start(f32[2,16,64,128]{3,2,1,0:T(8,128)S(1)} %fusion.11) | copy-start | bytes 3145732
  20.1 2.8 %collective-permute-start.1 = (f32[1032,128]{1,0:T(8,128)S(1)}, f32[1032,128]{1,0:T(8,128)S(1)}, u32[]{:S(2)}, u32[]{:S(2)}) collective-permute-start(f32[1032,128]{1,0:T(8,128)S(1)} %select_maximum_fusion.4), channel_id=1, source_target_pairs={{0,8},{16,24},{32,40},{48,56},{64,72},{80,88},{96,104},{112,120},{... | collective-permute-start | bytes 1585160 | tf_op jit(solution)/shard_map/ppermute | solution.py:17
  23.2 0.7 collective-permute-start.2
  24.2 19.9 %collective-permute-start.3 = (f32[1032,128]{1,0:T(8,128)S(1)}, f32[1032,128]{1,0:T(8,128)S(1)}, u32[]{:S(2)}, u32[]{:S(2)}) collective-permute-start(f32[1032,128]{1,0:T(8,128)S(1)} %select_maximum_fusion.2), channel_id=1, source_target_pairs={{8,16},{24,32},{40,48},{56,64},{72,80},{88,96},{104,112},{120,128}... | collective-permute-start | bytes 1585160 | tf_op jit(solution)/shard_map/ppermute | solution.py:17
  25.5 37.6 %collective-permute-start.4 = (f32[1032,128]{1,0:T(8,128)S(1)}, f32[1032,128]{1,0:T(8,128)}, u32[]{:S(2)}, u32[]{:S(2)}) collective-permute-start(f32[1032,128]{1,0:T(8,128)S(1)} %select_maximum_fusion.2), channel_id=1, source_target_pairs={{8,48},{24,64},{40,80},{56,96},{72,112},{88,128},{104,144},{120,16... | collective-permute-start | bytes 1585160 | tf_op jit(solution)/shard_map/ppermute | solution.py:17
  26.8 37.1 %collective-permute-start.5 = (f32[1032,128]{1,0:T(8,128)S(1)}, f32[1032,128]{1,0:T(8,128)}, u32[]{:S(2)}, u32[]{:S(2)}) collective-permute-start(f32[1032,128]{1,0:T(8,128)S(1)} %select_maximum_fusion.2), channel_id=1, source_target_pairs={{8,88},{24,104},{40,120},{56,136},{72,152},{88,168},{104,184},{120... | collective-permute-start | bytes 1585160 | tf_op jit(solution)/shard_map/ppermute | solution.py:17
  28.2 35.6 %collective-permute-start.6 = (f32[1032,128]{1,0:T(8,128)S(1)}, f32[1032,128]{1,0:T(8,128)}, u32[]{:S(2)}, u32[]{:S(2)}) collective-permute-start(f32[1032,128]{1,0:T(8,128)S(1)} %select_maximum_fusion.2), channel_id=1, source_target_pairs={{8,120},{24,136},{40,152},{56,168},{72,184},{88,200},{104,216},{12... | collective-permute-start | bytes 1585160 | tf_op jit(solution)/shard_map/ppermute | solution.py:17
  68.3 12.2 %collective-permute-start.7 = (f32[1032,128]{1,0:T(8,128)}, f32[1032,128]{1,0:T(8,128)}, u32[]{:S(2)}, u32[]{:S(2)}) collective-permute-start(f32[1032,128]{1,0:T(8,128)} %fusion.23), channel_id=1, source_target_pairs={{0,8},{16,24},{32,40},{48,56},{64,72},{80,88},{96,104},{112,120},{... | collective-permute-start | bytes 1585160 | tf_op jit(solution)/shard_map/ppermute | solution.py:17
  80.4 2.5 %copy-start.1 = (f32[2,16,64,128]{3,2,1,0:T(8,128)S(1)}, f32[2,16,64,128]{3,2,1,0:T(8,128)}, u32[]{:S(2)}) copy-start(f32[2,16,64,128]{3,2,1,0:T(8,128)} %copy-done) | copy-start | bytes 3145732
  83.4 1.6 %copy-start.2 = (f32[2,256,1,16,64]{1,0,4,3,2:T(2,128)S(1)}, f32[2,256,1,16,64]{1,0,4,3,2:T(2,128)}, u32[]{:S(2)}) copy-start(f32[2,256,1,16,64]{1,0,4,3,2:T(2,128)} %reshape.634) | copy-start | bytes 6291460
  83.4 1.8 %copy-start.5 = (bf16[2,256,16,64]{1,0,3,2:T(2,128)(2,1)S(1)}, bf16[2,256,16,64]{1,0,3,2:T(2,128)(2,1)}, u32[]{:S(2)}) copy-start(bf16[2,256,16,64]{1,0,3,2:T(2,128)(2,1)} %copy-done.4) | copy-start | bytes 3145732
  83.4 1.8 %copy-start.6 = (pred[2,256,256]{2,1,0:T(8,128)(4,1)S(1)}, pred[2,256,256]{2,1,0:T(8,128)(4,1)}, u32[]{:S(2)}) copy-start(pred[2,256,256]{2,1,0:T(8,128)(4,1)} %compare_and_fusion) | copy-start | bytes 393220
  83.4 1.8 %copy-start.11 = (f32[16]{0:T(128)S(1)}, f32[16]{0:T(128)}, u32[]{:S(2)}) copy-start(f32[16]{0:T(128)} %param.33) | copy-start | bytes 196
  90.0 19.3 %copy-start.9 = (f32[1024]{0:T(1024)S(1)}, f32[1024]{0:T(1024)}, u32[]{:S(2)}) copy-start(f32[1024]{0:T(1024)} %param.34) | copy-start | bytes 12292

commit v9 on v8

--- a/solution.py
+++ b/solution.py
@@ -38,7 +38,7 @@
     return (packed[rows, :count].reshape(gain_shape), packed[:rows].reshape(state_shape))
 
 
-def entering_state(gain, state, axis):
+def entering_state(gain, state, axis, ride):
     count = lax.axis_size(axis)
     chips = count // 2
     shapes = (gain.shape, state.shape)
@@ -58,6 +58,7 @@
     far_next = unpack(fetch(packed, 5, 1), *shapes)
     near_last = unpack(fetch(packed, 3, 0), *shapes)
     near_next = unpack(fetch(packed, 1, 0), *shapes)
+    near_next, ride = lax.optimization_barrier((near_next, ride))
     near = fold(near_last, near_next)
     far = fold(far_last, far_next)
     held = jnp.where(even, pack(*near), pack(*far))
@@ -67,7 +68,7 @@
     _, far_state = unpack(jnp.where(even, other, held), *shapes)
     behind = near_gain[..., None, None] * far_state + near_state
     odd_entering = pair[0][..., None, None] * behind + pair[1]
-    return jnp.where(even, behind, odd_entering)
+    return jnp.where(even, behind, odd_entering), ride
 
 
 def summed_over(value, axis):
@@ -178,12 +179,13 @@
     empty = jnp.zeros((groups_local, heads_group, head_size, state_size), jnp.float32)
     zero_states, summary = recur(empty)
     device_gain = carry_gain[0] * carry_gain[1]
-    entering = entering_state(device_gain, summary, "seq")
+    skip = d_skip.reshape(groups_local, heads_group)[..., None]
+    base = y_intra + skip * x_heads.astype(jnp.float32)
+    entering, base = entering_state(device_gain, summary, "seq", base)
     states, _ = recur(entering)
     product = jnp.einsum("cqgn,cghpn->cqghp", c_float, states, precision=lax.Precision.HIGHEST)
     y_inter = product * link.transpose(0, 3, 1, 2)[..., None]
-    skip = d_skip.reshape(groups_local, heads_group)[..., None]
-    mixed = y_intra + y_inter + skip * x_heads.astype(jnp.float32)
+    mixed = base + y_inter
     gated = mixed.reshape(tok_rows, inner_local) * jax.nn.silu(z_proj.astype(jnp.float32))
     squares = summed_over(jnp.sum(gated * gated, axis=-1), "tp")
     scale = lax.rsqrt(squares / (inner_local * lax.axis_size("tp")) + 1e-05)

time: 114 us -> 106 us (0.930)
  the two profiles are of different devices: /device:TPU:2 before, /device:TPU:6 now
where the time goes in v9:
time: 106 us; the launch traced here: 105 us
  waiting for transfers between devices  32.1 us (30%)
  blocking collectives  17.9 us (17%)
  other arithmetic  17 us (16%)
  local copies, waits for them, and re-layouts  16.3 us (15%)
  starting transfers between devices  13.7 us (13%)
  matrix products  7.14 us (7%)
    ppermute x7, waiting for transfers between devices, shifted(): return lax.ppermute(block, axis, pairs)  29.7 us
    all_to_all x1, blocking collectives, summed_over(): return lax.all_to_all(spread, axis, 0, 0, tiled=False).sum(0)  17.9 us
    ppermute x7, starting transfers between devices, shifted(): return lax.ppermute(block, axis, pairs)  11.8 us
    unnamed x36, local copies, waits for them, and re-layouts  5.33 us
    dot_general x1, matrix products, on_device(): jnp.einsum('cghqs,csghp->cqghp', mixing, x_heads, preferred_element_type=...  4.25 us
    convert_element_type x2, other arithmetic, causal_conv(): return jax.nn.silu(result).astype(jnp.bfloat16)  3.67 us
    slice x5, local copies, waits for them, and re-layouts, unpack(): packed[:rows].reshape(state_shape)  2.41 us
    ppermute x1, waiting for transfers between devices, from_behind(): return lax.ppermute(block, axis, route)  2.4 us
  transfers between devices with their start and end apart: 8, of which 4 were waited for; matrix products, arithmetic and copies ran while one was open for 15% of the time, Pallas kernels for 0%

profile of v9, /device:TPU:6, one launch (start us, length us, event | category | flops | bytes accessed | tf_op | source)
XLA Modules:
  0.0 104.8 jit_solution(15785840343137182225)
XLA Ops:
  0.0 0.8 fusion.34
  1.6 0.7 slice.243
  2.7 1.9 %collective-permute-start = (bf16[3,1408]{0,1:T(8,128)(2,1)S(1)}, bf16[3,1408]{0,1:T(8,128)(2,1)S(1)}, u32[]{:S(2)}, u32[]{:S(2)}) collective-permute-start(bf16[3,1408]{0,1:T(8,128)(2,1)S(1)} %copy.94), channel_id=1, source_target_pairs={{0,8},{8,16},{16,24},{24,32},{32,40},{40,48},{48,56},{56,64},{64,7... | collective-permute-start | bytes 25352 | tf_op jit(solution)/shard_map/ppermute | solution.py:13
  5.3 0.9 broadcast_multiply_fusion
  6.2 1.2 %reduce-window.6 = f32[2,16,2,128]{3,1,2,0:T(8,128)S(1)} reduce-window(f32[2,16,2,128]{3,1,2,0:T(8,128)S(1)} %copy_bitcast_fusion.1, f32[]{:T(128)} %constant.131.clone.1), window={size=1x1x1x128 pad=0_0x0_0x0_0x127_0}, to_apply=%region_0.1 | reduce-window | flops 1040384 | bytes 65540 | tf_op jit(solution)/shard_map/reduce-window
  8.5 0.9 slice_convert_fusion.3
  9.6 1.0 copy.99
  11.1 2.4 %collective-permute-done = bf16[3,1408]{0,1:T(8,128)(2,1)S(1)} collective-permute-done((bf16[3,1408]{0,1:T(8,128)(2,1)S(1)}, bf16[3,1408]{0,1:T(8,128)(2,1)S(1)}, u32[]{:S(2)}, u32[]{:S(2)}) %collective-permute-start) | collective-permute-done | bytes 8480 | tf_op jit(solution)/shard_map/ppermute | solution.py:13
  14.1 0.8 multiply_convert_fusion.8
  14.9 0.7 convert_element_type.129
  15.7 2.8 %multiply_convert_fusion.5 = bf16[512,1024]{0,1:T(8,128)(2,1)S(1)} fusion(bf16[512,1024]{0,1:T(8,128)(2,1)S(1)} %copy.95, bf16[3,1024]{0,1:T(8,128)(2,1)S(1)} %slice.293, f32[1024]{0:T(1024)S(1)} %bitcast.168, f32[1024]{0:T(1024)S(1)} %bitcast.169, f32[1024]{0:T(1024)S(1)} %bitcast.167, f32[1024]{0:T(1024)S(1)} %bitcast.166, f32[1024]{0:T(1024)S(1)} %copy-done.11, ...), kind=kLoop, calls=%fused_computation.24 | loop fusion | flops 15728640 | bytes 2125824 | tf_op jit(solution)/shard_map/convert_element_type | solution.py:89
  19.0 1.7 %fusion.11 = f32[2,16,64,128]{3,2,1,0:T(8,128)S(1)} fusion(f32[2,16,256]{2,1,0:T(8,128)S(1)} %fusion.26, f32[2,256,128]{2,1,0:T(8,128)S(1)} %copy-done.9, bf16[2,256,16,64]{1,0,3,2:T(2,128)(2,1)S(1)} %reshape.620), kind=kOutput, calls=%fused_computation.15 | convolution fusion | flops 136314880 | bytes 2392064 | tf_op jit(solution)/shard_map/cghsn,csghp->cghpn/dot_general | solution.py:158
  20.8 1.3 %collective-permute-start.1 = (f32[1032,128]{1,0:T(8,128)S(1)}, f32[1032,128]{1,0:T(8,128)S(1)}, u32[]{:S(2)}, u32[]{:S(2)}) collective-permute-start(f32[1032,128]{1,0:T(8,128)S(1)} %select_maximum_fusion.4), channel_id=1, source_target_pairs={{0,8},{16,24},{32,40},{48,56},{64,72},{80,88},{96,104},{112,120},{... | collective-permute-start | bytes 1585160 | tf_op jit(solution)/shard_map/ppermute | solution.py:17
  22.2 1.5 %collective-permute-done.1 = f32[1032,128]{1,0:T(8,128)S(1)} collective-permute-done((f32[1032,128]{1,0:T(8,128)S(1)}, f32[1032,128]{1,0:T(8,128)S(1)}, u32[]{:S(2)}, u32[]{:S(2)}) %collective-permute-start.1) | collective-permute-done | bytes 528416 | tf_op jit(solution)/shard_map/ppermute | solution.py:17
  24.0 1.5 %collective-permute-start.2 = (f32[1032,128]{1,0:T(8,128)S(1)}, f32[1032,128]{1,0:T(8,128)}, u32[]{:S(2)}, u32[]{:S(2)}) collective-permute-start(f32[1032,128]{1,0:T(8,128)S(1)} %select_maximum_fusion.3), channel_id=1, source_target_pairs={{8,24},{24,40},{40,56},{56,72},{72,88},{88,104},{104,120},{120,136... | collective-permute-start | bytes 1585160 | tf_op jit(solution)/shard_map/ppermute | solution.py:17
  25.7 2.3 %reshape.648 = f32[2,256,1,16,64]{1,0,4,3,2:T(2,128)} reshape(bf16[512,1024]{0,1:T(8,128)(2,1)S(1)} %multiply_convert_fusion.5) | data formatting | bytes 3145728 | tf_op jit(solution)/shard_map/convert_element_type | solution.py:183
  28.2 1.2 %slice.308 = f32[1024,128]{1,0:T(8,128)S(1)} slice(f32[1032,128]{1,0:T(8,128)} %collective-permute-done.2), slice={[0:1024], [0:128]} | slice | bytes 1048576 | tf_op jit(solution)/shard_map/slice | solution.py:38
  30.3 1.3 %collective-permute-start.3 = (f32[1032,128]{1,0:T(8,128)S(1)}, f32[1032,128]{1,0:T(8,128)S(1)}, u32[]{:S(2)}, u32[]{:S(2)}) collective-permute-start(f32[1032,128]{1,0:T(8,128)S(1)} %select_maximum_fusion.2), channel_id=1, source_target_pairs={{8,16},{24,32},{40,48},{56,64},{72,80},{88,96},{104,112},{120,128}... | collective-permute-start | bytes 1585160 | tf_op jit(solution)/shard_map/ppermute | solution.py:17
  33.0 1.3 %collective-permute-start.4 = (f32[1032,128]{1,0:T(8,128)S(1)}, f32[1032,128]{1,0:T(8,128)}, u32[]{:S(2)}, u32[]{:S(2)}) collective-permute-start(f32[1032,128]{1,0:T(8,128)S(1)} %select_maximum_fusion.2), channel_id=1, source_target_pairs={{8,48},{24,64},{40,80},{56,96},{72,112},{88,128},{104,144},{120,16... | collective-permute-start | bytes 1585160 | tf_op jit(solution)/shard_map/ppermute | solution.py:17
  34.3 4.3 %bitcast_add_fusion = f32[2,256,1,16,64]{1,4,3,0,2:T(8,128)} fusion(f32[2,256,1,16,64]{1,0,4,3,2:T(2,128)S(1)} %copy-done.3, f32[2,16,256]{2,1,0:T(8,128)S(1)} %bitcast.165, f32[2,16,256]{2,1,0:T(8,128)S(1)} %get-tuple-element.81, f32[2,256,256]{2,1,0:T(8,128)S(1)} %fusion.35, pred[2,256,256]{2,1,0:T(8,128)(4,1)S(1)} %compare_and_fusion, ...), kind=kOutput, calls=%fused_computation.18 | convolution fusion | flops 282066944 | bytes 5963840 | tf_op jit(solution)/shard_map/cghqs,csghp->cqghp/dot_general | solution.py:152
  38.6 8.0 %collective-permute-done.3 = f32[1032,128]{1,0:T(8,128)S(1)} collective-permute-done((f32[1032,128]{1,0:T(8,128)S(1)}, f32[1032,128]{1,0:T(8,128)S(1)}, u32[]{:S(2)}, u32[]{:S(2)}) %collective-permute-start.3) | collective-permute-done | bytes 528416 | tf_op jit(solution)/shard_map/ppermute | solution.py:17
  46.7 0.8 copy-done.7
  47.6 20.2 %collective-permute-done.4 = f32[1032,128]{1,0:T(8,128)} collective-permute-done((f32[1032,128]{1,0:T(8,128)S(1)}, f32[1032,128]{1,0:T(8,128)}, u32[]{:S(2)}, u32[]{:S(2)}) %collective-permute-start.4) | collective-permute-done | bytes 528416 | tf_op jit(solution)/shard_map/ppermute | solution.py:17
  67.8 1.1 %slice.313 = f32[1024,128]{1,0:T(8,128)S(1)} slice(f32[1032,128]{1,0:T(8,128)} %collective-permute-done.4), slice={[0:1024], [0:128]} | slice | bytes 1048576 | tf_op jit(solution)/shard_map/slice | solution.py:38
  69.9 5.0 %collective-permute-start.7 = (f32[1032,128]{1,0:T(8,128)S(1)}, f32[1032,128]{1,0:T(8,128)}, u32[]{:S(2)}, u32[]{:S(2)}) collective-permute-start(f32[1032,128]{1,0:T(8,128)S(1)} %fusion.22), channel_id=1, source_target_pairs={{0,8},{16,24},{32,40},{48,56},{64,72},{80,88},{96,104},{112,120},{... | collective-permute-start | bytes 1585160 | tf_op jit(solution)/shard_map/ppermute | solution.py:17
  75.0 1.5 %copy.106 = bf16[512,1024]{0,1:T(8,128)(2,1)S(1)} copy(bf16[512,1024]{1,0:T(8,128)(2,1)} %param.25) | data formatting | bytes 2097152 | tf_op args[2]
  76.7 1.2 %slice_select_fusion = f32[1024,128]{1,0:T(8,128)S(1)} fusion(f32[1032,128]{1,0:T(8,128)S(1)} %fusion.22, f32[1032,128]{1,0:T(8,128)} %collective-permute-done.7, pred[]{:T(512)S(6)} %eq.75), kind=kLoop, calls=%fused_computation.45 | loop fusion | flops 131072 | bytes 1572865 | tf_op jit(solution)/shard_map/jit(_where)/select_n | solution.py:68
  78.4 1.0 fusion.17
  80.4 1.6 %copy.105 = f32[2,256,1,16,64]{1,0,4,3,2:T(2,128)S(1)} copy(f32[2,256,1,16,64]{1,4,3,0,2:T(8,128)S(1)} %fusion.12) | data formatting | bytes 4194304 | tf_op jit(solution)/shard_map/add | solution.py:188
  82.9 17.9 %all_to_all.6 = f32[8,1,512]{2,1,0:T(1,128)S(1)} all-to-all(f32[8,1,512]{2,1,0:T(1,128)S(1)} %broadcast_in_dim.143), channel_id=1, replica_groups=mesh['seq'=64,'tp'=8] {'tp'}, dimensions={0} | all-to-all | bytes 32768 | tf_op jit(solution)/shard_map/all_to_all | solution.py:77
  100.9 1.7 %multiply_convert_fusion.4 = bf16[512,1024]{0,1:T(8,128)(2,1)} fusion(f32[1024]{0:T(1024)S(1)} %copy-done.12, f32[512]{0:T(512)S(1)} %add_rsqrt_fusion, f32[512,1024]{0,1:T(8,128)S(1)} %bitcast.143, bf16[512,1024]{0,1:T(8,128)(2,1)S(1)} %copy.106), kind=kLoop, calls=%fused_computation.20 | loop fusion | flops 4718592 | bytes 4200448 | tf_op jit(solution)/shard_map/convert_element_type | solution.py:192
  102.6 2.3 %copy.108 = bf16[512,1024]{1,0:T(8,128)(2,1)} copy(bf16[512,1024]{0,1:T(8,128)(2,1)} %multiply_convert_fusion.4) | data formatting | bytes 2097152 | tf_op jit(solution)/shard_map/convert_element_type | solution.py:192
  (102 shorter events, 11.6 us)
Async XLA Ops:
  0.0 13.8 %copy-start.10 = (s32[512]{0:T(512)S(1)}, s32[512]{0:T(512)}, u32[]{:S(2)}) copy-start(s32[512]{0:T(512)} %param.35) | copy-start | bytes 6148
  0.0 10.5 %copy-start.4 = (bf16[512,1024]{1,0:T(8,128)(2,1)S(1)}, bf16[512,1024]{1,0:T(8,128)(2,1)}, u32[]{:S(2)}) copy-start(bf16[512,1024]{1,0:T(8,128)(2,1)} %param.23) | copy-start | bytes 3145732
  0.0 14.1 %copy-start.13 = (f32[2,128]{1,0:T(2,128)S(1)}, f32[2,128]{1,0:T(2,128)}, u32[]{:S(2)}) copy-start(f32[2,128]{1,0:T(2,128)} %param.30) | copy-start | bytes 3076
  2.7 10.9 %collective-permute-start = (bf16[3,1408]{0,1:T(8,128)(2,1)S(1)}, bf16[3,1408]{0,1:T(8,128)(2,1)S(1)}, u32[]{:S(2)}, u32[]{:S(2)}) collective-permute-start(bf16[3,1408]{0,1:T(8,128)(2,1)S(1)} %copy.94), channel_id=1, source_target_pairs={{0,8},{8,16},{16,24},{24,32},{32,40},{40,48},{48,56},{56,64},{64,7... | collective-permute-start | bytes 25352 | tf_op jit(solution)/shard_map/ppermute | solution.py:13
  10.6 5.1 %copy-start.11 = (f32[1024]{0:T(1024)S(1)}, f32[1024]{0:T(1024)}, u32[]{:S(2)}) copy-start(f32[1024]{0:T(1024)} %param.29) | copy-start | bytes 12292
  15.7 3.3 %copy-start.9 = (f32[2,256,128]{2,1,0:T(8,128)S(1)}, f32[2,256,128]{2,1,0:T(8,128)}, u32[]{:S(2)}) copy-start(f32[2,256,128]{2,1,0:T(8,128)} %convert_element_type.129) | copy-start | bytes 786436
  18.8 1.9 %copy-start.5 = (bf16[2,256,16,64]{1,0,3,2:T(2,128)(2,1)}, bf16[2,256,16,64]{1,0,3,2:T(2,128)(2,1)S(1)}, u32[]{:S(2)}) copy-start(bf16[2,256,16,64]{1,0,3,2:T(2,128)(2,1)S(1)} %reshape.620) | copy-start | bytes 3145732
  20.6 3.3 %copy-start = (f32[2,16,64,128]{3,2,1,0:T(8,128)}, f32[2,16,64,128]{3,2,1,0:T(8,128)S(1)}, u32[]{:S(2)}) copy-start(f32[2,16,64,128]{3,2,1,0:T(8,128)S(1)} %fusion.11) | copy-start | bytes 3145732
  20.8 2.8 %collective-permute-start.1 = (f32[1032,128]{1,0:T(8,128)S(1)}, f32[1032,128]{1,0:T(8,128)S(1)}, u32[]{:S(2)}, u32[]{:S(2)}) collective-permute-start(f32[1032,128]{1,0:T(8,128)S(1)} %select_maximum_fusion.4), channel_id=1, source_target_pairs={{0,8},{16,24},{32,40},{48,56},{64,72},{80,88},{96,104},{112,120},{... | collective-permute-start | bytes 1585160 | tf_op jit(solution)/shard_map/ppermute | solution.py:17
  24.0 4.3 %collective-permute-start.2 = (f32[1032,128]{1,0:T(8,128)S(1)}, f32[1032,128]{1,0:T(8,128)}, u32[]{:S(2)}, u32[]{:S(2)}) collective-permute-start(f32[1032,128]{1,0:T(8,128)S(1)} %select_maximum_fusion.3), channel_id=1, source_target_pairs={{8,24},{24,40},{40,56},{56,72},{72,88},{88,104},{104,120},{120,136... | collective-permute-start | bytes 1585160 | tf_op jit(solution)/shard_map/ppermute | solution.py:17
  28.0 6.3 %copy-start.3 = (f32[2,256,1,16,64]{1,0,4,3,2:T(2,128)S(1)}, f32[2,256,1,16,64]{1,0,4,3,2:T(2,128)}, u32[]{:S(2)}) copy-start(f32[2,256,1,16,64]{1,0,4,3,2:T(2,128)} %reshape.648) | copy-start | bytes 6291460
  28.0 6.3 %copy-start.6 = (bf16[2,256,16,64]{1,0,3,2:T(2,128)(2,1)S(1)}, bf16[2,256,16,64]{1,0,3,2:T(2,128)(2,1)}, u32[]{:S(2)}) copy-start(bf16[2,256,16,64]{1,0,3,2:T(2,128)(2,1)} %copy-done.5) | copy-start | bytes 3145732
  28.0 6.3 %copy-start.14 = (f32[16]{0:T(128)S(1)}, f32[16]{0:T(128)}, u32[]{:S(2)}) copy-start(f32[16]{0:T(128)} %param.33) | copy-start | bytes 196
  30.3 16.3 %collective-permute-start.3 = (f32[1032,128]{1,0:T(8,128)S(1)}, f32[1032,128]{1,0:T(8,128)S(1)}, u32[]{:S(2)}, u32[]{:S(2)}) collective-permute-start(f32[1032,128]{1,0:T(8,128)S(1)} %select_maximum_fusion.2), channel_id=1, source_target_pairs={{8,16},{24,32},{40,48},{56,64},{72,80},{88,96},{104,112},{120,128}... | collective-permute-start | bytes 1585160 | tf_op jit(solution)/shard_map/ppermute | solution.py:17
  31.6 15.0 %collective-permute-start.5 = (f32[1032,128]{1,0:T(8,128)S(1)}, f32[1032,128]{1,0:T(8,128)S(1)}, u32[]{:S(2)}, u32[]{:S(2)}) collective-permute-start(f32[1032,128]{1,0:T(8,128)S(1)} %select_maximum_fusion.2), channel_id=1, source_target_pairs={{8,88},{24,104},{40,120},{56,136},{72,152},{88,168},{104,184},{120... | collective-permute-start | bytes 1585160 | tf_op jit(solution)/shard_map/ppermute | solution.py:17
  32.3 14.3 %collective-permute-start.6 = (f32[1032,128]{1,0:T(8,128)S(1)}, f32[1032,128]{1,0:T(8,128)S(1)}, u32[]{:S(2)}, u32[]{:S(2)}) collective-permute-start(f32[1032,128]{1,0:T(8,128)S(1)} %select_maximum_fusion.2), channel_id=1, source_target_pairs={{8,120},{24,136},{40,152},{56,168},{72,184},{88,200},{104,216},{12... | collective-permute-start | bytes 1585160 | tf_op jit(solution)/shard_map/ppermute | solution.py:17
  33.0 34.8 %collective-permute-start.4 = (f32[1032,128]{1,0:T(8,128)S(1)}, f32[1032,128]{1,0:T(8,128)}, u32[]{:S(2)}, u32[]{:S(2)}) collective-permute-start(f32[1032,128]{1,0:T(8,128)S(1)} %select_maximum_fusion.2), channel_id=1, source_target_pairs={{8,48},{24,64},{40,80},{56,96},{72,112},{88,128},{104,144},{120,16... | collective-permute-start | bytes 1585160 | tf_op jit(solution)/shard_map/ppermute | solution.py:17
  46.6 0.8 copy-start.7
  47.6 22.1 %copy-start.8 = (f32[1032,128]{1,0:T(8,128)S(1)}, f32[1032,128]{1,0:T(8,128)}, u32[]{:S(2)}) copy-start(f32[1032,128]{1,0:T(8,128)} %copy-done.7) | copy-start | bytes 1585156
  69.9 6.7 %collective-permute-start.7 = (f32[1032,128]{1,0:T(8,128)S(1)}, f32[1032,128]{1,0:T(8,128)}, u32[]{:S(2)}, u32[]{:S(2)}) collective-permute-start(f32[1032,128]{1,0:T(8,128)S(1)} %fusion.22), channel_id=1, source_target_pairs={{0,8},{16,24},{32,40},{48,56},{64,72},{80,88},{96,104},{112,120},{... | collective-permute-start | bytes 1585160 | tf_op jit(solution)/shard_map/ppermute | solution.py:17
  76.6 1.4 %copy-start.1 = (f32[2,16,64,128]{3,2,1,0:T(8,128)S(1)}, f32[2,16,64,128]{3,2,1,0:T(8,128)}, u32[]{:S(2)}) copy-start(f32[2,16,64,128]{3,2,1,0:T(8,128)} %copy-done) | copy-start | bytes 3145732
  78.4 1.6 %copy-start.2 = (f32[2,256,1,16,64]{1,4,3,0,2:T(8,128)S(1)}, f32[2,256,1,16,64]{1,4,3,0,2:T(8,128)}, u32[]{:S(2)}) copy-start(f32[2,256,1,16,64]{1,4,3,0,2:T(8,128)} %bitcast_add_fusion) | copy-start | bytes 6291460
  82.2 18.7 %copy-start.12 = (f32[1024]{0:T(1024)S(1)}, f32[1024]{0:T(1024)}, u32[]{:S(2)}) copy-start(f32[1024]{0:T(1024)} %param.34) | copy-start | bytes 12292

commit v10 on v9

--- a/solution.py
+++ b/solution.py
@@ -61,14 +61,19 @@
     near_next, ride = lax.optimization_barrier((near_next, ride))
     near = fold(near_last, near_next)
     far = fold(far_last, far_next)
-    held = jnp.where(even, pack(*near), pack(*far))
+    own = even.astype(jnp.float32)
+    peer = 1.0 - own
+    held = own * pack(*near) + peer * pack(*far)
     swap = [(2 * c, 2 * c + 1) for c in range(chips)] + [(2 * c + 1, 2 * c) for c in range(chips)]
     other = shifted(held, axis, swap)
-    near_gain, near_state = unpack(jnp.where(even, held, other), *shapes)
-    _, far_state = unpack(jnp.where(even, other, held), *shapes)
+    held_gain, held_state = unpack(held, *shapes)
+    other_gain, other_state = unpack(other, *shapes)
+    near_gain = own * held_gain + peer * other_gain
+    near_state = own * held_state + peer * other_state
+    far_state = own * other_state + peer * held_state
     behind = near_gain[..., None, None] * far_state + near_state
     odd_entering = pair[0][..., None, None] * behind + pair[1]
-    return jnp.where(even, behind, odd_entering), ride
+    return own * behind + peer * odd_entering, ride
 
 
 def summed_over(value, axis):

time: 106 us -> 108 us (1.019)
  other arithmetic: 17 us -> 18.7 us
    add x0 -> x3, other arithmetic: none -> 2.37 us  [the longest x1 1.31 us: entering_state(): far_state = own * other_state + peer * held_state]
    select_n x4 -> x0, other arithmetic: 1.47 us -> none  [the longest x1 1.19 us: entering_state(): _, far_state = unpack(jnp.where(even, other, held), *shapes)]
    slice x5 -> x4, local copies, waits for them, and re-layouts: 2.41 us -> 2.37 us  [unpack(): packed[:rows].reshape(state_shape)]
  transfers between devices with their start and end apart: 8 -> 8, of which waited for: 4 -> 5; matrix products, arithmetic and copies ran while one was open for 15% -> 14% of each run, Pallas kernels for 0% -> 0%
where the time goes in v10:
time: 108 us; the launch traced here: 107 us
  waiting for transfers between devices  32.3 us (30%)
  other arithmetic  18.7 us (17%)
  blocking collectives  17.9 us (17%)
  local copies, waits for them, and re-layouts  16.3 us (15%)
  starting transfers between devices  13.8 us (13%)
  matrix products  7.13 us (7%)
    ppermute x7, waiting for transfers between devices, shifted(): return lax.ppermute(block, axis, pairs)  29.9 us
    all_to_all x1, blocking collectives, summed_over(): return lax.all_to_all(spread, axis, 0, 0, tiled=False).sum(0)  17.9 us
    ppermute x7, starting transfers between devices, shifted(): return lax.ppermute(block, axis, pairs)  11.9 us
    unnamed x36, local copies, waits for them, and re-layouts  5.32 us
    dot_general x1, matrix products, on_device(): jnp.einsum('cghqs,csghp->cqghp', mixing, x_heads, preferred_element_type=...  4.25 us
    convert_element_type x2, other arithmetic, causal_conv(): return jax.nn.silu(result).astype(jnp.bfloat16)  3.67 us
    ppermute x1, waiting for transfers between devices, from_behind(): return lax.ppermute(block, axis, route)  2.4 us
    slice x4, local copies, waits for them, and re-layouts, unpack(): packed[:rows].reshape(state_shape)  2.37 us
  transfers between devices with their start and end apart: 8, of which 5 were waited for; matrix products, arithmetic and copies ran while one was open for 14% of the time, Pallas kernels for 0%

profile of v10, /device:TPU:6, one launch (start us, length us, event | category | flops | bytes accessed | tf_op | source)
XLA Modules:
  0.0 106.7 jit_solution(8412548717466937160)
XLA Ops:
  0.0 0.8 fusion.38
  1.6 0.7 slice.246
  2.7 1.9 %collective-permute-start = (bf16[3,1408]{0,1:T(8,128)(2,1)S(1)}, bf16[3,1408]{0,1:T(8,128)(2,1)S(1)}, u32[]{:S(2)}, u32[]{:S(2)}) collective-permute-start(bf16[3,1408]{0,1:T(8,128)(2,1)S(1)} %copy.94), channel_id=1, source_target_pairs={{0,8},{8,16},{16,24},{24,32},{32,40},{40,48},{48,56},{56,64},{64,7... | collective-permute-start | bytes 25352 | tf_op jit(solution)/shard_map/ppermute | solution.py:13
  5.3 0.9 broadcast_multiply_fusion
  6.2 1.2 %reduce-window.6 = f32[2,16,2,128]{3,1,2,0:T(8,128)S(1)} reduce-window(f32[2,16,2,128]{3,1,2,0:T(8,128)S(1)} %copy_bitcast_fusion.1, f32[]{:T(128)} %constant.132.clone.1), window={size=1x1x1x128 pad=0_0x0_0x0_0x127_0}, to_apply=%region_0.1 | reduce-window | flops 1040384 | bytes 65540 | tf_op jit(solution)/shard_map/reduce-window
  8.5 0.9 slice_convert_fusion.3
  9.6 1.0 copy.99
  11.1 2.4 %collective-permute-done = bf16[3,1408]{0,1:T(8,128)(2,1)S(1)} collective-permute-done((bf16[3,1408]{0,1:T(8,128)(2,1)S(1)}, bf16[3,1408]{0,1:T(8,128)(2,1)S(1)}, u32[]{:S(2)}, u32[]{:S(2)}) %collective-permute-start) | collective-permute-done | bytes 8480 | tf_op jit(solution)/shard_map/ppermute | solution.py:13
  14.1 0.8 multiply_convert_fusion.8
  15.7 2.8 %multiply_convert_fusion.5 = bf16[512,1024]{0,1:T(8,128)(2,1)S(1)} fusion(bf16[512,1024]{0,1:T(8,128)(2,1)S(1)} %copy.95, bf16[3,1024]{0,1:T(8,128)(2,1)S(1)} %slice.297, f32[1024]{0:T(1024)S(1)} %bitcast.168, f32[1024]{0:T(1024)S(1)} %bitcast.169, f32[1024]{0:T(1024)S(1)} %bitcast.167, f32[1024]{0:T(1024)S(1)} %bitcast.166, f32[1024]{0:T(1024)S(1)} %copy-done.11, ...), kind=kLoop, calls=%fused_computation.24 | loop fusion | flops 15728640 | bytes 2125824 | tf_op jit(solution)/shard_map/convert_element_type | solution.py:94
  19.0 1.7 %fusion.11 = f32[2,16,64,128]{3,2,1,0:T(8,128)S(1)} fusion(f32[2,16,256]{2,1,0:T(8,128)S(1)} %fusion.28, f32[2,256,128]{2,1,0:T(8,128)S(1)} %copy-done.9, bf16[2,256,16,64]{1,0,3,2:T(2,128)(2,1)S(1)} %reshape.720), kind=kOutput, calls=%fused_computation.15 | convolution fusion | flops 136314880 | bytes 2392064 | tf_op jit(solution)/shard_map/cghsn,csghp->cghpn/dot_general | solution.py:163
  20.8 1.3 %collective-permute-start.1 = (f32[1032,128]{1,0:T(8,128)S(1)}, f32[1032,128]{1,0:T(8,128)S(1)}, u32[]{:S(2)}, u32[]{:S(2)}) collective-permute-start(f32[1032,128]{1,0:T(8,128)S(1)} %select_maximum_fusion.4), channel_id=1, source_target_pairs={{0,8},{16,24},{32,40},{48,56},{64,72},{80,88},{96,104},{112,120},{... | collective-permute-start | bytes 1585160 | tf_op jit(solution)/shard_map/ppermute | solution.py:17
  22.2 1.5 %collective-permute-done.1 = f32[1032,128]{1,0:T(8,128)S(1)} collective-permute-done((f32[1032,128]{1,0:T(8,128)S(1)}, f32[1032,128]{1,0:T(8,128)S(1)}, u32[]{:S(2)}, u32[]{:S(2)}) %collective-permute-start.1) | collective-permute-done | bytes 528416 | tf_op jit(solution)/shard_map/ppermute | solution.py:17
  24.0 1.5 %collective-permute-start.2 = (f32[1032,128]{1,0:T(8,128)S(1)}, f32[1032,128]{1,0:T(8,128)}, u32[]{:S(2)}, u32[]{:S(2)}) collective-permute-start(f32[1032,128]{1,0:T(8,128)S(1)} %select_maximum_fusion.3), channel_id=1, source_target_pairs={{8,24},{24,40},{40,56},{56,72},{72,88},{88,104},{104,120},{120,136... | collective-permute-start | bytes 1585160 | tf_op jit(solution)/shard_map/ppermute | solution.py:17
  25.7 2.3 %reshape.744 = f32[2,256,1,16,64]{1,0,4,3,2:T(2,128)} reshape(bf16[512,1024]{0,1:T(8,128)(2,1)S(1)} %multiply_convert_fusion.5) | data formatting | bytes 3145728 | tf_op jit(solution)/shard_map/convert_element_type | solution.py:188
  28.2 1.2 %slice.312 = f32[1024,128]{1,0:T(8,128)S(1)} slice(f32[1032,128]{1,0:T(8,128)} %collective-permute-done.2), slice={[0:1024], [0:128]} | slice | bytes 1048576 | tf_op jit(solution)/shard_map/slice | solution.py:38
  30.3 1.3 %collective-permute-start.3 = (f32[1032,128]{1,0:T(8,128)S(1)}, f32[1032,128]{1,0:T(8,128)S(1)}, u32[]{:S(2)}, u32[]{:S(2)}) collective-permute-start(f32[1032,128]{1,0:T(8,128)S(1)} %select_maximum_fusion.2), channel_id=1, source_target_pairs={{8,16},{24,32},{40,48},{56,64},{72,80},{88,96},{104,112},{120,128}... | collective-permute-start | bytes 1585160 | tf_op jit(solution)/shard_map/ppermute | solution.py:17
  33.0 1.3 %collective-permute-start.4 = (f32[1032,128]{1,0:T(8,128)S(1)}, f32[1032,128]{1,0:T(8,128)}, u32[]{:S(2)}, u32[]{:S(2)}) collective-permute-start(f32[1032,128]{1,0:T(8,128)S(1)} %select_maximum_fusion.2), channel_id=1, source_target_pairs={{8,48},{24,64},{40,80},{56,96},{72,112},{88,128},{104,144},{120,16... | collective-permute-start | bytes 1585160 | tf_op jit(solution)/shard_map/ppermute | solution.py:17
  34.3 4.2 %bitcast_add_fusion = f32[2,256,1,16,64]{1,4,3,0,2:T(8,128)} fusion(f32[2,256,1,16,64]{1,0,4,3,2:T(2,128)S(1)} %copy-done.3, f32[2,16,256]{2,1,0:T(8,128)S(1)} %bitcast.165, f32[2,16,256]{2,1,0:T(8,128)S(1)} %get-tuple-element.83, f32[2,256,256]{2,1,0:T(8,128)S(1)} %fusion.39, pred[2,256,256]{2,1,0:T(8,128)(4,1)S(1)} %compare_and_fusion, ...), kind=kOutput, calls=%fused_computation.18 | convolution fusion | flops 282066944 | bytes 5963840 | tf_op jit(solution)/shard_map/cghqs,csghp->cqghp/dot_general | solution.py:157
  38.6 8.0 %collective-permute-done.3 = f32[1032,128]{1,0:T(8,128)S(1)} collective-permute-done((f32[1032,128]{1,0:T(8,128)S(1)}, f32[1032,128]{1,0:T(8,128)S(1)}, u32[]{:S(2)}, u32[]{:S(2)}) %collective-permute-start.3) | collective-permute-done | bytes 528416 | tf_op jit(solution)/shard_map/ppermute | solution.py:17
  46.7 0.8 copy-done.7
  47.6 20.2 %collective-permute-done.4 = f32[1032,128]{1,0:T(8,128)} collective-permute-done((f32[1032,128]{1,0:T(8,128)S(1)}, f32[1032,128]{1,0:T(8,128)}, u32[]{:S(2)}, u32[]{:S(2)}) %collective-permute-start.4) | collective-permute-done | bytes 528416 | tf_op jit(solution)/shard_map/ppermute | solution.py:17
  67.8 1.1 %slice.317 = f32[1024,128]{1,0:T(8,128)S(1)} slice(f32[1032,128]{1,0:T(8,128)} %collective-permute-done.4), slice={[0:1024], [0:128]} | slice | bytes 1048576 | tf_op jit(solution)/shard_map/slice | solution.py:38
  69.9 0.9 fusion.23
  70.7 5.1 %collective-permute-start.7 = (f32[1032,128]{1,0:T(8,128)}, f32[1032,128]{1,0:T(8,128)}, u32[]{:S(2)}, u32[]{:S(2)}) collective-permute-start(f32[1032,128]{1,0:T(8,128)} %fusion.23), channel_id=1, source_target_pairs={{0,8},{16,24},{32,40},{48,56},{64,72},{80,88},{96,104},{112,120},{... | collective-permute-start | bytes 1585160 | tf_op jit(solution)/shard_map/ppermute | solution.py:17
  75.9 1.5 %copy.106 = bf16[512,1024]{0,1:T(8,128)(2,1)S(1)} copy(bf16[512,1024]{1,0:T(8,128)(2,1)} %param.25) | data formatting | bytes 2097152 | tf_op args[2]
  77.7 1.3 %multiply_add_fusion.2 = (f32[1024,128]{1,0:T(8,128)S(1)}, f32[1024,128]{1,0:T(8,128)S(1)}) fusion(f32[1032,128]{1,0:T(8,128)} %fusion.23, f32[1032,128]{1,0:T(8,128)} %collective-permute-done.7, f32[]{:T(128)S(6)} %sub.35, f32[]{:T(128)S(6)} %convert_element_type.138), kind=kLoop, calls=%fused_computation.53 | loop fusion | flops 786432 | bytes 2097160 | tf_op jit(solution)/shard_map/add | solution.py:73
  80.3 1.0 fusion.17
  82.3 1.6 %copy.105 = f32[2,256,1,16,64]{1,0,4,3,2:T(2,128)S(1)} copy(f32[2,256,1,16,64]{1,4,3,0,2:T(8,128)S(1)} %fusion.12) | data formatting | bytes 4194304 | tf_op jit(solution)/shard_map/add | solution.py:193
  84.8 17.9 %all_to_all.6 = f32[8,1,512]{2,1,0:T(1,128)S(1)} all-to-all(f32[8,1,512]{2,1,0:T(1,128)S(1)} %broadcast_in_dim.144), channel_id=1, replica_groups=mesh['seq'=64,'tp'=8] {'tp'}, dimensions={0} | all-to-all | bytes 32768 | tf_op jit(solution)/shard_map/all_to_all | solution.py:82
  102.7 1.7 %multiply_convert_fusion.4 = bf16[512,1024]{0,1:T(8,128)(2,1)} fusion(f32[1024]{0:T(1024)S(1)} %copy-done.12, f32[512]{0:T(512)S(1)} %add_rsqrt_fusion, f32[512,1024]{0,1:T(8,128)S(1)} %bitcast.143, bf16[512,1024]{0,1:T(8,128)(2,1)S(1)} %copy.106), kind=kLoop, calls=%fused_computation.20 | loop fusion | flops 4718592 | bytes 4200448 | tf_op jit(solution)/shard_map/convert_element_type | solution.py:197
  104.4 2.3 %copy.108 = bf16[512,1024]{1,0:T(8,128)(2,1)} copy(bf16[512,1024]{0,1:T(8,128)(2,1)} %multiply_convert_fusion.4) | data formatting | bytes 2097152 | tf_op jit(solution)/shard_map/convert_element_type | solution.py:197
  (100 shorter events, 13.1 us)
Async XLA Ops:
  0.0 13.8 %copy-start.10 = (s32[512]{0:T(512)S(1)}, s32[512]{0:T(512)}, u32[]{:S(2)}) copy-start(s32[512]{0:T(512)} %param.35) | copy-start | bytes 6148
  0.0 10.5 %copy-start.4 = (bf16[512,1024]{1,0:T(8,128)(2,1)S(1)}, bf16[512,1024]{1,0:T(8,128)(2,1)}, u32[]{:S(2)}) copy-start(bf16[512,1024]{1,0:T(8,128)(2,1)} %param.23) | copy-start | bytes 3145732
  0.0 14.1 %copy-start.13 = (f32[2,128]{1,0:T(2,128)S(1)}, f32[2,128]{1,0:T(2,128)}, u32[]{:S(2)}) copy-start(f32[2,128]{1,0:T(2,128)} %param.30) | copy-start | bytes 3076
  2.7 10.9 %collective-permute-start = (bf16[3,1408]{0,1:T(8,128)(2,1)S(1)}, bf16[3,1408]{0,1:T(8,128)(2,1)S(1)}, u32[]{:S(2)}, u32[]{:S(2)}) collective-permute-start(bf16[3,1408]{0,1:T(8,128)(2,1)S(1)} %copy.94), channel_id=1, source_target_pairs={{0,8},{8,16},{16,24},{24,32},{32,40},{40,48},{48,56},{56,64},{64,7... | collective-permute-start | bytes 25352 | tf_op jit(solution)/shard_map/ppermute | solution.py:13
  10.6 5.1 %copy-start.11 = (f32[1024]{0:T(1024)S(1)}, f32[1024]{0:T(1024)}, u32[]{:S(2)}) copy-start(f32[1024]{0:T(1024)} %param.29) | copy-start | bytes 12292
  15.7 3.3 %copy-start.9 = (f32[2,256,128]{2,1,0:T(8,128)S(1)}, f32[2,256,128]{2,1,0:T(8,128)}, u32[]{:S(2)}) copy-start(f32[2,256,128]{2,1,0:T(8,128)} %convert_element_type.132) | copy-start | bytes 786436
  18.8 1.9 %copy-start.5 = (bf16[2,256,16,64]{1,0,3,2:T(2,128)(2,1)}, bf16[2,256,16,64]{1,0,3,2:T(2,128)(2,1)S(1)}, u32[]{:S(2)}) copy-start(bf16[2,256,16,64]{1,0,3,2:T(2,128)(2,1)S(1)} %reshape.720) | copy-start | bytes 3145732
  20.6 3.3 %copy-start = (f32[2,16,64,128]{3,2,1,0:T(8,128)}, f32[2,16,64,128]{3,2,1,0:T(8,128)S(1)}, u32[]{:S(2)}) copy-start(f32[2,16,64,128]{3,2,1,0:T(8,128)S(1)} %fusion.11) | copy-start | bytes 3145732
  20.8 2.8 %collective-permute-start.1 = (f32[1032,128]{1,0:T(8,128)S(1)}, f32[1032,128]{1,0:T(8,128)S(1)}, u32[]{:S(2)}, u32[]{:S(2)}) collective-permute-start(f32[1032,128]{1,0:T(8,128)S(1)} %select_maximum_fusion.4), channel_id=1, source_target_pairs={{0,8},{16,24},{32,40},{48,56},{64,72},{80,88},{96,104},{112,120},{... | collective-permute-start | bytes 1585160 | tf_op jit(solution)/shard_map/ppermute | solution.py:17
  24.0 4.3 %collective-permute-start.2 = (f32[1032,128]{1,0:T(8,128)S(1)}, f32[1032,128]{1,0:T(8,128)}, u32[]{:S(2)}, u32[]{:S(2)}) collective-permute-start(f32[1032,128]{1,0:T(8,128)S(1)} %select_maximum_fusion.3), channel_id=1, source_target_pairs={{8,24},{24,40},{40,56},{56,72},{72,88},{88,104},{104,120},{120,136... | collective-permute-start | bytes 1585160 | tf_op jit(solution)/shard_map/ppermute | solution.py:17
  28.0 6.3 %copy-start.3 = (f32[2,256,1,16,64]{1,0,4,3,2:T(2,128)S(1)}, f32[2,256,1,16,64]{1,0,4,3,2:T(2,128)}, u32[]{:S(2)}) copy-start(f32[2,256,1,16,64]{1,0,4,3,2:T(2,128)} %reshape.744) | copy-start | bytes 6291460
  28.0 6.3 %copy-start.6 = (bf16[2,256,16,64]{1,0,3,2:T(2,128)(2,1)S(1)}, bf16[2,256,16,64]{1,0,3,2:T(2,128)(2,1)}, u32[]{:S(2)}) copy-start(bf16[2,256,16,64]{1,0,3,2:T(2,128)(2,1)} %copy-done.5) | copy-start | bytes 3145732
  28.0 6.4 %copy-start.14 = (f32[16]{0:T(128)S(1)}, f32[16]{0:T(128)}, u32[]{:S(2)}) copy-start(f32[16]{0:T(128)} %param.33) | copy-start | bytes 196
  30.3 16.3 %collective-permute-start.3 = (f32[1032,128]{1,0:T(8,128)S(1)}, f32[1032,128]{1,0:T(8,128)S(1)}, u32[]{:S(2)}, u32[]{:S(2)}) collective-permute-start(f32[1032,128]{1,0:T(8,128)S(1)} %select_maximum_fusion.2), channel_id=1, source_target_pairs={{8,16},{24,32},{40,48},{56,64},{72,80},{88,96},{104,112},{120,128}... | collective-permute-start | bytes 1585160 | tf_op jit(solution)/shard_map/ppermute | solution.py:17
  31.6 15.0 %collective-permute-start.5 = (f32[1032,128]{1,0:T(8,128)S(1)}, f32[1032,128]{1,0:T(8,128)S(1)}, u32[]{:S(2)}, u32[]{:S(2)}) collective-permute-start(f32[1032,128]{1,0:T(8,128)S(1)} %select_maximum_fusion.2), channel_id=1, source_target_pairs={{8,88},{24,104},{40,120},{56,136},{72,152},{88,168},{104,184},{120... | collective-permute-start | bytes 1585160 | tf_op jit(solution)/shard_map/ppermute | solution.py:17
  32.3 14.3 %collective-permute-start.6 = (f32[1032,128]{1,0:T(8,128)S(1)}, f32[1032,128]{1,0:T(8,128)S(1)}, u32[]{:S(2)}, u32[]{:S(2)}) collective-permute-start(f32[1032,128]{1,0:T(8,128)S(1)} %select_maximum_fusion.2), channel_id=1, source_target_pairs={{8,120},{24,136},{40,152},{56,168},{72,184},{88,200},{104,216},{12... | collective-permute-start | bytes 1585160 | tf_op jit(solution)/shard_map/ppermute | solution.py:17
  33.0 34.8 %collective-permute-start.4 = (f32[1032,128]{1,0:T(8,128)S(1)}, f32[1032,128]{1,0:T(8,128)}, u32[]{:S(2)}, u32[]{:S(2)}) collective-permute-start(f32[1032,128]{1,0:T(8,128)S(1)} %select_maximum_fusion.2), channel_id=1, source_target_pairs={{8,48},{24,64},{40,80},{56,96},{72,112},{88,128},{104,144},{120,16... | collective-permute-start | bytes 1585160 | tf_op jit(solution)/shard_map/ppermute | solution.py:17
  46.6 0.8 copy-start.7
  47.6 22.1 %copy-start.8 = (f32[1032,128]{1,0:T(8,128)S(1)}, f32[1032,128]{1,0:T(8,128)}, u32[]{:S(2)}) copy-start(f32[1032,128]{1,0:T(8,128)} %copy-done.7) | copy-start | bytes 1585156
  70.7 9.0 %copy-start.1 = (f32[2,16,64,128]{3,2,1,0:T(8,128)S(1)}, f32[2,16,64,128]{3,2,1,0:T(8,128)}, u32[]{:S(2)}) copy-start(f32[2,16,64,128]{3,2,1,0:T(8,128)} %copy-done) | copy-start | bytes 3145732
  70.7 7.0 %collective-permute-start.7 = (f32[1032,128]{1,0:T(8,128)}, f32[1032,128]{1,0:T(8,128)}, u32[]{:S(2)}, u32[]{:S(2)}) collective-permute-start(f32[1032,128]{1,0:T(8,128)} %fusion.23), channel_id=1, source_target_pairs={{0,8},{16,24},{32,40},{48,56},{64,72},{80,88},{96,104},{112,120},{... | collective-permute-start | bytes 1585160 | tf_op jit(solution)/shard_map/ppermute | solution.py:17
  80.2 1.6 %copy-start.2 = (f32[2,256,1,16,64]{1,4,3,0,2:T(8,128)S(1)}, f32[2,256,1,16,64]{1,4,3,0,2:T(8,128)}, u32[]{:S(2)}) copy-start(f32[2,256,1,16,64]{1,4,3,0,2:T(8,128)} %bitcast_add_fusion) | copy-start | bytes 6291460
  84.1 18.6 %copy-start.12 = (f32[1024]{0:T(1024)S(1)}, f32[1024]{0:T(1024)}, u32[]{:S(2)}) copy-start(f32[1024]{0:T(1024)} %param.34) | copy-start | bytes 12292

commit v11 on v9

--- a/solution.py
+++ b/solution.py
@@ -186,8 +186,10 @@
     product = jnp.einsum("cqgn,cghpn->cqghp", c_float, states, precision=lax.Precision.HIGHEST)
     y_inter = product * link.transpose(0, 3, 1, 2)[..., None]
     mixed = base + y_inter
-    gated = mixed.reshape(tok_rows, inner_local) * jax.nn.silu(z_proj.astype(jnp.float32))
-    squares = summed_over(jnp.sum(gated * gated, axis=-1), "tp")
+    gate = jax.nn.silu(z_proj.astype(jnp.float32)).reshape(mixed.shape)
+    gated = mixed * gate
+    squares = summed_over(jnp.sum(gated * gated, axis=(2, 3, 4)).reshape(tok_rows), "tp")
+    gated = gated.reshape(tok_rows, inner_local)
     scale = lax.rsqrt(squares / (inner_local * lax.axis_size("tp")) + 1e-05)
     return (gated * scale[:, None] * norm_gain).astype(jnp.bfloat16)
 

time: 106 us -> 127 us (1.20)
  the two profiles are of different devices: /device:TPU:6 before, /device:TPU:19 now
where the time goes in v11:
time: 127 us; the launch traced here: 126 us
  starting transfers between devices  37.4 us (29%)
  local copies, waits for them, and re-layouts  30.8 us (24%)
  other arithmetic  25.9 us (20%)
  waiting for transfers between devices  23.4 us (18%)
  matrix products  8.03 us (6%)
    ppermute x7, starting transfers between devices, shifted(): return lax.ppermute(block, axis, pairs)  23.6 us
    ppermute x7, waiting for transfers between devices, shifted(): return lax.ppermute(block, axis, pairs)  20.1 us
    all_to_all x1, starting transfers between devices, summed_over(): return lax.all_to_all(spread, axis, 0, 0, tiled=False).sum(0)  10 us
    convert_element_type x2, other arithmetic, causal_conv(): return jax.nn.silu(result).astype(jnp.bfloat16)  6.96 us
    reshape x2, local copies, waits for them, and re-layouts, on_device(): gate = jax.nn.silu(z_proj.astype(jnp.float32)).reshape(mixed.shape)  6.04 us
    convert_element_type x2, local copies, waits for them, and re-layouts, on_device(): base = y_intra + skip * x_heads.astype(jnp.float32)  6.02 us
    dot_general x1, matrix products, on_device(): jnp.einsum('cghqs,csghp->cqghp', mixing, x_heads, preferred_element_type=...  4.13 us
    another operation x5, local copies, waits for them, and re-layouts  4 us
  transfers between devices with their start and end apart: 9, of which 4 were waited for; matrix products, arithmetic and copies ran while one was open for 24% of the time, Pallas kernels for 0%

profile of v11, /device:TPU:19, one launch (start us, length us, event | category | flops | bytes accessed | tf_op | source)
XLA Modules:
  0.0 126.1 jit_solution(9531382433040779970)
XLA Ops:
  2.3 3.8 %collective-permute-start = (bf16[3,1408]{1,0:T(4,128)(2,1)S(1)}, bf16[3,1408]{1,0:T(4,128)(2,1)S(1)}, u32[]{:S(2)}, u32[]{:S(2)}) collective-permute-start(bf16[3,1408]{1,0:T(4,128)(2,1)S(1)} %pad_maximum_fusion.2), channel_id=1, source_target_pairs={{0,8},{8,16},{16,24},{24,32},{32,40},{40,48},{48,56},{56,64},{64,7... | collective-permute-start | bytes 25352 | tf_op jit(solution)/shard_map/ppermute | solution.py:13
  7.0 1.3 %bitcast_convert_fusion.3 = (f32[2,128]{1,0:T(2,128)}, f32[2,128]{1,0:T(2,128)}, f32[2,128]{1,0:T(2,128)}, f32[2,128]{1,0:T(2,128)}) fusion(bf16[4,2,128]{2,1,0:T(2,128)(2,1)} %param.28), kind=kLoop, calls=%fused_computation.99 | loop fusion | flops 1024 | bytes 6144 | tf_op jit(solution)/shard_map/mul | solution.py:88
  9.8 1.2 reduce-window.6
  15.6 5.3 %multiply_convert_fusion.5 = bf16[512,1024]{1,0:T(8,128)(2,1)S(1)} fusion(bf16[512,1024]{1,0:T(8,128)(2,1)} %param.23, bf16[3,1024]{1,0:T(4,128)(2,1)S(1)} %slice.293, f32[1024]{0:T(1024)S(1)} %bitcast.165, f32[1024]{0:T(1024)S(1)} %bitcast.166, f32[1024]{0:T(1024)S(1)} %bitcast.164, f32[1024]{0:T(1024)S(1)} %bitcast.163, f32[1024]{0:T(1024)} %param.29, ...), kind=kLoop, calls=%fused_computation.23 | loop fusion | flops 15728640 | bytes 2125824 | tf_op jit(solution)/shard_map/convert_element_type | solution.py:89
  20.9 1.3 %reshape.658 = bf16[2,256,16,64]{3,2,1,0:T(8,128)(2,1)S(1)} reshape(bf16[512,1024]{1,0:T(8,128)(2,1)S(1)} %multiply_convert_fusion.5) | data formatting | bytes 2097152 | tf_op jit(solution)/shard_map/reshape.144
  22.3 2.5 %copy.75 = bf16[2,256,16,64]{1,3,2,0:T(8,128)(2,1)} copy(bf16[2,256,16,64]{3,2,1,0:T(8,128)(2,1)S(1)} %reshape.658) | data formatting | bytes 2097152 | tf_op jit(solution)/shard_map/reshape.144
  24.8 1.6 %multiply_convert_fusion.8 = bf16[512,2,128]{2,0,1:T(8,128)(2,1)S(1)} fusion(bf16[512,2,128]{2,0,1:T(8,128)(2,1)S(1)} %copy.72, bf16[3,2,128]{2,0,1:T(4,128)(2,1)S(1)} %slice_bitcast_fusion, f32[2,128]{1,0:T(2,128)} %get-tuple-element.96, f32[2,128]{1,0:T(2,128)} %get-tuple-element.97, f32[2,128]{1,0:T(2,128)} %get-tuple-element.95, ...), kind=kLoop, calls=%fused_computation.49 | loop fusion | flops 3932160 | bytes 532992 | tf_op jit(solution)/shard_map/convert_element_type | solution.py:89
  27.2 2.7 %fusion.10 = f32[2,16,64,128]{3,2,1,0:T(8,128)S(1)} fusion(bf16[2,256,16,64]{1,3,2,0:T(8,128)(2,1)} %copy.75, f32[2,16,256]{2,1,0:T(8,128)S(1)} %fusion.24, f32[2,256,128]{2,1,0:T(8,128)S(1)} %convert_element_type.129), kind=kOutput, calls=%fused_computation.14 | convolution fusion | flops 136314880 | bytes 2392064 | tf_op jit(solution)/shard_map/cghsn,csghp->cghpn/dot_general | solution.py:158
  30.1 1.3 %collective-permute-start.1 = (f32[1032,128]{1,0:T(8,128)S(1)}, f32[1032,128]{1,0:T(8,128)S(1)}, u32[]{:S(2)}, u32[]{:S(2)}) collective-permute-start(f32[1032,128]{1,0:T(8,128)S(1)} %select_maximum_fusion.4), channel_id=1, source_target_pairs={{0,8},{16,24},{32,40},{48,56},{64,72},{80,88},{96,104},{112,120},{... | collective-permute-start | bytes 1585160 | tf_op jit(solution)/shard_map/ppermute | solution.py:17
  31.4 2.5 %collective-permute-done.1 = f32[1032,128]{1,0:T(8,128)S(1)} collective-permute-done((f32[1032,128]{1,0:T(8,128)S(1)}, f32[1032,128]{1,0:T(8,128)S(1)}, u32[]{:S(2)}, u32[]{:S(2)}) %collective-permute-start.1) | collective-permute-done | bytes 528416 | tf_op jit(solution)/shard_map/ppermute | solution.py:17
  35.6 4.4 %collective-permute-start.2 = (f32[1032,128]{1,0:T(8,128)}, f32[1032,128]{1,0:T(8,128)}, u32[]{:S(2)}, u32[]{:S(2)}) collective-permute-start(f32[1032,128]{1,0:T(8,128)} %select_maximum_fusion.3), channel_id=1, source_target_pairs={{8,24},{24,40},{40,56},{56,72},{72,88},{88,104},{104,120},{120,136... | collective-permute-start | bytes 1585160 | tf_op jit(solution)/shard_map/ppermute | solution.py:17
  40.9 2.5 %reshape.656 = f32[2,256,1,16,64]{4,3,1,0,2:T(8,128)} reshape(bf16[512,1024]{1,0:T(8,128)(2,1)S(1)} %multiply_convert_fusion.5) | data formatting | bytes 3145728 | tf_op jit(solution)/shard_map/convert_element_type | solution.py:183
  43.4 3.5 %copy.78 = f32[2,256,1,16,64]{1,4,3,0,2:T(8,128)S(1)} copy(f32[2,256,1,16,64]{4,3,1,0,2:T(8,128)} %reshape.656) | data formatting | bytes 4194304 | tf_op jit(solution)/shard_map/convert_element_type | solution.py:183
  47.2 1.2 slice.308
  49.2 2.8 %collective-permute-start.5 = (f32[1032,128]{1,0:T(8,128)S(1)}, f32[1032,128]{1,0:T(8,128)S(1)}, u32[]{:S(2)}, u32[]{:S(2)}) collective-permute-start(f32[1032,128]{1,0:T(8,128)S(1)} %select_maximum_fusion.2), channel_id=1, source_target_pairs={{8,88},{24,104},{40,120},{56,136},{72,152},{88,168},{104,184},{120... | collective-permute-start | bytes 1585160 | tf_op jit(solution)/shard_map/ppermute | solution.py:17
  52.0 3.7 %collective-permute-start.6 = (f32[1032,128]{1,0:T(8,128)S(1)}, f32[1032,128]{1,0:T(8,128)S(1)}, u32[]{:S(2)}, u32[]{:S(2)}) collective-permute-start(f32[1032,128]{1,0:T(8,128)S(1)} %select_maximum_fusion.2), channel_id=1, source_target_pairs={{8,120},{24,136},{40,152},{56,168},{72,184},{88,200},{104,216},{12... | collective-permute-start | bytes 1585160 | tf_op jit(solution)/shard_map/ppermute | solution.py:17
  55.7 2.1 %collective-permute-start.3 = (f32[1032,128]{1,0:T(8,128)S(1)}, f32[1032,128]{1,0:T(8,128)}, u32[]{:S(2)}, u32[]{:S(2)}) collective-permute-start(f32[1032,128]{1,0:T(8,128)S(1)} %select_maximum_fusion.2), channel_id=1, source_target_pairs={{8,16},{24,32},{40,48},{56,64},{72,80},{88,96},{104,112},{120,128}... | collective-permute-start | bytes 1585160 | tf_op jit(solution)/shard_map/ppermute | solution.py:17
  57.8 2.1 %collective-permute-start.4 = (f32[1032,128]{1,0:T(8,128)S(1)}, f32[1032,128]{1,0:T(8,128)}, u32[]{:S(2)}, u32[]{:S(2)}) collective-permute-start(f32[1032,128]{1,0:T(8,128)S(1)} %select_maximum_fusion.2), channel_id=1, source_target_pairs={{8,48},{24,64},{40,80},{56,96},{72,112},{88,128},{104,144},{120,16... | collective-permute-start | bytes 1585160 | tf_op jit(solution)/shard_map/ppermute | solution.py:17
  59.9 4.1 %bitcast_add_fusion = f32[2,256,1,16,64]{1,4,3,0,2:T(8,128)} fusion(f32[2,256,1,16,64]{1,4,3,0,2:T(8,128)S(1)} %copy.78, bf16[2,256,16,64]{1,3,2,0:T(8,128)(2,1)S(1)} %copy-done.4, f32[2,16,256]{2,1,0:T(8,128)S(1)} %bitcast.162, f32[2,16,256]{2,1,0:T(8,128)S(1)} %get-tuple-element.83, f32[2,256,256]{2,1,0:T(8,128)S(1)} %fusion.33, ...), kind=kOutput, calls=%fused_computation.18 | convolution fusion | flops 282066944 | bytes 5963840 | tf_op jit(solution)/shard_map/cghqs,csghp->cqghp/dot_general | solution.py:152
  64.0 9.5 %collective-permute-done.5 = f32[1032,128]{1,0:T(8,128)S(1)} collective-permute-done((f32[1032,128]{1,0:T(8,128)S(1)}, f32[1032,128]{1,0:T(8,128)S(1)}, u32[]{:S(2)}, u32[]{:S(2)}) %collective-permute-start.5) | collective-permute-done | bytes 528416 | tf_op jit(solution)/shard_map/ppermute | solution.py:17
  73.5 8.1 %collective-permute-done.6 = f32[1032,128]{1,0:T(8,128)S(1)} collective-permute-done((f32[1032,128]{1,0:T(8,128)S(1)}, f32[1032,128]{1,0:T(8,128)S(1)}, u32[]{:S(2)}, u32[]{:S(2)}) %collective-permute-start.6) | collective-permute-done | bytes 528416 | tf_op jit(solution)/shard_map/ppermute | solution.py:17
  82.5 1.2 slice.311
  86.6 7.3 %collective-permute-start.7 = (f32[1032,128]{1,0:T(8,128)S(1)}, f32[1032,128]{1,0:T(8,128)}, u32[]{:S(2)}, u32[]{:S(2)}) collective-permute-start(f32[1032,128]{1,0:T(8,128)S(1)} %fusion.20), channel_id=1, source_target_pairs={{0,8},{16,24},{32,40},{48,56},{64,72},{80,88},{96,104},{112,120},{... | collective-permute-start | bytes 1585160 | tf_op jit(solution)/shard_map/ppermute | solution.py:17
  94.5 2.5 %reshape.657 = f32[2,256,1,16,64]{4,3,1,0,2:T(8,128)} reshape(f32[512,1024]{1,0:T(8,128)S(1)} %convert_multiply_fusion) | data formatting | bytes 4194304 | tf_op jit(solution)/shard_map/reshape | solution.py:189
  97.0 3.5 %copy.80 = f32[2,256,1,16,64]{1,4,3,0,2:T(8,128)S(1)} copy(f32[2,256,1,16,64]{4,3,1,0,2:T(8,128)} %reshape.657) | data formatting | bytes 4194304 | tf_op jit(solution)/shard_map/reshape | solution.py:189
  100.6 1.1 broadcast_select_fusion
  101.8 1.2 slice_select_fusion
  105.1 2.0 %multiply_reduce_fusion = (f32[2,256]{1,0:T(2,128)S(1)}, f32[2,256,1,16,64]{1,4,3,0,2:T(8,128)}) fusion(f32[2,256,1,16,64]{1,4,3,0,2:T(8,128)S(1)} %copy.80, f32[2,256,1,16,64]{1,4,3,0,2:T(8,128)S(1)} %copy-done.2, f32[2,256,16]{1,2,0:T(8,128)S(1)} %fusion.25, f32[2,16,64,256]{3,2,1,0:T(8,128)S(1)} %fusion.17), kind=kLoop, calls=%fused_computation.20 | loop fusion | flops 2620928 | bytes 8423424 | tf_op jit(solution)/shard_map/reduce_sum | solution.py:191
  107.7 10.0 %all-to-all-start = ((f32[8,1,512]{2,1,0:T(1,128)}), f32[8,1,512]{2,1,0:T(1,128)S(1)}, u32[]{:S(2)}, u32[]{:S(2)}) async-start(f32[8,1,512]{2,1,0:T(1,128)} %broadcast_in_dim.145), calls=%async_computation | async-start | bytes 32768 | tf_op jit(solution)/shard_map/all_to_all | solution.py:77
  117.7 3.2 %copy.81 = f32[2,256,1,16,64]{1,0,4,3,2:T(2,128)S(1)} copy(f32[2,256,1,16,64]{1,4,3,0,2:T(8,128)} %get-tuple-element.74) | data formatting | bytes 4194304 | tf_op jit(solution)/shard_map/mul | solution.py:190
  121.2 3.3 %all-to-all-done = f32[8,1,512]{2,1,0:T(1,128)S(1)} async-done(((f32[8,1,512]{2,1,0:T(1,128)}), f32[8,1,512]{2,1,0:T(1,128)S(1)}, u32[]{:S(2)}, u32[]{:S(2)}) %all-to-all-start) | async-done | bytes 16416 | tf_op jit(solution)/shard_map/all_to_all | solution.py:77
  124.8 1.3 %copy.83 = bf16[512,1024]{1,0:T(8,128)(2,1)} copy(bf16[512,1024]{0,1:T(8,128)(2,1)S(1)} %multiply_convert_fusion.4) | data formatting | bytes 2097152 | tf_op jit(solution)/shard_map/convert_element_type | solution.py:194
  (110 shorter events, 21.4 us)
Async XLA Ops:
  2.3 10.9 %collective-permute-start = (bf16[3,1408]{1,0:T(4,128)(2,1)S(1)}, bf16[3,1408]{1,0:T(4,128)(2,1)S(1)}, u32[]{:S(2)}, u32[]{:S(2)}) collective-permute-start(bf16[3,1408]{1,0:T(4,128)(2,1)S(1)} %pad_maximum_fusion.2), channel_id=1, source_target_pairs={{0,8},{8,16},{16,24},{24,32},{32,40},{40,48},{48,56},{56,64},{64,7... | collective-permute-start | bytes 25352 | tf_op jit(solution)/shard_map/ppermute | solution.py:13
  14.2 1.4 %copy-start.11 = (pred[512]{0:T(512)(128)(4,1)}, pred[512]{0:T(512)(128)(4,1)S(1)}, u32[]{:S(2)}) copy-start(pred[512]{0:T(512)(128)(4,1)S(1)} %get-tuple-element.90) | copy-start | bytes 1540
  14.2 1.4 %copy-start.12 = (pred[512]{0:T(512)(128)(4,1)}, pred[512]{0:T(512)(128)(4,1)S(1)}, u32[]{:S(2)}) copy-start(pred[512]{0:T(512)(128)(4,1)S(1)} %get-tuple-element.91) | copy-start | bytes 1540
  14.2 1.4 %copy-start.13 = (pred[512]{0:T(512)(128)(4,1)}, pred[512]{0:T(512)(128)(4,1)S(1)}, u32[]{:S(2)}) copy-start(pred[512]{0:T(512)(128)(4,1)S(1)} %get-tuple-element.98) | copy-start | bytes 1540
  29.9 4.3 %copy-start = (f32[2,16,64,128]{3,2,1,0:T(8,128)}, f32[2,16,64,128]{3,2,1,0:T(8,128)S(1)}, u32[]{:S(2)}) copy-start(f32[2,16,64,128]{3,2,1,0:T(8,128)S(1)} %fusion.10) | copy-start | bytes 3145732
  29.9 4.1 %copy-start.16 = (f32[16]{0:T(128)S(1)}, f32[16]{0:T(128)}, u32[]{:S(2)}) copy-start(f32[16]{0:T(128)} %get-tuple-element.104) | copy-start | bytes 196
  30.1 3.8 %collective-permute-start.1 = (f32[1032,128]{1,0:T(8,128)S(1)}, f32[1032,128]{1,0:T(8,128)S(1)}, u32[]{:S(2)}, u32[]{:S(2)}) collective-permute-start(f32[1032,128]{1,0:T(8,128)S(1)} %select_maximum_fusion.4), channel_id=1, source_target_pairs={{0,8},{16,24},{32,40},{48,56},{64,72},{80,88},{96,104},{112,120},{... | collective-permute-start | bytes 1585160 | tf_op jit(solution)/shard_map/ppermute | solution.py:17
  35.6 11.6 %collective-permute-start.2 = (f32[1032,128]{1,0:T(8,128)}, f32[1032,128]{1,0:T(8,128)}, u32[]{:S(2)}, u32[]{:S(2)}) collective-permute-start(f32[1032,128]{1,0:T(8,128)} %select_maximum_fusion.3), channel_id=1, source_target_pairs={{8,24},{24,40},{40,56},{56,72},{72,88},{88,104},{104,120},{120,136... | collective-permute-start | bytes 1585160 | tf_op jit(solution)/shard_map/ppermute | solution.py:17
  46.9 12.9 %copy-start.4 = (bf16[2,256,16,64]{1,3,2,0:T(8,128)(2,1)S(1)}, bf16[2,256,16,64]{1,3,2,0:T(8,128)(2,1)}, u32[]{:S(2)}) copy-start(bf16[2,256,16,64]{1,3,2,0:T(8,128)(2,1)} %copy.75) | copy-start | bytes 3145732
  46.9 12.9 %copy-start.9 = (pred[2,256,256]{2,1,0:T(8,128)(4,1)S(1)}, pred[2,256,256]{2,1,0:T(8,128)(4,1)}, u32[]{:S(2)}) copy-start(pred[2,256,256]{2,1,0:T(8,128)(4,1)} %compare_and_fusion) | copy-start | bytes 393220
  46.9 12.9 %copy-start.17 = (f32[16]{0:T(128)S(1)}, f32[16]{0:T(128)}, u32[]{:S(2)}) copy-start(f32[16]{0:T(128)} %param.33) | copy-start | bytes 196
  49.2 24.3 %collective-permute-start.5 = (f32[1032,128]{1,0:T(8,128)S(1)}, f32[1032,128]{1,0:T(8,128)S(1)}, u32[]{:S(2)}, u32[]{:S(2)}) collective-permute-start(f32[1032,128]{1,0:T(8,128)S(1)} %select_maximum_fusion.2), channel_id=1, source_target_pairs={{8,88},{24,104},{40,120},{56,136},{72,152},{88,168},{104,184},{120... | collective-permute-start | bytes 1585160 | tf_op jit(solution)/shard_map/ppermute | solution.py:17
  52.0 29.6 %collective-permute-start.6 = (f32[1032,128]{1,0:T(8,128)S(1)}, f32[1032,128]{1,0:T(8,128)S(1)}, u32[]{:S(2)}, u32[]{:S(2)}) collective-permute-start(f32[1032,128]{1,0:T(8,128)S(1)} %select_maximum_fusion.2), channel_id=1, source_target_pairs={{8,120},{24,136},{40,152},{56,168},{72,184},{88,200},{104,216},{12... | collective-permute-start | bytes 1585160 | tf_op jit(solution)/shard_map/ppermute | solution.py:17
  55.7 26.9 %collective-permute-start.3 = (f32[1032,128]{1,0:T(8,128)S(1)}, f32[1032,128]{1,0:T(8,128)}, u32[]{:S(2)}, u32[]{:S(2)}) collective-permute-start(f32[1032,128]{1,0:T(8,128)S(1)} %select_maximum_fusion.2), channel_id=1, source_target_pairs={{8,16},{24,32},{40,48},{56,64},{72,80},{88,96},{104,112},{120,128}... | collective-permute-start | bytes 1585160 | tf_op jit(solution)/shard_map/ppermute | solution.py:17
  57.8 26.6 %collective-permute-start.4 = (f32[1032,128]{1,0:T(8,128)S(1)}, f32[1032,128]{1,0:T(8,128)}, u32[]{:S(2)}, u32[]{:S(2)}) collective-permute-start(f32[1032,128]{1,0:T(8,128)S(1)} %select_maximum_fusion.2), channel_id=1, source_target_pairs={{8,48},{24,64},{40,80},{56,96},{72,112},{88,128},{104,144},{120,16... | collective-permute-start | bytes 1585160 | tf_op jit(solution)/shard_map/ppermute | solution.py:17
  73.5 8.1 %copy-start.5 = (f32[1032,128]{1,0:T(8,128)}, f32[1032,128]{1,0:T(8,128)S(1)}, u32[]{:S(2)}) copy-start(f32[1032,128]{1,0:T(8,128)S(1)} %collective-permute-done.5) | copy-start | bytes 1585156
  81.6 0.8 copy-start.7
  82.4 3.9 %copy-start.6 = (f32[1032,128]{1,0:T(8,128)S(1)}, f32[1032,128]{1,0:T(8,128)}, u32[]{:S(2)}) copy-start(f32[1032,128]{1,0:T(8,128)} %copy-done.5) | copy-start | bytes 1585156
  82.4 3.9 %copy-start.8 = (f32[1032,128]{1,0:T(8,128)S(1)}, f32[1032,128]{1,0:T(8,128)}, u32[]{:S(2)}) copy-start(f32[1032,128]{1,0:T(8,128)} %copy-done.7) | copy-start | bytes 1585156
  85.5 8.4 %copy-start.3 = (bf16[512,1024]{1,0:T(8,128)(2,1)S(1)}, bf16[512,1024]{1,0:T(8,128)(2,1)}, u32[]{:S(2)}) copy-start(bf16[512,1024]{1,0:T(8,128)(2,1)} %param.25) | copy-start | bytes 3145732
  86.6 14.0 %collective-permute-start.7 = (f32[1032,128]{1,0:T(8,128)S(1)}, f32[1032,128]{1,0:T(8,128)}, u32[]{:S(2)}, u32[]{:S(2)}) collective-permute-start(f32[1032,128]{1,0:T(8,128)S(1)} %fusion.20), channel_id=1, source_target_pairs={{0,8},{16,24},{32,40},{48,56},{64,72},{80,88},{96,104},{112,120},{... | collective-permute-start | bytes 1585160 | tf_op jit(solution)/shard_map/ppermute | solution.py:17
  100.6 2.4 %copy-start.10 = (f32[16]{0:T(128)S(1)}, f32[16]{0:T(128)}, u32[]{:S(2)}) copy-start(f32[16]{0:T(128)} %get-tuple-element.77) | copy-start | bytes 196
  101.8 1.4 %copy-start.1 = (f32[2,16,64,128]{3,2,1,0:T(8,128)S(1)}, f32[2,16,64,128]{3,2,1,0:T(8,128)}, u32[]{:S(2)}) copy-start(f32[2,16,64,128]{3,2,1,0:T(8,128)} %copy-done) | copy-start | bytes 3145732
  101.8 1.4 %copy-start.15 = (f32[16]{0:T(128)S(1)}, f32[16]{0:T(128)}, u32[]{:S(2)}) copy-start(f32[16]{0:T(128)} %get-tuple-element.101) | copy-start | bytes 196
  103.5 1.6 %copy-start.2 = (f32[2,256,1,16,64]{1,4,3,0,2:T(8,128)S(1)}, f32[2,256,1,16,64]{1,4,3,0,2:T(8,128)}, u32[]{:S(2)}) copy-start(f32[2,256,1,16,64]{1,4,3,0,2:T(8,128)} %bitcast_add_fusion) | copy-start | bytes 6291460
  107.7 16.7 %all-to-all-start = ((f32[8,1,512]{2,1,0:T(1,128)}), f32[8,1,512]{2,1,0:T(1,128)S(1)}, u32[]{:S(2)}, u32[]{:S(2)}) async-start(f32[8,1,512]{2,1,0:T(1,128)} %broadcast_in_dim.145), calls=%async_computation | async-start | bytes 32768 | tf_op jit(solution)/shard_map/all_to_all | solution.py:77
  121.0 3.5 %copy-start.14 = (f32[1024]{0:T(1024)S(1)}, f32[1024]{0:T(1024)}, u32[]{:S(2)}) copy-start(f32[1024]{0:T(1024)} %param.34) | copy-start | bytes 12292

commit v12 on v9

--- a/solution.py
+++ b/solution.py
@@ -183,7 +183,10 @@
     base = y_intra + skip * x_heads.astype(jnp.float32)
     entering, base = entering_state(device_gain, summary, "seq", base)
     states, _ = recur(entering)
-    product = jnp.einsum("cqgn,cghpn->cqghp", c_float, states, precision=lax.Precision.HIGHEST)
+    high = states.astype(jnp.bfloat16)
+    rest = (states - high.astype(jnp.float32)).astype(jnp.bfloat16)
+    product = jnp.einsum("cqgn,cghpn->cqghp", c_out, high, preferred_element_type=jnp.float32)
+    product = product + jnp.einsum("cqgn,cghpn->cqghp", c_out, rest, preferred_element_type=jnp.float32)
     y_inter = product * link.transpose(0, 3, 1, 2)[..., None]
     mixed = base + y_inter
     gated = mixed.reshape(tok_rows, inner_local) * jax.nn.silu(z_proj.astype(jnp.float32))

time: 106 us -> 112 us (1.057)
  local copies, waits for them, and re-layouts: 16.3 us -> 21 us
    unnamed x36, local copies, waits for them, and re-layouts: 5.33 us -> 7.44 us
    another operation x5 -> x4, other arithmetic: 2.34 us -> 2.1 us
  transfers between devices with their start and end apart: 8 -> 8, of which waited for: 4 -> 4; matrix products, arithmetic and copies ran while one was open for 15% -> 14% of each run, Pallas kernels for 0% -> 0%
where the time goes in v12:
time: 112 us; the launch traced here: 111 us
  waiting for transfers between devices  31.8 us (28%)
  local copies, waits for them, and re-layouts  21 us (19%)
  other arithmetic  18 us (16%)
  blocking collectives  17.9 us (16%)
  starting transfers between devices  13.3 us (12%)
  matrix products  8.09 us (7%)
    ppermute x7, waiting for transfers between devices, shifted(): return lax.ppermute(block, axis, pairs)  29.3 us
    all_to_all x1, blocking collectives, summed_over(): return lax.all_to_all(spread, axis, 0, 0, tiled=False).sum(0)  17.9 us
    ppermute x7, starting transfers between devices, shifted(): return lax.ppermute(block, axis, pairs)  11.4 us
    unnamed x36, local copies, waits for them, and re-layouts  7.44 us
    dot_general x1, matrix products, on_device(): jnp.einsum('cghqs,csghp->cqghp', mixing, x_heads, preferred_element_type=...  4.24 us
    convert_element_type x2, other arithmetic, causal_conv(): return jax.nn.silu(result).astype(jnp.bfloat16)  3.67 us
    dot_general x1, matrix products, on_device(): jnp.einsum('cghsn,csghp->cghpn', b_weighted, x_heads, preferred_element_t...  2.75 us
    ppermute x1, waiting for transfers between devices, from_behind(): return lax.ppermute(block, axis, route)  2.51 us
  transfers between devices with their start and end apart: 8, of which 4 were waited for; matrix products, arithmetic and copies ran while one was open for 14% of the time, Pallas kernels for 0%

profile of v12, /device:TPU:6, one launch (start us, length us, event | category | flops | bytes accessed | tf_op | source)
XLA Modules:
  0.0 110.6 jit_solution(2998096047761588141)
XLA Ops:
  2.7 1.9 %collective-permute-start = (bf16[3,1408]{0,1:T(8,128)(2,1)S(1)}, bf16[3,1408]{0,1:T(8,128)(2,1)}, u32[]{:S(2)}, u32[]{:S(2)}) collective-permute-start(bf16[3,1408]{0,1:T(8,128)(2,1)S(1)} %copy.94), channel_id=1, source_target_pairs={{0,8},{8,16},{16,24},{24,32},{32,40},{40,48},{48,56},{56,64},{64,7... | collective-permute-start | bytes 25352 | tf_op jit(solution)/shard_map/ppermute | solution.py:13
  5.3 0.9 broadcast_multiply_fusion
  6.2 1.2 %reduce-window.6 = f32[2,16,2,128]{3,1,2,0:T(8,128)S(1)} reduce-window(f32[2,16,2,128]{3,1,2,0:T(8,128)S(1)} %copy_bitcast_fusion.1, f32[]{:T(128)} %constant.131.clone.1), window={size=1x1x1x128 pad=0_0x0_0x0_0x127_0}, to_apply=%region_0.1 | reduce-window | flops 1040384 | bytes 65540 | tf_op jit(solution)/shard_map/reduce-window
  8.5 0.9 slice_convert_fusion.3
  9.6 1.0 copy.99
  11.1 2.5 %collective-permute-done = bf16[3,1408]{0,1:T(8,128)(2,1)} collective-permute-done((bf16[3,1408]{0,1:T(8,128)(2,1)S(1)}, bf16[3,1408]{0,1:T(8,128)(2,1)}, u32[]{:S(2)}, u32[]{:S(2)}) %collective-permute-start) | collective-permute-done | bytes 8480 | tf_op jit(solution)/shard_map/ppermute | solution.py:13
  14.7 0.8 slice.298
  15.7 0.8 multiply_convert_fusion.8
  16.6 1.0 slice.293
  17.5 2.8 %multiply_convert_fusion.5 = bf16[512,1024]{0,1:T(8,128)(2,1)S(1)} fusion(bf16[512,1024]{0,1:T(8,128)(2,1)S(1)} %copy.95, bf16[3,1024]{0,1:T(8,128)(2,1)S(1)} %slice.293, f32[1024]{0:T(1024)S(1)} %bitcast.159, f32[1024]{0:T(1024)S(1)} %bitcast.160, f32[1024]{0:T(1024)S(1)} %bitcast.158, f32[1024]{0:T(1024)S(1)} %bitcast.157, f32[1024]{0:T(1024)S(1)} %copy-done.11, ...), kind=kLoop, calls=%fused_computation.24 | loop fusion | flops 15728640 | bytes 2125824 | tf_op jit(solution)/shard_map/convert_element_type | solution.py:89
  20.4 1.1 %reshape.629 = bf16[2,256,16,64]{1,0,3,2:T(2,128)(2,1)} reshape(bf16[512,1024]{0,1:T(8,128)(2,1)S(1)} %multiply_convert_fusion.5) | data formatting | bytes 2097152 | tf_op jit(solution)/shard_map/reshape.143
  21.6 2.7 %fusion.11 = f32[2,16,64,128]{3,2,1,0:T(8,128)S(1)} fusion(f32[2,16,256]{2,1,0:T(8,128)S(1)} %fusion.27, f32[2,256,128]{2,1,0:T(8,128)S(1)} %convert_element_type.148, bf16[2,256,16,64]{1,0,3,2:T(2,128)(2,1)} %reshape.629), kind=kOutput, calls=%fused_computation.15 | convolution fusion | flops 136314880 | bytes 2392064 | tf_op jit(solution)/shard_map/cghsn,csghp->cghpn/dot_general | solution.py:158
  24.6 1.3 %collective-permute-start.1 = (f32[1032,128]{1,0:T(8,128)S(1)}, f32[1032,128]{1,0:T(8,128)S(1)}, u32[]{:S(2)}, u32[]{:S(2)}) collective-permute-start(f32[1032,128]{1,0:T(8,128)S(1)} %select_maximum_fusion.4), channel_id=1, source_target_pairs={{0,8},{16,24},{32,40},{48,56},{64,72},{80,88},{96,104},{112,120},{... | collective-permute-start | bytes 1585160 | tf_op jit(solution)/shard_map/ppermute | solution.py:17
  25.9 1.5 %collective-permute-done.1 = f32[1032,128]{1,0:T(8,128)S(1)} collective-permute-done((f32[1032,128]{1,0:T(8,128)S(1)}, f32[1032,128]{1,0:T(8,128)S(1)}, u32[]{:S(2)}, u32[]{:S(2)}) %collective-permute-start.1) | collective-permute-done | bytes 528416 | tf_op jit(solution)/shard_map/ppermute | solution.py:17
  28.4 0.8 select_maximum_fusion.3
  29.2 1.5 %collective-permute-start.2 = (f32[1032,128]{1,0:T(8,128)}, f32[1032,128]{1,0:T(8,128)}, u32[]{:S(2)}, u32[]{:S(2)}) collective-permute-start(f32[1032,128]{1,0:T(8,128)} %select_maximum_fusion.3), channel_id=1, source_target_pairs={{8,24},{24,40},{40,56},{56,72},{72,88},{88,104},{104,120},{120,136... | collective-permute-start | bytes 1585160 | tf_op jit(solution)/shard_map/ppermute | solution.py:17
  30.9 2.3 %reshape.653 = f32[2,256,1,16,64]{1,0,4,3,2:T(2,128)} reshape(bf16[512,1024]{0,1:T(8,128)(2,1)S(1)} %multiply_convert_fusion.5) | data formatting | bytes 3145728 | tf_op jit(solution)/shard_map/convert_element_type | solution.py:183
  33.5 1.2 %slice.308 = f32[1024,128]{1,0:T(8,128)S(1)} slice(f32[1032,128]{1,0:T(8,128)} %collective-permute-done.2), slice={[0:1024], [0:128]} | slice | bytes 1048576 | tf_op jit(solution)/shard_map/slice | solution.py:38
  35.6 1.3 %collective-permute-start.3 = (f32[1032,128]{1,0:T(8,128)S(1)}, f32[1032,128]{1,0:T(8,128)S(1)}, u32[]{:S(2)}, u32[]{:S(2)}) collective-permute-start(f32[1032,128]{1,0:T(8,128)S(1)} %select_maximum_fusion.2), channel_id=1, source_target_pairs={{8,16},{24,32},{40,48},{56,64},{72,80},{88,96},{104,112},{120,128}... | collective-permute-start | bytes 1585160 | tf_op jit(solution)/shard_map/ppermute | solution.py:17
  38.3 1.3 %collective-permute-start.4 = (f32[1032,128]{1,0:T(8,128)S(1)}, f32[1032,128]{1,0:T(8,128)}, u32[]{:S(2)}, u32[]{:S(2)}) collective-permute-start(f32[1032,128]{1,0:T(8,128)S(1)} %select_maximum_fusion.2), channel_id=1, source_target_pairs={{8,48},{24,64},{40,80},{56,96},{72,112},{88,128},{104,144},{120,16... | collective-permute-start | bytes 1585160 | tf_op jit(solution)/shard_map/ppermute | solution.py:17
  39.6 4.2 %bitcast_add_fusion = f32[2,256,1,16,64]{1,4,3,0,2:T(8,128)} fusion(f32[2,256,1,16,64]{1,0,4,3,2:T(2,128)S(1)} %copy-done.2, f32[2,16,256]{2,1,0:T(8,128)S(1)} %bitcast.156, f32[2,16,256]{2,1,0:T(8,128)S(1)} %get-tuple-element.83, f32[2,256,256]{2,1,0:T(8,128)S(1)} %fusion.37, pred[2,256,256]{2,1,0:T(8,128)(4,1)S(1)} %compare_and_fusion, ...), kind=kOutput, calls=%fused_computation.18 | convolution fusion | flops 282066944 | bytes 5963840 | tf_op jit(solution)/shard_map/cghqs,csghp->cqghp/dot_general | solution.py:152
  43.8 8.1 %collective-permute-done.3 = f32[1032,128]{1,0:T(8,128)S(1)} collective-permute-done((f32[1032,128]{1,0:T(8,128)S(1)}, f32[1032,128]{1,0:T(8,128)S(1)}, u32[]{:S(2)}, u32[]{:S(2)}) %collective-permute-start.3) | collective-permute-done | bytes 528416 | tf_op jit(solution)/shard_map/ppermute | solution.py:17
  53.8 19.6 %collective-permute-done.4 = f32[1032,128]{1,0:T(8,128)} collective-permute-done((f32[1032,128]{1,0:T(8,128)S(1)}, f32[1032,128]{1,0:T(8,128)}, u32[]{:S(2)}, u32[]{:S(2)}) %collective-permute-start.4) | collective-permute-done | bytes 528416 | tf_op jit(solution)/shard_map/ppermute | solution.py:17
  73.4 1.1 slice.313
  75.5 4.6 %collective-permute-start.7 = (f32[1032,128]{1,0:T(8,128)S(1)}, f32[1032,128]{1,0:T(8,128)}, u32[]{:S(2)}, u32[]{:S(2)}) collective-permute-start(f32[1032,128]{1,0:T(8,128)S(1)} %fusion.22), channel_id=1, source_target_pairs={{0,8},{16,24},{32,40},{48,56},{64,72},{80,88},{96,104},{112,120},{... | collective-permute-start | bytes 1585160 | tf_op jit(solution)/shard_map/ppermute | solution.py:17
  80.1 1.5 %copy.106 = bf16[512,1024]{0,1:T(8,128)(2,1)S(1)} copy(bf16[512,1024]{1,0:T(8,128)(2,1)} %param.25) | data formatting | bytes 2097152 | tf_op args[2]
  81.9 1.1 slice_select_fusion
  84.2 1.1 %copy-done.3 = f32[2,256,1,16,64]{1,4,3,0,2:T(8,128)S(1)} copy-done((f32[2,256,1,16,64]{1,4,3,0,2:T(8,128)S(1)}, f32[2,256,1,16,64]{1,4,3,0,2:T(8,128)}, u32[]{:S(2)}) %copy-start.3) | copy-done | bytes 2097176
  86.2 1.6 %copy.105 = f32[2,256,1,16,64]{1,0,4,3,2:T(2,128)S(1)} copy(f32[2,256,1,16,64]{1,4,3,0,2:T(8,128)S(1)} %fusion.12) | data formatting | bytes 4194304 | tf_op jit(solution)/shard_map/add | solution.py:191
  88.7 17.9 %all_to_all.6 = f32[8,1,512]{2,1,0:T(1,128)S(1)} all-to-all(f32[8,1,512]{2,1,0:T(1,128)S(1)} %broadcast_in_dim.143), channel_id=1, replica_groups=mesh['seq'=64,'tp'=8] {'tp'}, dimensions={0} | all-to-all | bytes 32768 | tf_op jit(solution)/shard_map/all_to_all | solution.py:77
  106.6 1.7 %multiply_convert_fusion.4 = bf16[512,1024]{0,1:T(8,128)(2,1)} fusion(f32[1024]{0:T(1024)S(1)} %copy-done.12, f32[512]{0:T(512)S(1)} %add_rsqrt_fusion, f32[512,1024]{0,1:T(8,128)S(1)} %bitcast.136, bf16[512,1024]{0,1:T(8,128)(2,1)S(1)} %copy.106), kind=kLoop, calls=%fused_computation.20 | loop fusion | flops 4718592 | bytes 4200448 | tf_op jit(solution)/shard_map/convert_element_type | solution.py:195
  108.3 2.3 %copy.108 = bf16[512,1024]{1,0:T(8,128)(2,1)} copy(bf16[512,1024]{0,1:T(8,128)(2,1)} %multiply_convert_fusion.4) | data formatting | bytes 2097152 | tf_op jit(solution)/shard_map/convert_element_type | solution.py:195
  (102 shorter events, 16.3 us)
Async XLA Ops:
  0.0 14.6 %copy-start.10 = (s32[512]{0:T(512)S(1)}, s32[512]{0:T(512)}, u32[]{:S(2)}) copy-start(s32[512]{0:T(512)} %param.35) | copy-start | bytes 6148
  0.0 10.5 %copy-start.4 = (bf16[512,1024]{1,0:T(8,128)(2,1)S(1)}, bf16[512,1024]{1,0:T(8,128)(2,1)}, u32[]{:S(2)}) copy-start(bf16[512,1024]{1,0:T(8,128)(2,1)} %param.23) | copy-start | bytes 3145732
  0.0 15.7 %copy-start.13 = (f32[2,128]{1,0:T(2,128)S(1)}, f32[2,128]{1,0:T(2,128)}, u32[]{:S(2)}) copy-start(f32[2,128]{1,0:T(2,128)} %param.30) | copy-start | bytes 3076
  2.7 11.0 %collective-permute-start = (bf16[3,1408]{0,1:T(8,128)(2,1)S(1)}, bf16[3,1408]{0,1:T(8,128)(2,1)}, u32[]{:S(2)}, u32[]{:S(2)}) collective-permute-start(bf16[3,1408]{0,1:T(8,128)(2,1)S(1)} %copy.94), channel_id=1, source_target_pairs={{0,8},{8,16},{16,24},{24,32},{32,40},{40,48},{48,56},{56,64},{64,7... | collective-permute-start | bytes 25352 | tf_op jit(solution)/shard_map/ppermute | solution.py:13
  10.6 7.0 %copy-start.11 = (f32[1024]{0:T(1024)S(1)}, f32[1024]{0:T(1024)}, u32[]{:S(2)}) copy-start(f32[1024]{0:T(1024)} %param.29) | copy-start | bytes 12292
  24.6 2.8 %collective-permute-start.1 = (f32[1032,128]{1,0:T(8,128)S(1)}, f32[1032,128]{1,0:T(8,128)S(1)}, u32[]{:S(2)}, u32[]{:S(2)}) collective-permute-start(f32[1032,128]{1,0:T(8,128)S(1)} %select_maximum_fusion.4), channel_id=1, source_target_pairs={{0,8},{16,24},{32,40},{48,56},{64,72},{80,88},{96,104},{112,120},{... | collective-permute-start | bytes 1585160 | tf_op jit(solution)/shard_map/ppermute | solution.py:17
  27.4 0.8 copy-start
  29.2 4.2 %collective-permute-start.2 = (f32[1032,128]{1,0:T(8,128)}, f32[1032,128]{1,0:T(8,128)}, u32[]{:S(2)}, u32[]{:S(2)}) collective-permute-start(f32[1032,128]{1,0:T(8,128)} %select_maximum_fusion.3), channel_id=1, source_target_pairs={{8,24},{24,40},{40,56},{56,72},{72,88},{88,104},{104,120},{120,136... | collective-permute-start | bytes 1585160 | tf_op jit(solution)/shard_map/ppermute | solution.py:17
  33.2 6.3 %copy-start.2 = (f32[2,256,1,16,64]{1,0,4,3,2:T(2,128)S(1)}, f32[2,256,1,16,64]{1,0,4,3,2:T(2,128)}, u32[]{:S(2)}) copy-start(f32[2,256,1,16,64]{1,0,4,3,2:T(2,128)} %reshape.653) | copy-start | bytes 6291460
  33.2 6.3 %copy-start.5 = (bf16[2,256,16,64]{1,0,3,2:T(2,128)(2,1)S(1)}, bf16[2,256,16,64]{1,0,3,2:T(2,128)(2,1)}, u32[]{:S(2)}) copy-start(bf16[2,256,16,64]{1,0,3,2:T(2,128)(2,1)} %reshape.629) | copy-start | bytes 3145732
  33.2 6.3 %copy-start.14 = (f32[16]{0:T(128)S(1)}, f32[16]{0:T(128)}, u32[]{:S(2)}) copy-start(f32[16]{0:T(128)} %param.33) | copy-start | bytes 196
  35.6 16.4 %collective-permute-start.3 = (f32[1032,128]{1,0:T(8,128)S(1)}, f32[1032,128]{1,0:T(8,128)S(1)}, u32[]{:S(2)}, u32[]{:S(2)}) collective-permute-start(f32[1032,128]{1,0:T(8,128)S(1)} %select_maximum_fusion.2), channel_id=1, source_target_pairs={{8,16},{24,32},{40,48},{56,64},{72,80},{88,96},{104,112},{120,128}... | collective-permute-start | bytes 1585160 | tf_op jit(solution)/shard_map/ppermute | solution.py:17
  36.9 15.2 %collective-permute-start.5 = (f32[1032,128]{1,0:T(8,128)S(1)}, f32[1032,128]{1,0:T(8,128)S(1)}, u32[]{:S(2)}, u32[]{:S(2)}) collective-permute-start(f32[1032,128]{1,0:T(8,128)S(1)} %select_maximum_fusion.2), channel_id=1, source_target_pairs={{8,88},{24,104},{40,120},{56,136},{72,152},{88,168},{104,184},{120... | collective-permute-start | bytes 1585160 | tf_op jit(solution)/shard_map/ppermute | solution.py:17
  37.6 14.5 %collective-permute-start.6 = (f32[1032,128]{1,0:T(8,128)S(1)}, f32[1032,128]{1,0:T(8,128)S(1)}, u32[]{:S(2)}, u32[]{:S(2)}) collective-permute-start(f32[1032,128]{1,0:T(8,128)S(1)} %select_maximum_fusion.2), channel_id=1, source_target_pairs={{8,120},{24,136},{40,152},{56,168},{72,184},{88,200},{104,216},{12... | collective-permute-start | bytes 1585160 | tf_op jit(solution)/shard_map/ppermute | solution.py:17
  38.3 35.1 %collective-permute-start.4 = (f32[1032,128]{1,0:T(8,128)S(1)}, f32[1032,128]{1,0:T(8,128)}, u32[]{:S(2)}, u32[]{:S(2)}) collective-permute-start(f32[1032,128]{1,0:T(8,128)S(1)} %select_maximum_fusion.2), channel_id=1, source_target_pairs={{8,48},{24,64},{40,80},{56,96},{72,112},{88,128},{104,144},{120,16... | collective-permute-start | bytes 1585160 | tf_op jit(solution)/shard_map/ppermute | solution.py:17
  52.0 0.8 copy-start.6
  52.8 0.8 copy-start.8
  53.8 21.5 %copy-start.7 = (f32[1032,128]{1,0:T(8,128)S(1)}, f32[1032,128]{1,0:T(8,128)}, u32[]{:S(2)}) copy-start(f32[1032,128]{1,0:T(8,128)} %copy-done.6) | copy-start | bytes 1585156
  53.8 21.5 %copy-start.9 = (f32[1032,128]{1,0:T(8,128)S(1)}, f32[1032,128]{1,0:T(8,128)}, u32[]{:S(2)}) copy-start(f32[1032,128]{1,0:T(8,128)} %copy-done.8) | copy-start | bytes 1585156
  75.5 6.3 %collective-permute-start.7 = (f32[1032,128]{1,0:T(8,128)S(1)}, f32[1032,128]{1,0:T(8,128)}, u32[]{:S(2)}, u32[]{:S(2)}) collective-permute-start(f32[1032,128]{1,0:T(8,128)S(1)} %fusion.22), channel_id=1, source_target_pairs={{0,8},{16,24},{32,40},{48,56},{64,72},{80,88},{96,104},{112,120},{... | collective-permute-start | bytes 1585160 | tf_op jit(solution)/shard_map/ppermute | solution.py:17
  81.7 1.3 %copy-start.1 = (f32[1024,128]{1,0:T(8,128)S(1)}, f32[1024,128]{1,0:T(8,128)}, u32[]{:S(2)}) copy-start(f32[1024,128]{1,0:T(8,128)} %copy-done) | copy-start | bytes 1572868
  83.7 1.6 %copy-start.3 = (f32[2,256,1,16,64]{1,4,3,0,2:T(8,128)S(1)}, f32[2,256,1,16,64]{1,4,3,0,2:T(8,128)}, u32[]{:S(2)}) copy-start(f32[2,256,1,16,64]{1,4,3,0,2:T(8,128)} %bitcast_add_fusion) | copy-start | bytes 6291460
  88.0 18.6 %copy-start.12 = (f32[1024]{0:T(1024)S(1)}, f32[1024]{0:T(1024)}, u32[]{:S(2)}) copy-start(f32[1024]{0:T(1024)} %param.34) | copy-start | bytes 12292

commit v13 on v9

--- a/solution.py
+++ b/solution.py
@@ -2,6 +2,7 @@
 import jax.numpy as jnp
 from jax import lax
 from jax.sharding import PartitionSpec as P
+from jax.experimental import pallas as pl
 
 STATE = 128
 STRETCH = 256
@@ -75,6 +76,28 @@
     count = lax.axis_size(axis)
     spread = jnp.broadcast_to(value[None], (count,) + value.shape)
     return lax.all_to_all(spread, axis, 0, 0, tiled=False).sum(0)
+
+
+def scale_kernel(g_ref, s_ref, w_ref, o_ref):
+    o_ref[...] = (g_ref[...] * s_ref[...] * w_ref[...]).T.astype(o_ref.dtype)
+
+
+def scaled_out(gated, scale, gain, block):
+    rows, width = gated.shape
+    return pl.pallas_call(
+        scale_kernel,
+        grid=(rows // block,),
+        in_specs=[
+            pl.BlockSpec((width, block), lambda i: (0, i)),
+            pl.BlockSpec((1, block), lambda i: (0, i)),
+            pl.BlockSpec((width, 1), lambda i: (0, 0)),
+        ],
+        out_specs=pl.BlockSpec((block, width), lambda i: (i, 0)),
+        out_shape=jax.ShapeDtypeStruct((rows, width), jnp.bfloat16),
+        cost_estimate=pl.CostEstimate(
+            flops=2 * rows * width, transcendentals=0, bytes_accessed=6 * rows * width
+        ),
+    )(gated.T, scale[None, :], gain[:, None])
 
 
 def causal_conv(window, window_ids, weight, bias, rows):
@@ -189,7 +212,7 @@
     gated = mixed.reshape(tok_rows, inner_local) * jax.nn.silu(z_proj.astype(jnp.float32))
     squares = summed_over(jnp.sum(gated * gated, axis=-1), "tp")
     scale = lax.rsqrt(squares / (inner_local * lax.axis_size("tp")) + 1e-05)
-    return (gated * scale[:, None] * norm_gain).astype(jnp.bfloat16)
+    return scaled_out(gated, scale, norm_gain, block)
 
 
 def solution(mesh):

time: 106 us -> 112 us (1.057)
  blocking collectives: 17.9 us -> 0 us
  starting transfers between devices: 13.7 us -> 24 us
  waiting for transfers between devices: 32.1 us -> 37.7 us
  Pallas kernels: 0 us -> 3.22 us
  local copies, waits for them, and re-layouts: 16.3 us -> 19.4 us
    all_to_all x1 -> x0, blocking collectives: 17.9 us -> none  [summed_over(): return lax.all_to_all(spread, axis, 0, 0, tiled=False).sum(0)]
    all_to_all x0 -> x1, starting transfers between devices: none -> 10.3 us  [summed_over(): return lax.all_to_all(spread, axis, 0, 0, tiled=False).sum(0)]
    all_to_all x0 -> x1, waiting for transfers between devices: none -> 6.73 us  [summed_over(): return lax.all_to_all(spread, axis, 0, 0, tiled=False).sum(0)]
    pallas_call x0 -> x1, Pallas kernels: none -> 3.22 us  [scaled_out(): pl.pallas_call(scale_kernel, grid=(rows // block,), in_specs=[pl.BlockSpe...]
    unnamed x36 -> x42, local copies, waits for them, and re-layouts: 5.33 us -> 7.6 us
    convert_element_type x1 -> x0, local copies, waits for them, and re-layouts: 2.26 us -> none  [on_device(): return (gated * scale[:, None] * norm_gain).astype(jnp.bfloat16)]
    convert_element_type x1 -> x0, other arithmetic: 1.7 us -> none  [on_device(): return (gated * scale[:, None] * norm_gain).astype(jnp.bfloat16)]
    reduce_sum x1, other arithmetic: 0.68 us -> 2 us  [on_device(): squares = summed_over(jnp.sum(gated * gated, axis=-1), 'tp')]
  transfers between devices with their start and end apart: 8 -> 9, of which waited for: 4 -> 5; matrix products, arithmetic and copies ran while one was open for 15% -> 17% of each run, Pallas kernels for 0% -> 0%
where the time goes in v13:
time: 112 us; the launch traced here: 111 us
  waiting for transfers between devices  37.7 us (34%)
  starting transfers between devices  24 us (21%)
  local copies, waits for them, and re-layouts  19.4 us (17%)
  other arithmetic  18.1 us (16%)
  matrix products  8.24 us (7%)
  Pallas kernels  3.22 us (3%)
    ppermute x7, waiting for transfers between devices, shifted(): return lax.ppermute(block, axis, pairs)  29.2 us
    ppermute x7, starting transfers between devices, shifted(): return lax.ppermute(block, axis, pairs)  11.7 us
    all_to_all x1, starting transfers between devices, summed_over(): return lax.all_to_all(spread, axis, 0, 0, tiled=False).sum(0)  10.3 us
    unnamed x42, local copies, waits for them, and re-layouts  7.6 us
    all_to_all x1, waiting for transfers between devices, summed_over(): return lax.all_to_all(spread, axis, 0, 0, tiled=False).sum(0)  6.73 us
    dot_general x1, matrix products, on_device(): jnp.einsum('cghqs,csghp->cqghp', mixing, x_heads, preferred_element_type=...  4.26 us
    convert_element_type x2, other arithmetic, causal_conv(): return jax.nn.silu(result).astype(jnp.bfloat16)  3.67 us
    pallas_call x1, Pallas kernels, scaled_out(): pl.pallas_call(scale_kernel, grid=(rows // block,), in_specs=[pl.BlockSpe...  3.22 us
  transfers between devices with their start and end apart: 9, of which 5 were waited for; matrix products, arithmetic and copies ran while one was open for 17% of the time, Pallas kernels for 0%

profile of v13, /device:TPU:6, one launch (start us, length us, event | category | flops | bytes accessed | tf_op | source)
XLA Modules:
  0.0 111.1 jit_solution(4554827227060968734)
XLA Ops:
  2.7 1.9 %collective-permute-start = (bf16[3,1408]{0,1:T(8,128)(2,1)S(1)}, bf16[3,1408]{0,1:T(8,128)(2,1)S(1)}, u32[]{:S(2)}, u32[]{:S(2)}) collective-permute-start(bf16[3,1408]{0,1:T(8,128)(2,1)S(1)} %copy.100), channel_id=1, source_target_pairs={{0,8},{8,16},{16,24},{24,32},{32,40},{40,48},{48,56},{56,64},{64,7... | collective-permute-start | bytes 25352 | tf_op jit(solution)/shard_map/ppermute | solution.py:14
  5.3 0.9 broadcast_multiply_fusion
  6.2 1.2 %reduce-window.6 = f32[2,16,2,128]{3,1,2,0:T(8,128)S(1)} reduce-window(f32[2,16,2,128]{3,1,2,0:T(8,128)S(1)} %copy_bitcast_fusion.1, f32[]{:T(128)} %constant.131.clone.1), window={size=1x1x1x128 pad=0_0x0_0x0_0x127_0}, to_apply=%region_0.1 | reduce-window | flops 1040384 | bytes 65540 | tf_op jit(solution)/shard_map/reduce-window
  9.1 0.9 slice_convert_fusion.3
  10.2 1.0 copy.104
  11.7 1.8 %collective-permute-done = bf16[3,1408]{0,1:T(8,128)(2,1)S(1)} collective-permute-done((bf16[3,1408]{0,1:T(8,128)(2,1)S(1)}, bf16[3,1408]{0,1:T(8,128)(2,1)S(1)}, u32[]{:S(2)}, u32[]{:S(2)}) %collective-permute-start) | collective-permute-done | bytes 8480 | tf_op jit(solution)/shard_map/ppermute | solution.py:14
  14.7 0.8 multiply_convert_fusion.7
  15.6 2.8 %multiply_convert_fusion.4 = bf16[512,1024]{0,1:T(8,128)(2,1)S(1)} fusion(bf16[512,1024]{0,1:T(8,128)(2,1)S(1)} %copy.101, bf16[3,1024]{0,1:T(8,128)(2,1)S(1)} %slice.293, f32[1024]{0:T(1024)S(1)} %bitcast.171, f32[1024]{0:T(1024)S(1)} %bitcast.172, f32[1024]{0:T(1024)S(1)} %bitcast.170, f32[1024]{0:T(1024)S(1)} %bitcast.169, f32[1024]{0:T(1024)S(1)} %copy-done.13, ...), kind=kLoop, calls=%fused_computation.23 | loop fusion | flops 15728640 | bytes 2125824 | tf_op jit(solution)/shard_map/convert_element_type | solution.py:112
  18.4 1.1 reshape.632
  19.6 2.7 %fusion.11 = f32[2,16,64,128]{3,2,1,0:T(8,128)S(1)} fusion(f32[2,16,256]{2,1,0:T(8,128)S(1)} %fusion.26, f32[2,256,128]{2,1,0:T(8,128)S(1)} %convert_element_type.126, bf16[2,256,16,64]{1,0,3,2:T(2,128)(2,1)} %reshape.632), kind=kOutput, calls=%fused_computation.15 | convolution fusion | flops 136314880 | bytes 2392064 | tf_op jit(solution)/shard_map/cghsn,csghp->cghpn/dot_general | solution.py:181
  22.6 1.8 %collective-permute-start.1 = (f32[1032,128]{1,0:T(8,128)S(1)}, f32[1032,128]{1,0:T(8,128)S(1)}, u32[]{:S(2)}, u32[]{:S(2)}) collective-permute-start(f32[1032,128]{1,0:T(8,128)S(1)} %select_maximum_fusion.4), channel_id=1, source_target_pairs={{0,8},{16,24},{32,40},{48,56},{64,72},{80,88},{96,104},{112,120},{... | collective-permute-start | bytes 1585160 | tf_op jit(solution)/shard_map/ppermute | solution.py:18
  24.4 1.5 %collective-permute-done.1 = f32[1032,128]{1,0:T(8,128)S(1)} collective-permute-done((f32[1032,128]{1,0:T(8,128)S(1)}, f32[1032,128]{1,0:T(8,128)S(1)}, u32[]{:S(2)}, u32[]{:S(2)}) %collective-permute-start.1) | collective-permute-done | bytes 528416 | tf_op jit(solution)/shard_map/ppermute | solution.py:18
  26.2 0.8 select_maximum_fusion.3
  27.0 1.5 %collective-permute-start.2 = (f32[1032,128]{1,0:T(8,128)}, f32[1032,128]{1,0:T(8,128)}, u32[]{:S(2)}, u32[]{:S(2)}) collective-permute-start(f32[1032,128]{1,0:T(8,128)} %select_maximum_fusion.3), channel_id=1, source_target_pairs={{8,24},{24,40},{40,56},{56,72},{72,88},{88,104},{104,120},{120,136... | collective-permute-start | bytes 1585160 | tf_op jit(solution)/shard_map/ppermute | solution.py:18
  29.9 2.3 %reshape.660 = f32[2,256,1,16,64]{1,0,4,3,2:T(2,128)} reshape(bf16[512,1024]{0,1:T(8,128)(2,1)S(1)} %multiply_convert_fusion.4) | data formatting | bytes 3145728 | tf_op jit(solution)/shard_map/convert_element_type | solution.py:206
  32.5 1.2 %slice.308 = f32[1024,128]{1,0:T(8,128)S(1)} slice(f32[1032,128]{1,0:T(8,128)} %collective-permute-done.2), slice={[0:1024], [0:128]} | slice | bytes 1048576 | tf_op jit(solution)/shard_map/slice | solution.py:39
  34.6 1.3 %collective-permute-start.3 = (f32[1032,128]{1,0:T(8,128)S(1)}, f32[1032,128]{1,0:T(8,128)S(1)}, u32[]{:S(2)}, u32[]{:S(2)}) collective-permute-start(f32[1032,128]{1,0:T(8,128)S(1)} %select_maximum_fusion.2), channel_id=1, source_target_pairs={{8,16},{24,32},{40,48},{56,64},{72,80},{88,96},{104,112},{120,128}... | collective-permute-start | bytes 1585160 | tf_op jit(solution)/shard_map/ppermute | solution.py:18
  37.3 1.3 %collective-permute-start.4 = (f32[1032,128]{1,0:T(8,128)S(1)}, f32[1032,128]{1,0:T(8,128)}, u32[]{:S(2)}, u32[]{:S(2)}) collective-permute-start(f32[1032,128]{1,0:T(8,128)S(1)} %select_maximum_fusion.2), channel_id=1, source_target_pairs={{8,48},{24,64},{40,80},{56,96},{72,112},{88,128},{104,144},{120,16... | collective-permute-start | bytes 1585160 | tf_op jit(solution)/shard_map/ppermute | solution.py:18
  38.6 4.3 %bitcast_add_fusion = f32[2,256,1,16,64]{1,4,3,0,2:T(8,128)} fusion(f32[2,256,1,16,64]{1,0,4,3,2:T(2,128)S(1)} %copy-done.2, f32[2,16,256]{2,1,0:T(8,128)S(1)} %bitcast.168, f32[2,16,256]{2,1,0:T(8,128)S(1)} %copy-done.8, f32[2,256,256]{2,1,0:T(8,128)S(1)} %fusion.36, pred[2,256,256]{2,1,0:T(8,128)(4,1)S(1)} %copy-done.7, f32[16]{0:T(128)S(1)} %copy-done.17, ...), kind=kOutput, calls=%fused_computation.18 | convolution fusion | flops 282066944 | bytes 5963840 | tf_op jit(solution)/shard_map/cghqs,csghp->cqghp/dot_general | solution.py:175
  42.9 7.0 %collective-permute-done.3 = f32[1032,128]{1,0:T(8,128)S(1)} collective-permute-done((f32[1032,128]{1,0:T(8,128)S(1)}, f32[1032,128]{1,0:T(8,128)S(1)}, u32[]{:S(2)}, u32[]{:S(2)}) %collective-permute-start.3) | collective-permute-done | bytes 528416 | tf_op jit(solution)/shard_map/ppermute | solution.py:18
  50.9 20.6 %collective-permute-done.4 = f32[1032,128]{1,0:T(8,128)} collective-permute-done((f32[1032,128]{1,0:T(8,128)S(1)}, f32[1032,128]{1,0:T(8,128)}, u32[]{:S(2)}, u32[]{:S(2)}) %collective-permute-start.4) | collective-permute-done | bytes 528416 | tf_op jit(solution)/shard_map/ppermute | solution.py:18
  71.6 1.1 slice.313
  73.7 4.5 %collective-permute-start.7 = (f32[1032,128]{1,0:T(8,128)S(1)}, f32[1032,128]{1,0:T(8,128)S(1)}, u32[]{:S(2)}, u32[]{:S(2)}) collective-permute-start(f32[1032,128]{1,0:T(8,128)S(1)} %fusion.22), channel_id=1, source_target_pairs={{0,8},{16,24},{32,40},{48,56},{64,72},{80,88},{96,104},{112,120},{... | collective-permute-start | bytes 1585160 | tf_op jit(solution)/shard_map/ppermute | solution.py:18
  78.2 2.3 %copy.111 = bf16[512,1024]{0,1:T(8,128)(2,1)} copy(bf16[512,1024]{1,0:T(8,128)(2,1)} %param.25) | data formatting | bytes 2097152 | tf_op args[2]
  81.7 1.0 fusion.17
  83.7 1.6 %copy.110 = f32[2,256,1,16,64]{1,0,4,3,2:T(2,128)S(1)} copy(f32[2,256,1,16,64]{1,4,3,0,2:T(8,128)S(1)} %fusion.12) | data formatting | bytes 4194304 | tf_op jit(solution)/shard_map/add | solution.py:211
  85.5 1.0 copy-done
  86.6 2.0 %multiply_reduce_fusion = (f32[512]{0:T(512)S(1)}, f32[1024,512]{1,0:T(8,128)}) fusion(f32[512,1024]{0,1:T(8,128)S(1)} %bitcast.146, bf16[512,1024]{0,1:T(8,128)(2,1)S(1)} %copy-done), kind=kLoop, calls=%fused_computation.20 | loop fusion | flops 4193792 | bytes 5244928 | tf_op jit(solution)/shard_map/reduce_sum | solution.py:213
  89.2 10.3 %all-to-all-start = ((f32[8,1,512]{2,1,0:T(1,128)}), f32[8,1,512]{2,1,0:T(1,128)S(1)}, u32[]{:S(2)}, u32[]{:S(2)}) async-start(f32[8,1,512]{2,1,0:T(1,128)} %broadcast_in_dim.145), calls=%async_computation | async-start | bytes 32768 | tf_op jit(solution)/shard_map/all_to_all | solution.py:78
  99.5 1.0 copy.113.w_ref
  100.5 6.7 %all-to-all-done = f32[8,1,512]{2,1,0:T(1,128)S(1)} async-done(((f32[8,1,512]{2,1,0:T(1,128)}), f32[8,1,512]{2,1,0:T(1,128)S(1)}, u32[]{:S(2)}, u32[]{:S(2)}) %all-to-all-start) | async-done | bytes 16416 | tf_op jit(solution)/shard_map/all_to_all | solution.py:78
  107.9 3.2 %shard_map.127 = bf16[512,1024]{1,0:T(8,128)(2,1)} custom-call(f32[1024,512]{1,0:T(8,128)} %get-tuple-element.76.g_ref, f32[1,512]{1,0:T(1,128)} %bitcast.173, f32[1024,1]{1,0:T(8,128)} %copy.113.w_ref), custom_call_target="tpu_custom_call" | custom-call | flops 1048576 | bytes 3145728 | tf_op jit(solution)/shard_map/pallas_call | solution.py:87
  (109 shorter events, 17.0 us)
Async XLA Ops:
  0.0 13.8 %copy-start.10 = (s32[512]{0:T(512)S(1)}, s32[512]{0:T(512)}, u32[]{:S(2)}) copy-start(s32[512]{0:T(512)} %param.35) | copy-start | bytes 6148
  0.0 11.1 %copy-start.3 = (bf16[512,1024]{1,0:T(8,128)(2,1)S(1)}, bf16[512,1024]{1,0:T(8,128)(2,1)}, u32[]{:S(2)}) copy-start(bf16[512,1024]{1,0:T(8,128)(2,1)} %param.23) | copy-start | bytes 3145732
  0.0 14.6 %copy-start.16 = (f32[2,128]{1,0:T(2,128)S(1)}, f32[2,128]{1,0:T(2,128)}, u32[]{:S(2)}) copy-start(f32[2,128]{1,0:T(2,128)} %param.30) | copy-start | bytes 3076
  2.7 10.9 %collective-permute-start = (bf16[3,1408]{0,1:T(8,128)(2,1)S(1)}, bf16[3,1408]{0,1:T(8,128)(2,1)S(1)}, u32[]{:S(2)}, u32[]{:S(2)}) collective-permute-start(bf16[3,1408]{0,1:T(8,128)(2,1)S(1)} %copy.100), channel_id=1, source_target_pairs={{0,8},{8,16},{16,24},{24,32},{32,40},{40,48},{48,56},{56,64},{64,7... | collective-permute-start | bytes 25352 | tf_op jit(solution)/shard_map/ppermute | solution.py:14
  11.2 4.4 %copy-start.13 = (f32[1024]{0:T(1024)S(1)}, f32[1024]{0:T(1024)}, u32[]{:S(2)}) copy-start(f32[1024]{0:T(1024)} %param.29) | copy-start | bytes 12292
  22.6 3.3 %collective-permute-start.1 = (f32[1032,128]{1,0:T(8,128)S(1)}, f32[1032,128]{1,0:T(8,128)S(1)}, u32[]{:S(2)}, u32[]{:S(2)}) collective-permute-start(f32[1032,128]{1,0:T(8,128)S(1)} %select_maximum_fusion.4), channel_id=1, source_target_pairs={{0,8},{16,24},{32,40},{48,56},{64,72},{80,88},{96,104},{112,120},{... | collective-permute-start | bytes 1585160 | tf_op jit(solution)/shard_map/ppermute | solution.py:18
  26.1 0.8 copy-start.11
  27.0 5.5 %collective-permute-start.2 = (f32[1032,128]{1,0:T(8,128)}, f32[1032,128]{1,0:T(8,128)}, u32[]{:S(2)}, u32[]{:S(2)}) collective-permute-start(f32[1032,128]{1,0:T(8,128)} %select_maximum_fusion.3), channel_id=1, source_target_pairs={{8,24},{24,40},{40,56},{56,72},{72,88},{88,104},{104,120},{120,136... | collective-permute-start | bytes 1585160 | tf_op jit(solution)/shard_map/ppermute | solution.py:18
  29.9 3.8 %copy-start.12 = (f32[1,16]{1,0:T(1,128)S(1)}, f32[1,16]{1,0:T(1,128)}, u32[]{:S(2)}) copy-start(f32[1,16]{1,0:T(1,128)} %copy-done.11) | copy-start | bytes 196
  32.2 6.4 %copy-start.2 = (f32[2,256,1,16,64]{1,0,4,3,2:T(2,128)S(1)}, f32[2,256,1,16,64]{1,0,4,3,2:T(2,128)}, u32[]{:S(2)}) copy-start(f32[2,256,1,16,64]{1,0,4,3,2:T(2,128)} %reshape.660) | copy-start | bytes 6291460
  32.2 6.4 %copy-start.4 = (bf16[2,256,16,64]{1,0,3,2:T(2,128)(2,1)S(1)}, bf16[2,256,16,64]{1,0,3,2:T(2,128)(2,1)}, u32[]{:S(2)}) copy-start(bf16[2,256,16,64]{1,0,3,2:T(2,128)(2,1)} %reshape.632) | copy-start | bytes 3145732
  32.2 6.4 %copy-start.7 = (pred[2,256,256]{2,1,0:T(8,128)(4,1)S(1)}, pred[2,256,256]{2,1,0:T(8,128)(4,1)}, u32[]{:S(2)}) copy-start(pred[2,256,256]{2,1,0:T(8,128)(4,1)} %compare_and_fusion) | copy-start | bytes 393220
  32.2 6.4 %copy-start.8 = (f32[2,16,256]{2,1,0:T(8,128)S(1)}, f32[2,16,256]{2,1,0:T(8,128)}, u32[]{:S(2)}) copy-start(f32[2,16,256]{2,1,0:T(8,128)} %get-tuple-element.83) | copy-start | bytes 98308
  32.2 6.4 %copy-start.9 = (f32[2,256,1,16]{1,3,0,2:T(8,128)S(1)}, f32[2,256,1,16]{1,3,0,2:T(8,128)}, u32[]{:S(2)}) copy-start(f32[2,256,1,16]{1,3,0,2:T(8,128)} %copy.141) | copy-start | bytes 98308
  32.2 6.4 %copy-start.17 = (f32[16]{0:T(128)S(1)}, f32[16]{0:T(128)}, u32[]{:S(2)}) copy-start(f32[16]{0:T(128)} %param.33) | copy-start | bytes 196
  34.6 15.4 %collective-permute-start.3 = (f32[1032,128]{1,0:T(8,128)S(1)}, f32[1032,128]{1,0:T(8,128)S(1)}, u32[]{:S(2)}, u32[]{:S(2)}) collective-permute-start(f32[1032,128]{1,0:T(8,128)S(1)} %select_maximum_fusion.2), channel_id=1, source_target_pairs={{8,16},{24,32},{40,48},{56,64},{72,80},{88,96},{104,112},{120,128}... | collective-permute-start | bytes 1585160 | tf_op jit(solution)/shard_map/ppermute | solution.py:18
  35.9 14.1 %collective-permute-start.5 = (f32[1032,128]{1,0:T(8,128)S(1)}, f32[1032,128]{1,0:T(8,128)S(1)}, u32[]{:S(2)}, u32[]{:S(2)}) collective-permute-start(f32[1032,128]{1,0:T(8,128)S(1)} %select_maximum_fusion.2), channel_id=1, source_target_pairs={{8,88},{24,104},{40,120},{56,136},{72,152},{88,168},{104,184},{120... | collective-permute-start | bytes 1585160 | tf_op jit(solution)/shard_map/ppermute | solution.py:18
  36.6 13.4 %collective-permute-start.6 = (f32[1032,128]{1,0:T(8,128)S(1)}, f32[1032,128]{1,0:T(8,128)S(1)}, u32[]{:S(2)}, u32[]{:S(2)}) collective-permute-start(f32[1032,128]{1,0:T(8,128)S(1)} %select_maximum_fusion.2), channel_id=1, source_target_pairs={{8,120},{24,136},{40,152},{56,168},{72,184},{88,200},{104,216},{12... | collective-permute-start | bytes 1585160 | tf_op jit(solution)/shard_map/ppermute | solution.py:18
  37.3 34.3 %collective-permute-start.4 = (f32[1032,128]{1,0:T(8,128)S(1)}, f32[1032,128]{1,0:T(8,128)}, u32[]{:S(2)}, u32[]{:S(2)}) collective-permute-start(f32[1032,128]{1,0:T(8,128)S(1)} %select_maximum_fusion.2), channel_id=1, source_target_pairs={{8,48},{24,64},{40,80},{56,96},{72,112},{88,128},{104,144},{120,16... | collective-permute-start | bytes 1585160 | tf_op jit(solution)/shard_map/ppermute | solution.py:18
  50.0 0.8 copy-start.5
  50.9 22.5 %copy-start.6 = (f32[1032,128]{1,0:T(8,128)S(1)}, f32[1032,128]{1,0:T(8,128)}, u32[]{:S(2)}) copy-start(f32[1032,128]{1,0:T(8,128)} %copy-done.5) | copy-start | bytes 1585156
  73.7 6.8 %collective-permute-start.7 = (f32[1032,128]{1,0:T(8,128)S(1)}, f32[1032,128]{1,0:T(8,128)S(1)}, u32[]{:S(2)}, u32[]{:S(2)}) collective-permute-start(f32[1032,128]{1,0:T(8,128)S(1)} %fusion.22), channel_id=1, source_target_pairs={{0,8},{16,24},{32,40},{48,56},{64,72},{80,88},{96,104},{112,120},{... | collective-permute-start | bytes 1585160 | tf_op jit(solution)/shard_map/ppermute | solution.py:18
  80.6 0.7 copy-start.15
  81.7 1.6 %copy-start.1 = (f32[2,256,1,16,64]{1,4,3,0,2:T(8,128)S(1)}, f32[2,256,1,16,64]{1,4,3,0,2:T(8,128)}, u32[]{:S(2)}) copy-start(f32[2,256,1,16,64]{1,4,3,0,2:T(8,128)} %bitcast_add_fusion) | copy-start | bytes 6291460
  85.3 1.2 %copy-start = (bf16[512,1024]{0,1:T(8,128)(2,1)S(1)}, bf16[512,1024]{0,1:T(8,128)(2,1)}, u32[]{:S(2)}) copy-start(bf16[512,1024]{0,1:T(8,128)(2,1)} %copy.111) | copy-start | bytes 3145732
  86.6 12.9 %copy-start.14 = (f32[1024]{0:T(1024)S(1)}, f32[1024]{0:T(1024)}, u32[]{:S(2)}) copy-start(f32[1024]{0:T(1024)} %param.34) | copy-start | bytes 12292
  89.2 18.1 %all-to-all-start = ((f32[8,1,512]{2,1,0:T(1,128)}), f32[8,1,512]{2,1,0:T(1,128)S(1)}, u32[]{:S(2)}, u32[]{:S(2)}) async-start(f32[8,1,512]{2,1,0:T(1,128)} %broadcast_in_dim.145), calls=%async_computation | async-start | bytes 32768 | tf_op jit(solution)/shard_map/all_to_all | solution.py:78

commit v14 on v9

--- a/solution.py
+++ b/solution.py
@@ -181,12 +181,13 @@
     device_gain = carry_gain[0] * carry_gain[1]
     skip = d_skip.reshape(groups_local, heads_group)[..., None]
     base = y_intra + skip * x_heads.astype(jnp.float32)
-    entering, base = entering_state(device_gain, summary, "seq", base)
+    gate = jax.nn.silu(z_proj.astype(jnp.float32))
+    entering, (base, gate) = entering_state(device_gain, summary, "seq", (base, gate))
     states, _ = recur(entering)
     product = jnp.einsum("cqgn,cghpn->cqghp", c_float, states, precision=lax.Precision.HIGHEST)
     y_inter = product * link.transpose(0, 3, 1, 2)[..., None]
     mixed = base + y_inter
-    gated = mixed.reshape(tok_rows, inner_local) * jax.nn.silu(z_proj.astype(jnp.float32))
+    gated = mixed.reshape(tok_rows, inner_local) * gate
     squares = summed_over(jnp.sum(gated * gated, axis=-1), "tp")
     scale = lax.rsqrt(squares / (inner_local * lax.axis_size("tp")) + 1e-05)
     return (gated * scale[:, None] * norm_gain).astype(jnp.bfloat16)

time: 106 us -> 115 us (1.085)
  other arithmetic: 17 us -> 24 us
  waiting for transfers between devices: 32.1 us -> 28.4 us
  local copies, waits for them, and re-layouts: 16.3 us -> 19.5 us
    ppermute x7, waiting for transfers between devices: 29.7 us -> 26.6 us  [shifted(): return lax.ppermute(block, axis, pairs)]
    unnamed x36 -> x62, local copies, waits for them, and re-layouts: 5.33 us -> 7.88 us
    concatenate x3, other arithmetic: 0.11 us -> 2.5 us  [pack(): return jnp.concatenate([flat, row])]
    mul x0 -> x1, other arithmetic: none -> 1.86 us  [on_device(): gate = jax.nn.silu(z_proj.astype(jnp.float32))]
    reduce_sum x1, other arithmetic: 0.68 us -> 1.86 us  [on_device(): squares = summed_over(jnp.sum(gated * gated, axis=-1), 'tp')]
    dot_general x1, matrix products: 1.66 us -> 2.82 us  [on_device(): jnp.einsum('cghsn,csghp->cghpn', b_weighted, x_heads, preferred_element_t...]
  transfers between devices with their start and end apart: 8 -> 8, of which waited for: 4 -> 4; matrix products, arithmetic and copies ran while one was open for 15% -> 16% of each run, Pallas kernels for 0% -> 0%
where the time goes in v14:
time: 115 us; the launch traced here: 113 us
  waiting for transfers between devices  28.4 us (25%)
  other arithmetic  24 us (21%)
  local copies, waits for them, and re-layouts  19.5 us (17%)
  blocking collectives  17.9 us (16%)
  starting transfers between devices  14.6 us (13%)
  matrix products  8.28 us (7%)
    ppermute x7, waiting for transfers between devices, shifted(): return lax.ppermute(block, axis, pairs)  26.6 us
    all_to_all x1, blocking collectives, summed_over(): return lax.all_to_all(spread, axis, 0, 0, tiled=False).sum(0)  17.9 us
    ppermute x7, starting transfers between devices, shifted(): return lax.ppermute(block, axis, pairs)  12.7 us
    unnamed x62, local copies, waits for them, and re-layouts  7.88 us
    dot_general x1, matrix products, on_device(): jnp.einsum('cghqs,csghp->cqghp', mixing, x_heads, preferred_element_type=...  4.24 us
    convert_element_type x2, other arithmetic, causal_conv(): return jax.nn.silu(result).astype(jnp.bfloat16)  3.67 us
    slice x5, local copies, waits for them, and re-layouts, unpack(): packed[:rows].reshape(state_shape)  3.45 us
    dot_general x1, matrix products, on_device(): jnp.einsum('cghsn,csghp->cghpn', b_weighted, x_heads, preferred_element_t...  2.82 us
  transfers between devices with their start and end apart: 8, of which 4 were waited for; matrix products, arithmetic and copies ran while one was open for 16% of the time, Pallas kernels for 0%

profile of v14, /device:TPU:6, one launch (start us, length us, event | category | flops | bytes accessed | tf_op | source)
XLA Modules:
  0.0 113.3 jit_solution(6244047436176584895)
XLA Ops:
  2.7 1.9 %collective-permute-start = (bf16[3,1408]{0,1:T(8,128)(2,1)S(1)}, bf16[3,1408]{0,1:T(8,128)(2,1)S(1)}, u32[]{:S(2)}, u32[]{:S(2)}) collective-permute-start(bf16[3,1408]{0,1:T(8,128)(2,1)S(1)} %copy.94), channel_id=1, source_target_pairs={{0,8},{8,16},{16,24},{24,32},{32,40},{40,48},{48,56},{56,64},{64,7... | collective-permute-start | bytes 25352 | tf_op jit(solution)/shard_map/ppermute | solution.py:13
  5.3 0.9 broadcast_multiply_fusion
  6.2 1.2 %reduce-window.6 = f32[2,16,2,128]{3,1,2,0:T(8,128)S(1)} reduce-window(f32[2,16,2,128]{3,1,2,0:T(8,128)S(1)} %copy_bitcast_fusion.1, f32[]{:T(128)} %constant.131.clone.1), window={size=1x1x1x128 pad=0_0x0_0x0_0x127_0}, to_apply=%region_0.1 | reduce-window | flops 1040384 | bytes 65540 | tf_op jit(solution)/shard_map/reduce-window
  9.1 0.9 slice_convert_fusion.3
  10.1 1.0 copy.99
  11.7 1.8 %collective-permute-done = bf16[3,1408]{0,1:T(8,128)(2,1)S(1)} collective-permute-done((bf16[3,1408]{0,1:T(8,128)(2,1)S(1)}, bf16[3,1408]{0,1:T(8,128)(2,1)S(1)}, u32[]{:S(2)}, u32[]{:S(2)}) %collective-permute-start) | collective-permute-done | bytes 8480 | tf_op jit(solution)/shard_map/ppermute | solution.py:13
  16.2 2.8 %multiply_convert_fusion.5 = bf16[512,1024]{0,1:T(8,128)(2,1)S(1)} fusion(bf16[512,1024]{0,1:T(8,128)(2,1)S(1)} %copy.95, bf16[3,1024]{0,1:T(8,128)(2,1)S(1)} %slice.293, f32[1024]{0:T(1024)S(1)} %bitcast.167, f32[1024]{0:T(1024)S(1)} %bitcast.168, f32[1024]{0:T(1024)S(1)} %bitcast.166, f32[1024]{0:T(1024)S(1)} %bitcast.165, f32[1024]{0:T(1024)S(1)} %copy-done.23, ...), kind=kLoop, calls=%fused_computation.23 | loop fusion | flops 15728640 | bytes 2125824 | tf_op jit(solution)/shard_map/convert_element_type | solution.py:89
  19.5 2.8 %fusion.10 = f32[2,16,64,128]{3,2,1,0:T(8,128)S(1)} fusion(f32[2,16,256]{2,1,0:T(8,128)S(1)} %fusion.25, f32[2,256,128]{2,1,0:T(8,128)} %convert_element_type.129, bf16[2,256,16,64]{1,0,3,2:T(2,128)(2,1)S(1)} %reshape.620), kind=kOutput, calls=%fused_computation.14 | convolution fusion | flops 136314880 | bytes 2392064 | tf_op jit(solution)/shard_map/cghsn,csghp->cghpn/dot_general | solution.py:158
  22.3 1.0 copy-done.2
  23.4 0.8 select_maximum_fusion.4
  24.3 2.6 %collective-permute-start.1 = (f32[1032,128]{1,0:T(8,128)}, f32[1032,128]{1,0:T(8,128)}, u32[]{:S(2)}, u32[]{:S(2)}) collective-permute-start(f32[1032,128]{1,0:T(8,128)} %select_maximum_fusion.4), channel_id=1, source_target_pairs={{0,8},{16,24},{32,40},{48,56},{64,72},{80,88},{96,104},{112,120},{... | collective-permute-start | bytes 1585160 | tf_op jit(solution)/shard_map/ppermute | solution.py:17
  26.9 1.3 %copy.105 = bf16[512,1024]{0,1:T(8,128)(2,1)} copy(bf16[512,1024]{1,0:T(8,128)(2,1)S(1)} %copy-done.10) | data formatting | bytes 2097152 | tf_op args[2]
  28.2 1.9 %convert_multiply_fusion = f32[512,1024]{0,1:T(8,128)S(1)} fusion(bf16[512,1024]{0,1:T(8,128)(2,1)} %copy.105), kind=kLoop, calls=%fused_computation.9 | loop fusion | flops 2621440 | bytes 3145728 | tf_op jit(solution)/shard_map/jit(silu)/mul | solution.py:184
  30.1 1.1 slice.307
  33.8 1.5 %collective-permute-start.2 = (f32[1032,128]{1,0:T(8,128)}, f32[1032,128]{1,0:T(8,128)}, u32[]{:S(2)}, u32[]{:S(2)}) collective-permute-start(f32[1032,128]{1,0:T(8,128)} %select_maximum_fusion.3), channel_id=1, source_target_pairs={{8,24},{24,40},{40,56},{56,72},{72,88},{88,104},{104,120},{120,136... | collective-permute-start | bytes 1585160 | tf_op jit(solution)/shard_map/ppermute | solution.py:17
  36.7 2.3 %reshape.648 = f32[2,256,1,16,64]{1,0,4,3,2:T(2,128)} reshape(bf16[512,1024]{0,1:T(8,128)(2,1)S(1)} %multiply_convert_fusion.5) | data formatting | bytes 3145728 | tf_op jit(solution)/shard_map/convert_element_type | solution.py:183
  39.2 1.2 %slice.308 = f32[1024,128]{1,0:T(8,128)S(1)} slice(f32[1032,128]{1,0:T(8,128)} %collective-permute-done.2), slice={[0:1024], [0:128]} | slice | bytes 1048576 | tf_op jit(solution)/shard_map/slice | solution.py:38
  41.3 0.8 select_maximum_fusion.2
  42.1 1.3 %collective-permute-start.3 = (f32[1032,128]{1,0:T(8,128)}, f32[1032,128]{1,0:T(8,128)S(1)}, u32[]{:S(2)}, u32[]{:S(2)}) collective-permute-start(f32[1032,128]{1,0:T(8,128)} %select_maximum_fusion.2), channel_id=1, source_target_pairs={{8,16},{24,32},{40,48},{56,64},{72,80},{88,96},{104,112},{120,128}... | collective-permute-start | bytes 1585160 | tf_op jit(solution)/shard_map/ppermute | solution.py:17
  44.8 1.3 %collective-permute-start.4 = (f32[1032,128]{1,0:T(8,128)}, f32[1032,128]{1,0:T(8,128)}, u32[]{:S(2)}, u32[]{:S(2)}) collective-permute-start(f32[1032,128]{1,0:T(8,128)} %select_maximum_fusion.2), channel_id=1, source_target_pairs={{8,48},{24,64},{40,80},{56,96},{72,112},{88,128},{104,144},{120,16... | collective-permute-start | bytes 1585160 | tf_op jit(solution)/shard_map/ppermute | solution.py:17
  46.2 4.2 %bitcast_add_fusion = f32[2,256,1,16,64]{1,4,3,0,2:T(8,128)} fusion(f32[2,256,1,16,64]{1,0,4,3,2:T(2,128)S(1)} %copy-done.8, f32[2,16,256]{2,1,0:T(8,128)S(1)} %bitcast.164, f32[2,16,256]{2,1,0:T(8,128)S(1)} %copy-done.18, f32[2,256,256]{2,1,0:T(8,128)S(1)} %fusion.34, pred[2,256,256]{2,1,0:T(8,128)(4,1)S(1)} %copy-done.17, f32[16]{0:T(128)S(1)} %copy-done.27, ...), kind=kOutput, calls=%fused_computation.17 | convolution fusion | flops 282066944 | bytes 5963840 | tf_op jit(solution)/shard_map/cghqs,csghp->cqghp/dot_general | solution.py:152
  50.4 5.5 %collective-permute-done.3 = f32[1032,128]{1,0:T(8,128)S(1)} collective-permute-done((f32[1032,128]{1,0:T(8,128)}, f32[1032,128]{1,0:T(8,128)S(1)}, u32[]{:S(2)}, u32[]{:S(2)}) %collective-permute-start.3) | collective-permute-done | bytes 528416 | tf_op jit(solution)/shard_map/ppermute | solution.py:17
  57.8 19.8 %collective-permute-done.4 = f32[1032,128]{1,0:T(8,128)} collective-permute-done((f32[1032,128]{1,0:T(8,128)}, f32[1032,128]{1,0:T(8,128)}, u32[]{:S(2)}, u32[]{:S(2)}) %collective-permute-start.4) | collective-permute-done | bytes 528416 | tf_op jit(solution)/shard_map/ppermute | solution.py:17
  77.6 1.1 slice.313
  79.8 4.7 %collective-permute-start.7 = (f32[1032,128]{1,0:T(8,128)S(1)}, f32[1032,128]{1,0:T(8,128)S(1)}, u32[]{:S(2)}, u32[]{:S(2)}) collective-permute-start(f32[1032,128]{1,0:T(8,128)S(1)} %fusion.21), channel_id=1, source_target_pairs={{0,8},{16,24},{32,40},{48,56},{64,72},{80,88},{96,104},{112,120},{... | collective-permute-start | bytes 1585160 | tf_op jit(solution)/shard_map/ppermute | solution.py:17
  84.6 1.2 %collective-permute-done.7 = f32[1032,128]{1,0:T(8,128)S(1)} collective-permute-done((f32[1032,128]{1,0:T(8,128)S(1)}, f32[1032,128]{1,0:T(8,128)S(1)}, u32[]{:S(2)}, u32[]{:S(2)}) %collective-permute-start.7) | collective-permute-done | bytes 528416 | tf_op jit(solution)/shard_map/ppermute | solution.py:17
  86.5 1.0 fusion.16
  88.5 1.6 %copy.106 = f32[2,256,1,16,64]{1,0,4,3,2:T(2,128)S(1)} copy(f32[2,256,1,16,64]{1,4,3,0,2:T(8,128)S(1)} %fusion.11) | data formatting | bytes 4194304 | tf_op jit(solution)/shard_map/add | solution.py:189
  90.3 1.9 %multiply_reduce_fusion = (f32[512]{0:T(512)S(1)}, f32[512,1024]{0,1:T(8,128)}) fusion(f32[512,1024]{0,1:T(8,128)S(1)} %bitcast.142, f32[512,1024]{0,1:T(8,128)S(1)} %convert_multiply_fusion), kind=kLoop, calls=%fused_computation.20 | loop fusion | flops 1572352 | bytes 6293504 | tf_op jit(solution)/shard_map/reduce_sum | solution.py:191
  92.2 17.9 %all_to_all.6 = f32[8,1,512]{2,1,0:T(1,128)S(1)} all-to-all(f32[8,1,512]{2,1,0:T(1,128)S(1)} %broadcast_in_dim.143), channel_id=1, replica_groups=mesh['seq'=64,'tp'=8] {'tp'}, dimensions={0} | all-to-all | bytes 32768 | tf_op jit(solution)/shard_map/all_to_all | solution.py:77
  110.1 1.8 %multiply_convert_fusion.4 = bf16[512,1024]{0,1:T(8,128)(2,1)S(1)} fusion(f32[512,1024]{0,1:T(8,128)} %get-tuple-element.76, f32[1024]{0:T(1024)S(1)} %copy-done.24, f32[512]{0:T(512)S(1)} %add_rsqrt_fusion), kind=kLoop, calls=%fused_computation.19 | loop fusion | flops 1572864 | bytes 3151872 | tf_op jit(solution)/shard_map/convert_element_type | solution.py:193
  112.0 1.3 %copy.108 = bf16[512,1024]{1,0:T(8,128)(2,1)} copy(bf16[512,1024]{0,1:T(8,128)(2,1)S(1)} %multiply_convert_fusion.4) | data formatting | bytes 2097152 | tf_op jit(solution)/shard_map/convert_element_type | solution.py:193
  (129 shorter events, 20.3 us)
Async XLA Ops:
  0.0 13.8 %copy-start.20 = (s32[512]{0:T(512)S(1)}, s32[512]{0:T(512)}, u32[]{:S(2)}) copy-start(s32[512]{0:T(512)} %param.35) | copy-start | bytes 6148
  0.0 11.1 %copy-start.9 = (bf16[512,1024]{1,0:T(8,128)(2,1)S(1)}, bf16[512,1024]{1,0:T(8,128)(2,1)}, u32[]{:S(2)}) copy-start(bf16[512,1024]{1,0:T(8,128)(2,1)} %param.23) | copy-start | bytes 3145732
  0.0 14.6 %copy-start.26 = (f32[2,128]{1,0:T(2,128)S(1)}, f32[2,128]{1,0:T(2,128)}, u32[]{:S(2)}) copy-start(f32[2,128]{1,0:T(2,128)} %param.30) | copy-start | bytes 3076
  2.7 10.9 %collective-permute-start = (bf16[3,1408]{0,1:T(8,128)(2,1)S(1)}, bf16[3,1408]{0,1:T(8,128)(2,1)S(1)}, u32[]{:S(2)}, u32[]{:S(2)}) collective-permute-start(bf16[3,1408]{0,1:T(8,128)(2,1)S(1)} %copy.94), channel_id=1, source_target_pairs={{0,8},{8,16},{16,24},{24,32},{32,40},{40,48},{48,56},{56,64},{64,7... | collective-permute-start | bytes 25352 | tf_op jit(solution)/shard_map/ppermute | solution.py:13
  11.1 5.0 %copy-start.23 = (f32[1024]{0:T(1024)S(1)}, f32[1024]{0:T(1024)}, u32[]{:S(2)}) copy-start(f32[1024]{0:T(1024)} %param.29) | copy-start | bytes 12292
  19.3 4.1 %copy-start.11 = (bf16[2,256,16,64]{1,0,3,2:T(2,128)(2,1)}, bf16[2,256,16,64]{1,0,3,2:T(2,128)(2,1)S(1)}, u32[]{:S(2)}) copy-start(bf16[2,256,16,64]{1,0,3,2:T(2,128)(2,1)S(1)} %reshape.620) | copy-start | bytes 3145732
  19.4 7.4 %copy-start.10 = (bf16[512,1024]{1,0:T(8,128)(2,1)S(1)}, bf16[512,1024]{1,0:T(8,128)(2,1)}, u32[]{:S(2)}) copy-start(bf16[512,1024]{1,0:T(8,128)(2,1)} %param.25) | copy-start | bytes 3145732
  22.3 1.0 copy-start.2
  24.3 5.8 %collective-permute-start.1 = (f32[1032,128]{1,0:T(8,128)}, f32[1032,128]{1,0:T(8,128)}, u32[]{:S(2)}, u32[]{:S(2)}) collective-permute-start(f32[1032,128]{1,0:T(8,128)} %select_maximum_fusion.4), channel_id=1, source_target_pairs={{0,8},{16,24},{32,40},{48,56},{64,72},{80,88},{96,104},{112,120},{... | collective-permute-start | bytes 1585160 | tf_op jit(solution)/shard_map/ppermute | solution.py:17
  28.2 3.8 %copy-start.3 = (f32[2,16,64,128]{3,2,1,0:T(8,128)S(1)}, f32[2,16,64,128]{3,2,1,0:T(8,128)}, u32[]{:S(2)}) copy-start(f32[2,16,64,128]{3,2,1,0:T(8,128)} %copy-done.2) | copy-start | bytes 3145732
  32.8 1.0 copy-start.21
  33.8 5.4 %collective-permute-start.2 = (f32[1032,128]{1,0:T(8,128)}, f32[1032,128]{1,0:T(8,128)}, u32[]{:S(2)}, u32[]{:S(2)}) collective-permute-start(f32[1032,128]{1,0:T(8,128)} %select_maximum_fusion.3), channel_id=1, source_target_pairs={{8,24},{24,40},{40,56},{56,72},{72,88},{88,104},{104,120},{120,136... | collective-permute-start | bytes 1585160 | tf_op jit(solution)/shard_map/ppermute | solution.py:17
  36.7 3.8 %copy-start.22 = (f32[1,16]{1,0:T(1,128)S(1)}, f32[1,16]{1,0:T(1,128)}, u32[]{:S(2)}) copy-start(f32[1,16]{1,0:T(1,128)} %copy-done.21) | copy-start | bytes 196
  39.0 1.5 %copy-start.6 = (f32[1,16,64,128]{3,2,1,0:T(8,128)S(1)}, f32[1,16,64,128]{3,2,1,0:T(8,128)}, u32[]{:S(2)}) copy-start(f32[1,16,64,128]{3,2,1,0:T(8,128)} %copy-done.5) | copy-start | bytes 1572868
  39.0 7.2 %copy-start.8 = (f32[2,256,1,16,64]{1,0,4,3,2:T(2,128)S(1)}, f32[2,256,1,16,64]{1,0,4,3,2:T(2,128)}, u32[]{:S(2)}) copy-start(f32[2,256,1,16,64]{1,0,4,3,2:T(2,128)} %reshape.648) | copy-start | bytes 6291460
  39.0 7.2 %copy-start.12 = (bf16[2,256,16,64]{1,0,3,2:T(2,128)(2,1)S(1)}, bf16[2,256,16,64]{1,0,3,2:T(2,128)(2,1)}, u32[]{:S(2)}) copy-start(bf16[2,256,16,64]{1,0,3,2:T(2,128)(2,1)} %copy-done.11) | copy-start | bytes 3145732
  39.0 7.2 %copy-start.17 = (pred[2,256,256]{2,1,0:T(8,128)(4,1)S(1)}, pred[2,256,256]{2,1,0:T(8,128)(4,1)}, u32[]{:S(2)}) copy-start(pred[2,256,256]{2,1,0:T(8,128)(4,1)} %compare_and_fusion) | copy-start | bytes 393220
  39.0 7.2 %copy-start.18 = (f32[2,16,256]{2,1,0:T(8,128)S(1)}, f32[2,16,256]{2,1,0:T(8,128)}, u32[]{:S(2)}) copy-start(f32[2,16,256]{2,1,0:T(8,128)} %get-tuple-element.85) | copy-start | bytes 98308
  39.0 7.2 %copy-start.19 = (f32[2,256,1,16]{1,3,0,2:T(8,128)S(1)}, f32[2,256,1,16]{1,3,0,2:T(8,128)}, u32[]{:S(2)}) copy-start(f32[2,256,1,16]{1,3,0,2:T(8,128)} %copy.138) | copy-start | bytes 98308
  39.0 7.2 %copy-start.27 = (f32[16]{0:T(128)S(1)}, f32[16]{0:T(128)}, u32[]{:S(2)}) copy-start(f32[16]{0:T(128)} %param.33) | copy-start | bytes 196
  42.1 13.8 %collective-permute-start.3 = (f32[1032,128]{1,0:T(8,128)}, f32[1032,128]{1,0:T(8,128)S(1)}, u32[]{:S(2)}, u32[]{:S(2)}) collective-permute-start(f32[1032,128]{1,0:T(8,128)} %select_maximum_fusion.2), channel_id=1, source_target_pairs={{8,16},{24,32},{40,48},{56,64},{72,80},{88,96},{104,112},{120,128}... | collective-permute-start | bytes 1585160 | tf_op jit(solution)/shard_map/ppermute | solution.py:17
  43.4 12.6 %collective-permute-start.5 = (f32[1032,128]{1,0:T(8,128)}, f32[1032,128]{1,0:T(8,128)S(1)}, u32[]{:S(2)}, u32[]{:S(2)}) collective-permute-start(f32[1032,128]{1,0:T(8,128)} %select_maximum_fusion.2), channel_id=1, source_target_pairs={{8,88},{24,104},{40,120},{56,136},{72,152},{88,168},{104,184},{120... | collective-permute-start | bytes 1585160 | tf_op jit(solution)/shard_map/ppermute | solution.py:17
  44.1 11.9 %collective-permute-start.6 = (f32[1032,128]{1,0:T(8,128)}, f32[1032,128]{1,0:T(8,128)S(1)}, u32[]{:S(2)}, u32[]{:S(2)}) collective-permute-start(f32[1032,128]{1,0:T(8,128)} %select_maximum_fusion.2), channel_id=1, source_target_pairs={{8,120},{24,136},{40,152},{56,168},{72,184},{88,200},{104,216},{12... | collective-permute-start | bytes 1585160 | tf_op jit(solution)/shard_map/ppermute | solution.py:17
  44.8 32.7 %collective-permute-start.4 = (f32[1032,128]{1,0:T(8,128)}, f32[1032,128]{1,0:T(8,128)}, u32[]{:S(2)}, u32[]{:S(2)}) collective-permute-start(f32[1032,128]{1,0:T(8,128)} %select_maximum_fusion.2), channel_id=1, source_target_pairs={{8,48},{24,64},{40,80},{56,96},{72,112},{88,128},{104,144},{120,16... | collective-permute-start | bytes 1585160 | tf_op jit(solution)/shard_map/ppermute | solution.py:17
  57.7 21.7 %copy-start.14 = (f32[1032,128]{1,0:T(8,128)S(1)}, f32[1032,128]{1,0:T(8,128)}, u32[]{:S(2)}) copy-start(f32[1032,128]{1,0:T(8,128)} %copy-done.13) | copy-start | bytes 1585156
  57.8 21.7 %copy-start.16 = (f32[1032,128]{1,0:T(8,128)S(1)}, f32[1032,128]{1,0:T(8,128)}, u32[]{:S(2)}) copy-start(f32[1032,128]{1,0:T(8,128)} %copy-done.15) | copy-start | bytes 1585156
  79.8 6.0 %collective-permute-start.7 = (f32[1032,128]{1,0:T(8,128)S(1)}, f32[1032,128]{1,0:T(8,128)S(1)}, u32[]{:S(2)}, u32[]{:S(2)}) collective-permute-start(f32[1032,128]{1,0:T(8,128)S(1)} %fusion.21), channel_id=1, source_target_pairs={{0,8},{16,24},{32,40},{48,56},{64,72},{80,88},{96,104},{112,120},{... | collective-permute-start | bytes 1585160 | tf_op jit(solution)/shard_map/ppermute | solution.py:17
  84.6 1.4 %copy-start.1 = (f32[1024,128]{1,0:T(8,128)S(1)}, f32[1024,128]{1,0:T(8,128)}, u32[]{:S(2)}) copy-start(f32[1024,128]{1,0:T(8,128)} %copy-done) | copy-start | bytes 1572868
  84.6 1.4 %copy-start.4 = (f32[2,16,64,128]{3,2,1,0:T(8,128)S(1)}, f32[2,16,64,128]{3,2,1,0:T(8,128)}, u32[]{:S(2)}) copy-start(f32[2,16,64,128]{3,2,1,0:T(8,128)} %copy-done.2) | copy-start | bytes 3145732
  84.6 1.4 %copy-start.25 = (f32[16]{0:T(128)S(1)}, f32[16]{0:T(128)}, u32[]{:S(2)}) copy-start(f32[16]{0:T(128)} %get-tuple-element.103) | copy-start | bytes 196
  86.5 1.6 %copy-start.7 = (f32[2,256,1,16,64]{1,4,3,0,2:T(8,128)S(1)}, f32[2,256,1,16,64]{1,4,3,0,2:T(8,128)}, u32[]{:S(2)}) copy-start(f32[2,256,1,16,64]{1,4,3,0,2:T(8,128)} %bitcast_add_fusion) | copy-start | bytes 6291460
  90.3 19.8 %copy-start.24 = (f32[1024]{0:T(1024)S(1)}, f32[1024]{0:T(1024)}, u32[]{:S(2)}) copy-start(f32[1024]{0:T(1024)} %param.34) | copy-start | bytes 12292
  (4 other events, 3.2 us)
